TPU v7x, 512 devices: a whole 4x8x8 slice. The times are simulated.
512 devices in a mesh: dp: 64 (over z, y), tensor: 8 (over x, core).
Axes of the slice: x: 4, y: 8, z: 8, core: 2. Of those that a mesh axis runs over, the one named last changes fastest.
Arguments:
- hidden: bfloat16 [192, 256, 14336], P('dp', None, 'tensor'), may hold values from -6 to 6
- out_grad: bfloat16 [192, 256, 4096], P('dp', None, 'tensor'), may hold values from -0.29882812 to 0.29882812
- proj_in: bfloat16 [64, 14336], P(None, 'tensor'), may hold values from -0.046875 to 0.046875
- proj_out: bfloat16 [64, 4096], P(None, 'tensor'), may hold values from -0.09375 to 0.09375
- left_inv: float32 [64, 64], replicated, may hold values from -0.15 to 3, as said below
- right_inv: float32 [64, 64], replicated, may hold values from -0.15 to 3, as said below
- lengths: int32 [192], P('dp'), may hold values from 64 to 256
- language: int32 [192], P('dp'), may hold values from 0 to 99
- owner: int32 [100], replicated, may hold values from 0 to 63, as said below
Outputs:
- seq_grads: float32 [192, 4096], P('dp', 'tensor')
- owned_means: float32 [128, 4096], P('dp', 'tensor')
Inputs may be any that keep to these rules, and one draw needn't show every extreme that they name: `left_inv`: symmetric; diagonal entries 1 or more, off-diagonal entries of magnitude 0.15 or less. `right_inv`: symmetric; diagonal entries 1 or more, off-diagonal entries of magnitude 0.15 or less. Every owner holds 1 or 2 languages, and some owner holds 2.
All inputs are finite; a program needn't handle non-finite values.
Results may differ from a plain program's by a relative error of at most 0.0003.
Values sent between devices are 32-bit elements; how exact they have to be, the bound alone decides.
No kernel may reach another device: no remote copies, remote signals or barrier semaphores. Data moves between devices by JAX's collectives and lax.ppermute only.
A program may use at most 64 MiB of HBM per device.

v0:
```python
import jax
import jax.numpy as jnp
from jax import lax
from jax.sharding import PartitionSpec as P


def project(values, projection):
    flattened = values.reshape(-1, values.shape[-1])
    return lax.dot_general(
        flattened, projection, (((1,), (1,)), ((), ())), preferred_element_type=jnp.float32
    )


def per_device(hidden, out_grad, proj_in, proj_out, left_inv, right_inv, lengths, language, owner):
    highest = lax.Precision.HIGHEST
    seq_count = hidden.shape[0]
    seq_length = hidden.shape[1]
    proj_rank = proj_in.shape[0]
    tensor_size = lax.axis_size("tensor")
    row_width = proj_rank // tensor_size
    row_start = lax.axis_index("tensor") * row_width
    left_part = project(hidden, proj_in)
    right_part = project(out_grad, proj_out)
    token_mask = (jnp.arange(seq_length, dtype=jnp.int32)[None, :] < lengths[:, None]).astype(
        jnp.float32
    )
    left_full, right_full = lax.psum((left_part, right_part), "tensor")
    left_full = left_full.reshape(seq_count, seq_length, proj_rank)
    right_full = right_full.reshape(seq_count, seq_length, proj_rank) * token_mask[:, :, None]
    full_grads = jnp.einsum("sti,stj->sij", left_full, right_full, precision=highest)
    left_done = jnp.einsum("ik,skj->sij", left_inv, full_grads, precision=highest)
    full_pre = jnp.einsum("sik,kj->sij", left_done, right_inv, precision=highest)
    grad_rows = lax.dynamic_slice_in_dim(full_grads, row_start, row_width, 1)
    pre_rows = lax.dynamic_slice_in_dim(full_pre, row_start, row_width, 1)
    grad_flat = grad_rows.reshape(seq_count, row_width * proj_rank)
    pre_flat = pre_rows.reshape(seq_count, row_width * proj_rank)
    lang_total = owner.shape[0]
    dp_size = lax.axis_size("dp")
    slot_count = (lang_total + dp_size - 1) // dp_size
    owned_rows = slot_count * dp_size
    lang_index = jnp.arange(lang_total, dtype=jnp.int32)
    same_owner = (owner[:, None] == owner[None, :]) & (lang_index[None, :] < lang_index[:, None])
    lang_slot = jnp.sum(same_owner.astype(jnp.int32), axis=1)
    lang_place = owner * slot_count + lang_slot
    lang_hot = (language[:, None] == lang_index[None, :]).astype(jnp.int32)
    seq_place = jnp.sum(lang_hot * lang_place[None, :], axis=1)
    place_hot = (seq_place[:, None] == jnp.arange(owned_rows, dtype=jnp.int32)[None, :]).astype(
        jnp.float32
    )
    slot_table = jnp.dot(place_hot.T, pre_flat, precision=highest)
    slot_counts = jnp.sum(place_hot, axis=0)
    summed, counted = (
        lax.psum_scatter(slot_table, "dp", scatter_dimension=0, tiled=True),
        lax.psum_scatter(slot_counts, "dp", scatter_dimension=0, tiled=True),
    )
    owned_means = summed / jnp.maximum(counted, 1.0)[:, None]
    return (grad_flat, owned_means)


def solution(mesh):
    return jax.shard_map(
        per_device,
        mesh=mesh,
        in_specs=(
            P("dp", None, "tensor"),
            P("dp", None, "tensor"),
            P(None, "tensor"),
            P(None, "tensor"),
            P(),
            P(),
            P("dp"),
            P("dp"),
            P(),
        ),
        out_specs=(P("dp", "tensor"), P("dp", "tensor")),
        check_vma=False,
    )
```

profile of v0, /device:TPU:6, one launch (start us, length us, event | category | flops | bytes accessed | tf_op | source)
XLA Modules:
  0.0 252.7 jit_solution(2008518742955847189)
XLA Ops:
  7.2 0.0 copy-start
  7.2 0.0 all-reduce.8.cloned.1.call-start
  7.2 1.7 copy-done
  8.9 0.0 copy-start.1
  9.0 0.0 copy-start.2
  9.0 0.0 copy-start.6
  9.0 0.0 copy-start.7
  9.0 0.0 copy-start.5
  9.0 2.0 fusion.9
  10.9 0.0 copy-start.3
  11.0 0.0 copy-start.4
  11.0 0.7 copy.29
  11.7 0.0 copy-done.1
  11.7 0.0 copy-done.2
  11.7 0.4 fusion.10
  12.0 0.8 reshape.53
  12.8 0.0 all-reduce.8.cloned.1.call-update
  12.8 0.0 all-reduce.6.cloned.1.call-start
  12.9 0.0 copy-done.6
  12.9 0.2 convert_reduce_fusion
  13.1 0.0 copy-done.7
  13.1 0.2 select_reduce_fusion
  13.3 0.0 copy-done.5
  13.3 0.1 fusion.6
  13.4 73.3 %all-reduce.8.cloned.1.call-done = (f32[3,256,64]{1,2,0:T(8,128)}, f32[3,256,64]{1,0,2:T(4,128)}) async-done(((f32[3,256,64]{1,2,0:T(8,128)}, f32[3,256,64]{1,0,2:T(4,128)}), (f32[3,256,64]{1,2,0:T(8,128)}, f32[3,256,64]{1,0,2:T(4,128)})) %all-reduce.8.cloned.1.call-update) | async-done | bytes 393232 | tf_op jit(solution)/shard_map/psum | solution.py:27
  86.7 1.0 broadcast_multiply_fusion
  87.7 1.3 fusion
  89.0 0.0 copy-done.3
  89.0 0.3 convolution_bitcast_fusion
  89.3 0.0 copy-done.4
  89.3 0.3 fusion.3
  89.7 0.1 reshape.55
  89.8 1.1 fusion.7
  90.8 0.0 all-reduce.6.cloned.1.call-update
  90.9 0.1 convert_reduce_fusion.1
  91.0 1.3 dynamic-slice
  92.9 144.3 %all-reduce.1 = f32[128]{0:T(128)S(1)} all-reduce(f32[128]{0:T(128)S(1)} %convert_reduce_fusion.1), channel_id=3, replica_groups=mesh['dp'=64,'tensor'=8] {'dp'}, use_global_device_ids=true, to_apply=%region_6.0.clone | all-reduce | flops 128 | bytes 1024
  237.1 0.1 dynamic-slice_maximum_fusion
  237.2 0.7 reshape.54
  237.9 6.6 %all-reduce.6.cloned.1.call-done = f32[128,512]{1,0:T(8,128)} async-done(((f32[128,512]{1,0:T(8,128)}), f32[128,512]{1,0:T(8,128)}) %all-reduce.6.cloned.1.call-update) | async-done | bytes 262160
  244.5 1.4 dynamic-slice_divide_fusion
  (3 shorter events, 0.0 us)
Async XLA Ops:
  7.2 1.8 copy-start
  7.2 79.5 %all-reduce.8.cloned.1.call-start = ((), (), s32[]{:S(2)}) async-start(), calls=%async_computation.1 | async-start | bytes 917504 | tf_op jit(solution)/shard_map/psum | solution.py:27
  8.9 2.7 %copy-start.1 = (bf16[3,256,512]{2,1,0:T(8,128)(2,1)S(1)}, bf16[3,256,512]{2,1,0:T(8,128)(2,1)}, u32[]{:S(2)}) copy-start(bf16[3,256,512]{2,1,0:T(8,128)(2,1)} %param.10) | copy-start | bytes 2359300
  9.0 2.7 %copy-start.2 = (bf16[64,512]{1,0:T(8,128)(2,1)S(1)}, bf16[64,512]{1,0:T(8,128)(2,1)}, u32[]{:S(2)}) copy-start(bf16[64,512]{1,0:T(8,128)(2,1)} %param.12) | copy-start | bytes 196612
  9.0 4.0 %copy-start.6 = (s32[100]{0:T(128)S(1)}, s32[100]{0:T(128)}, u32[]{:S(2)}) copy-start(s32[100]{0:T(128)} %param.17) | copy-start | bytes 1204
  9.0 4.1 %copy-start.7 = (s32[3]{0:T(128)S(1)}, s32[3]{0:T(128)}, u32[]{:S(2)}) copy-start(s32[3]{0:T(128)} %param.16) | copy-start | bytes 40
  9.0 4.3 %copy-start.5 = (s32[3]{0:T(128)S(1)}, s32[3]{0:T(128)}, u32[]{:S(2)}) copy-start(s32[3]{0:T(128)} %param.15) | copy-start | bytes 40
  10.9 78.0 %copy-start.3 = (f32[64,64]{1,0:T(8,128)S(1)}, f32[64,64]{1,0:T(8,128)}, u32[]{:S(2)}) copy-start(f32[64,64]{1,0:T(8,128)} %param.13) | copy-start | bytes 49156
  11.0 78.4 %copy-start.4 = (f32[64,64]{1,0:T(8,128)S(1)}, f32[64,64]{1,0:T(8,128)}, u32[]{:S(2)}) copy-start(f32[64,64]{1,0:T(8,128)} %param.14) | copy-start | bytes 49156
  12.8 231.6 %all-reduce.6.cloned.1.call-start = ((), (), s32[]{:S(2)}) async-start(), calls=%async_computation | async-start | bytes 524288
Sparse Core Ops, SparseCore 0:
  13.0 73.6 all-reduce.7
  91.0 153.4 all-reduce.5
where the time goes:
time: 253 us
  blocking collectives  144 us (57%)
  waiting for transfers between devices  80 us (32%)
  between operations  14.8 us (6%)
  matrix products  5.34 us (2%)
  local copies, waits for them, and re-layouts  5.3 us (2%)
  other arithmetic  2.97 us (1%)
    unnamed x1, blocking collectives  144 us
    psum x1, waiting for transfers between devices, per_device(): left_full, right_full = lax.psum((left_part, right_part), 'tensor')  73.3 us
    unnamed x3, waiting for transfers between devices  6.63 us
  transfers between devices with their start and end apart: 2, of which 2 were waited for; matrix products, arithmetic and copies ran while one was open for 1% of the time, Pallas kernels for 0%

commit v1 on v0

--- a/solution.py
+++ b/solution.py
@@ -4,11 +4,21 @@
 from jax.sharding import PartitionSpec as P
 
 
-def project(values, projection):
+def project_t(values, projection):
     flattened = values.reshape(-1, values.shape[-1])
     return lax.dot_general(
-        flattened, projection, (((1,), (1,)), ((), ())), preferred_element_type=jnp.float32
+        projection, flattened, (((1,), (1,)), ((), ())), preferred_element_type=jnp.float32
     )
+
+
+def tensor_sum(parts, tensor_size):
+    feat, tokens = parts.shape
+    block = feat // tensor_size
+    chunks = parts.reshape(tensor_size, block, tokens)
+    mine = jnp.sum(lax.all_to_all(chunks, "tensor", 0, 0, tiled=True), axis=0)
+    spread = jnp.broadcast_to(mine[None], (tensor_size, block, tokens))
+    whole = lax.all_to_all(spread, "tensor", 0, 0, tiled=True)
+    return whole.reshape(feat, tokens)
 
 
 def per_device(hidden, out_grad, proj_in, proj_out, left_inv, right_inv, lengths, language, owner):
@@ -19,19 +29,20 @@
     tensor_size = lax.axis_size("tensor")
     row_width = proj_rank // tensor_size
     row_start = lax.axis_index("tensor") * row_width
-    left_part = project(hidden, proj_in)
-    right_part = project(out_grad, proj_out)
+    left_part = project_t(hidden, proj_in)
+    right_part = project_t(out_grad, proj_out)
+    both = tensor_sum(jnp.concatenate([left_part, right_part], axis=0), tensor_size)
+    left_t = both[:proj_rank].reshape(proj_rank, seq_count, seq_length)
+    right_t = both[proj_rank:].reshape(proj_rank, seq_count, seq_length)
     token_mask = (jnp.arange(seq_length, dtype=jnp.int32)[None, :] < lengths[:, None]).astype(
         jnp.float32
     )
-    left_full, right_full = lax.psum((left_part, right_part), "tensor")
-    left_full = left_full.reshape(seq_count, seq_length, proj_rank)
-    right_full = right_full.reshape(seq_count, seq_length, proj_rank) * token_mask[:, :, None]
-    full_grads = jnp.einsum("sti,stj->sij", left_full, right_full, precision=highest)
-    left_done = jnp.einsum("ik,skj->sij", left_inv, full_grads, precision=highest)
-    full_pre = jnp.einsum("sik,kj->sij", left_done, right_inv, precision=highest)
+    right_t = right_t * token_mask[None, :, :]
+    full_grads = jnp.einsum("ist,jst->sij", left_t, right_t, precision=highest)
+    inv_rows = lax.dynamic_slice_in_dim(left_inv, row_start, row_width, 0)
     grad_rows = lax.dynamic_slice_in_dim(full_grads, row_start, row_width, 1)
-    pre_rows = lax.dynamic_slice_in_dim(full_pre, row_start, row_width, 1)
+    left_done = jnp.einsum("ik,skj->sij", inv_rows, full_grads, precision=highest)
+    pre_rows = jnp.einsum("sik,kj->sij", left_done, right_inv, precision=highest)
     grad_flat = grad_rows.reshape(seq_count, row_width * proj_rank)
     pre_flat = pre_rows.reshape(seq_count, row_width * proj_rank)
     lang_total = owner.shape[0]
@@ -49,10 +60,15 @@
     )
     slot_table = jnp.dot(place_hot.T, pre_flat, precision=highest)
     slot_counts = jnp.sum(place_hot, axis=0)
-    summed, counted = (
-        lax.psum_scatter(slot_table, "dp", scatter_dimension=0, tiled=True),
-        lax.psum_scatter(slot_counts, "dp", scatter_dimension=0, tiled=True),
+    width = slot_table.shape[1]
+    count_row = jnp.zeros((dp_size, 1, width), jnp.float32)
+    count_row = count_row.at[:, 0, :slot_count].set(slot_counts.reshape(dp_size, slot_count))
+    payload = jnp.concatenate(
+        [slot_table.reshape(dp_size, slot_count, width), count_row], axis=1
     )
+    gathered = jnp.sum(lax.all_to_all(payload, "dp", 0, 0, tiled=True), axis=0)
+    summed = gathered[:slot_count]
+    counted = gathered[slot_count, :slot_count]
     owned_means = summed / jnp.maximum(counted, 1.0)[:, None]
     return (grad_flat, owned_means)
 

time: 253 us -> 73.9 us (0.29)
  the two profiles are of different devices: /device:TPU:6 before, /device:TPU:8 now
where the time goes in v1:
time: 73.9 us; the launch traced here: 73.4 us
  waiting for transfers between devices  35.6 us (48%)
  starting transfers between devices  24.5 us (33%)
  local copies, waits for them, and re-layouts  6.34 us (9%)
  matrix products  4.03 us (5%)
  other arithmetic  2.19 us (3%)
  between operations  0.82 us (1%)
    all_to_all x1, waiting for transfers between devices, per_device(): gathered = jnp.sum(lax.all_to_all(payload, 'dp', 0, 0, tiled=True), axis=0)  18.5 us
    all_to_all x1, starting transfers between devices, per_device(): gathered = jnp.sum(lax.all_to_all(payload, 'dp', 0, 0, tiled=True), axis=0)  16.6 us
    all_to_all x1, waiting for transfers between devices, tensor_sum(): mine = jnp.sum(lax.all_to_all(chunks, 'tensor', 0, 0, tiled=True), axis=0)  8.56 us
    all_to_all x1, waiting for transfers between devices, tensor_sum(): whole = lax.all_to_all(spread, 'tensor', 0, 0, tiled=True)  8.55 us
    all_to_all x1, starting transfers between devices, tensor_sum(): mine = jnp.sum(lax.all_to_all(chunks, 'tensor', 0, 0, tiled=True), axis=0)  4.43 us
    all_to_all x1, starting transfers between devices, tensor_sum(): whole = lax.all_to_all(spread, 'tensor', 0, 0, tiled=True)  3.45 us
    dot_general x2, matrix products, project_t(): lax.dot_general(projection, flattened, (((1,), (1,)), ((), ())), preferre...  2.28 us
    unnamed x14, local copies, waits for them, and re-layouts  1.79 us
  transfers between devices with their start and end apart: 3, of which 3 were waited for; matrix products, arithmetic and copies ran while one was open for 2% of the time, Pallas kernels for 0%

profile of v1, /device:TPU:8, one launch (start us, length us, event | category | flops | bytes accessed | tf_op | source)
XLA Modules:
  0.0 73.4 jit_solution(16223021856503936236)
XLA Ops:
  0.6 0.0 copy-start
  0.6 0.0 copy-start.2
  0.7 0.0 copy-start.1
  0.7 1.7 %copy-done = bf16[3,256,1792]{2,1,0:T(8,128)(2,1)S(1)} copy-done((bf16[3,256,1792]{2,1,0:T(8,128)(2,1)S(1)}, bf16[3,256,1792]{2,1,0:T(8,128)(2,1)}, u32[]{:S(2)}) %copy-start) | copy-done | bytes 2752536
  2.4 0.0 copy-start.5
  2.4 0.0 copy-start.6
  2.4 1.9 %fusion.16 = f32[64,768]{1,0:T(8,128)S(1)} fusion(bf16[64,1792]{1,0:T(8,128)(2,1)} %param.13, bf16[768,1792]{1,0:T(8,128)(2,1)S(1)} %bitcast.20), kind=kOutput, calls=%fused_computation.33 | convolution fusion | flops 176160768 | bytes 3178496 | tf_op jit(solution)/shard_map/dot_general | solution.py:9
  4.3 0.0 copy-start.4
  4.4 0.0 copy-done.2
  4.4 0.0 copy-done.1
  4.4 0.4 fusion.17
  4.7 0.8 %pad_maximum_fusion = f32[128,768]{1,0:T(8,128)} fusion(f32[64,768]{1,0:T(8,128)S(1)} %fusion.17, f32[64,768]{1,0:T(8,128)S(1)} %fusion.16), kind=kLoop, calls=%fused_computation.3 | loop fusion | flops 98304 | bytes 786432 | tf_op jit(solution)/shard_map/concatenate | solution.py:34
  5.5 0.0 copy-start.3
  5.5 4.4 %all-to-all-start = ((f32[8,16,768]{2,1,0:T(8,128)}), f32[8,16,768]{2,1,0:T(8,128)S(1)}, u32[]{:S(2)}, u32[]{:S(2)}) async-start(f32[8,16,768]{2,1,0:T(8,128)} %bitcast.2), calls=%async_computation | async-start | bytes 786432 | tf_op jit(solution)/shard_map/all_to_all | solution.py:18
  9.9 0.0 copy-done.5
  9.9 0.2 convert_reduce_fusion
  10.1 0.0 copy-done.6
  10.1 0.2 select_reduce_fusion
  10.3 8.6 %all-to-all-done = f32[8,16,768]{2,1,0:T(8,128)S(1)} async-done(((f32[8,16,768]{2,1,0:T(8,128)}), f32[8,16,768]{2,1,0:T(8,128)S(1)}, u32[]{:S(2)}, u32[]{:S(2)}) %all-to-all-start) | async-done | bytes 393248 | tf_op jit(solution)/shard_map/all_to_all | solution.py:18
  18.9 0.8 %broadcast_in_dim.2 = f32[8,16,768]{2,1,0:T(8,128)} broadcast(f32[16,768]{1,0:T(8,128)S(1)} %reduce_sum.45), dimensions={1,2} | broadcast | bytes 442368 | tf_op jit(solution)/shard_map/broadcast_in_dim | solution.py:19
  19.7 3.5 %all-to-all-start.1 = ((f32[8,16,768]{2,1,0:T(8,128)}), f32[8,16,768]{2,1,0:T(8,128)S(1)}, u32[]{:S(2)}, u32[]{:S(2)}) async-start(f32[8,16,768]{2,1,0:T(8,128)} %broadcast_in_dim.2), calls=%async_computation.1 | async-start | bytes 786432 | tf_op jit(solution)/shard_map/all_to_all | solution.py:20
  23.1 0.1 convert_reduce_fusion.1
  23.2 0.1 reshape.128
  23.4 0.0 copy-done.4
  23.4 0.1 fusion.8
  23.5 8.5 %all-to-all-done.1 = f32[8,16,768]{2,1,0:T(8,128)S(1)} async-done(((f32[8,16,768]{2,1,0:T(8,128)}), f32[8,16,768]{2,1,0:T(8,128)S(1)}, u32[]{:S(2)}, u32[]{:S(2)}) %all-to-all-start.1) | async-done | bytes 393248 | tf_op jit(solution)/shard_map/all_to_all | solution.py:20
  32.0 0.7 fusion.15
  32.7 1.0 %reshape.124 = f32[64,3,256]{2,1,0:T(4,128)S(1)} reshape(f32[4,16,768]{2,1,0:T(8,128)} %get-tuple-element.14) | data formatting | bytes 393216 | tf_op jit(solution)/shard_map/reshape | solution.py:35
  33.7 0.1 reshape.125
  33.9 0.3 fusion
  34.3 0.9 %convolution_bitcast_fusion = f32[3,8,64]{2,1,0:T(8,128)S(1)} fusion(f32[3,64,64]{2,1,0:T(8,128)S(1)} %fusion, f32[64,64]{1,0:T(8,128)} %param.15, s32[]{:T(128)S(6)} %select_n.4), kind=kOutput, calls=%fused_computation | convolution fusion | flops 1179648 | bytes 59396 | tf_op jit(solution)/shard_map/ik,skj->sij/dot_general | solution.py:44
  35.1 0.0 copy-done.3
  35.1 0.1 fusion.4
  35.3 0.1 reshape.131
  35.4 0.4 fusion.9
  35.8 1.1 %copy.18 = f32[64,3,512]{2,1,0:T(4,128)} copy(f32[64,3,512]{2,0,1:T(8,128)S(1)} %select_maximum_fusion) | data formatting | bytes 786432 | tf_op jit(solution)/shard_map/concatenate | solution.py:66
  36.9 16.6 %all-to-all-start.2 = ((f32[64,3,512]{2,1,0:T(4,128)}), f32[64,3,512]{2,1,0:T(4,128)S(1)}, u32[]{:S(2)}, u32[]{:S(2)}) async-start(f32[64,3,512]{2,1,0:T(4,128)} %copy.18), calls=%async_computation.2 | async-start | bytes 1048576 | tf_op jit(solution)/shard_map/all_to_all | solution.py:69
  53.5 0.7 reshape.126
  54.1 18.5 %all-to-all-done.2 = f32[64,3,512]{2,1,0:T(4,128)S(1)} async-done(((f32[64,3,512]{2,1,0:T(4,128)}), f32[64,3,512]{2,1,0:T(4,128)S(1)}, u32[]{:S(2)}, u32[]{:S(2)}) %all-to-all-start.2) | async-done | bytes 393248 | tf_op jit(solution)/shard_map/all_to_all | solution.py:69
  72.7 0.1 reduce_sum.49
  72.8 0.7 slice_divide_fusion
  (7 shorter events, 0.1 us)
Async XLA Ops:
  0.6 1.8 %copy-start = (bf16[3,256,1792]{2,1,0:T(8,128)(2,1)S(1)}, bf16[3,256,1792]{2,1,0:T(8,128)(2,1)}, u32[]{:S(2)}) copy-start(bf16[3,256,1792]{2,1,0:T(8,128)(2,1)} %param.11) | copy-start | bytes 8257540
  0.6 3.7 %copy-start.2 = (bf16[64,512]{1,0:T(8,128)(2,1)S(1)}, bf16[64,512]{1,0:T(8,128)(2,1)}, u32[]{:S(2)}) copy-start(bf16[64,512]{1,0:T(8,128)(2,1)} %param.14) | copy-start | bytes 196612
  0.7 3.7 %copy-start.1 = (bf16[3,256,512]{2,1,0:T(8,128)(2,1)S(1)}, bf16[3,256,512]{2,1,0:T(8,128)(2,1)}, u32[]{:S(2)}) copy-start(bf16[3,256,512]{2,1,0:T(8,128)(2,1)} %param.12) | copy-start | bytes 2359300
  2.4 7.5 %copy-start.5 = (s32[100]{0:T(128)S(1)}, s32[100]{0:T(128)}, u32[]{:S(2)}) copy-start(s32[100]{0:T(128)} %param.19) | copy-start | bytes 1204
  2.4 7.7 %copy-start.6 = (s32[3]{0:T(128)S(1)}, s32[3]{0:T(128)}, u32[]{:S(2)}) copy-start(s32[3]{0:T(128)} %param.18) | copy-start | bytes 40
  4.3 19.0 %copy-start.4 = (s32[3]{0:T(128)S(1)}, s32[3]{0:T(128)}, u32[]{:S(2)}) copy-start(s32[3]{0:T(128)} %param.17) | copy-start | bytes 40
  5.5 29.6 %copy-start.3 = (f32[64,64]{1,0:T(8,128)S(1)}, f32[64,64]{1,0:T(8,128)}, u32[]{:S(2)}) copy-start(f32[64,64]{1,0:T(8,128)} %param.16) | copy-start | bytes 49156
  5.5 13.4 %all-to-all-start = ((f32[8,16,768]{2,1,0:T(8,128)}), f32[8,16,768]{2,1,0:T(8,128)S(1)}, u32[]{:S(2)}, u32[]{:S(2)}) async-start(f32[8,16,768]{2,1,0:T(8,128)} %bitcast.2), calls=%async_computation | async-start | bytes 786432 | tf_op jit(solution)/shard_map/all_to_all | solution.py:18
  19.7 12.3 %all-to-all-start.1 = ((f32[8,16,768]{2,1,0:T(8,128)}), f32[8,16,768]{2,1,0:T(8,128)S(1)}, u32[]{:S(2)}, u32[]{:S(2)}) async-start(f32[8,16,768]{2,1,0:T(8,128)} %broadcast_in_dim.2), calls=%async_computation.1 | async-start | bytes 786432 | tf_op jit(solution)/shard_map/all_to_all | solution.py:20
  36.9 35.8 %all-to-all-start.2 = ((f32[64,3,512]{2,1,0:T(4,128)}), f32[64,3,512]{2,1,0:T(4,128)S(1)}, u32[]{:S(2)}, u32[]{:S(2)}) async-start(f32[64,3,512]{2,1,0:T(4,128)} %copy.18), calls=%async_computation.2 | async-start | bytes 1048576 | tf_op jit(solution)/shard_map/all_to_all | solution.py:69

commit v2 on v1

--- a/solution.py
+++ b/solution.py
@@ -32,13 +32,22 @@
     left_part = project_t(hidden, proj_in)
     right_part = project_t(out_grad, proj_out)
     both = tensor_sum(jnp.concatenate([left_part, right_part], axis=0), tensor_size)
-    left_t = both[:proj_rank].reshape(proj_rank, seq_count, seq_length)
-    right_t = both[proj_rank:].reshape(proj_rank, seq_count, seq_length)
-    token_mask = (jnp.arange(seq_length, dtype=jnp.int32)[None, :] < lengths[:, None]).astype(
-        jnp.float32
+    left_t = both[:proj_rank]
+    right_t = both[proj_rank:]
+    token_seq = jnp.repeat(lengths, seq_length, total_repeat_length=seq_count * seq_length)
+    token_pos = jnp.arange(seq_count * seq_length, dtype=jnp.int32) % seq_length
+    right_t = right_t * (token_pos < token_seq).astype(jnp.float32)[None, :]
+    full_grads = jnp.stack(
+        [
+            lax.dot_general(
+                left_t[:, s * seq_length : (s + 1) * seq_length],
+                right_t[:, s * seq_length : (s + 1) * seq_length],
+                (((1,), (1,)), ((), ())),
+                precision=highest,
+            )
+            for s in range(seq_count)
+        ]
     )
-    right_t = right_t * token_mask[None, :, :]
-    full_grads = jnp.einsum("ist,jst->sij", left_t, right_t, precision=highest)
     inv_rows = lax.dynamic_slice_in_dim(left_inv, row_start, row_width, 0)
     grad_rows = lax.dynamic_slice_in_dim(full_grads, row_start, row_width, 1)
     left_done = jnp.einsum("ik,skj->sij", inv_rows, full_grads, precision=highest)
@@ -61,14 +70,17 @@
     slot_table = jnp.dot(place_hot.T, pre_flat, precision=highest)
     slot_counts = jnp.sum(place_hot, axis=0)
     width = slot_table.shape[1]
-    count_row = jnp.zeros((dp_size, 1, width), jnp.float32)
-    count_row = count_row.at[:, 0, :slot_count].set(slot_counts.reshape(dp_size, slot_count))
+    count_pad = 128
     payload = jnp.concatenate(
-        [slot_table.reshape(dp_size, slot_count, width), count_row], axis=1
+        [
+            slot_table.reshape(dp_size, slot_count * width),
+            jnp.pad(slot_counts.reshape(dp_size, slot_count), ((0, 0), (0, count_pad - slot_count))),
+        ],
+        axis=1,
     )
     gathered = jnp.sum(lax.all_to_all(payload, "dp", 0, 0, tiled=True), axis=0)
-    summed = gathered[:slot_count]
-    counted = gathered[slot_count, :slot_count]
+    summed = gathered[: slot_count * width].reshape(slot_count, width)
+    counted = gathered[slot_count * width : slot_count * width + slot_count]
     owned_means = summed / jnp.maximum(counted, 1.0)[:, None]
     return (grad_flat, owned_means)
 

time: 73.9 us -> 67.7 us (0.916)
  waiting for transfers between devices: 35.6 us -> 28.7 us
  local copies, waits for them, and re-layouts: 6.34 us -> 3.68 us
  other arithmetic: 2.19 us -> 4.07 us
  matrix products: 4.03 us -> 5.62 us
    all_to_all x1, waiting for transfers between devices: 18.5 us -> 14.1 us  [per_device(): gathered = jnp.sum(lax.all_to_all(payload, 'dp', 0, 0, tiled=True), axis=0)]
    all_to_all x1, waiting for transfers between devices: 8.55 us -> 6.1 us  [tensor_sum(): whole = lax.all_to_all(spread, 'tensor', 0, 0, tiled=True)]
    convert_element_type x1, other arithmetic: 0.07 us -> 1.92 us  [per_device(): right_t = right_t * (token_pos < token_seq).astype(jnp.float32)[None, :]]
    unnamed x14, local copies, waits for them, and re-layouts: 1.79 us -> 0.38 us
    dot_general x2, matrix products: 2.28 us -> 3.6 us  [project_t(): lax.dot_general(projection, flattened, (((1,), (1,)), ((), ())), preferre...]
    concatenate x1 -> x0, local copies, waits for them, and re-layouts: 1.06 us -> none  [per_device(): jnp.concatenate([slot_table.reshape(dp_size, slot_count, width), count_ro...]
    all_to_all x0 -> x1, local copies, waits for them, and re-layouts: none -> 0.91 us  [per_device(): gathered = jnp.sum(lax.all_to_all(payload, 'dp', 0, 0, tiled=True), axis=0)]
    reshape x2 -> x3, local copies, waits for them, and re-layouts: 1.13 us -> 0.23 us  [the longest x1 0.13 us: per_device(): slot_counts.reshape(dp_size, slot_count)]
  transfers between devices with their start and end apart: 3 -> 3, of which waited for: 3 -> 3; matrix products, arithmetic and copies ran while one was open for 2% -> 6% of each run, Pallas kernels for 0% -> 0%
where the time goes in v2:
time: 67.7 us; the launch traced here: 67.3 us
  waiting for transfers between devices  28.7 us (42%)
  starting transfers between devices  24.3 us (36%)
  matrix products  5.62 us (8%)
  other arithmetic  4.07 us (6%)
  local copies, waits for them, and re-layouts  3.68 us (5%)
  between operations  0.84 us (1%)
    all_to_all x1, starting transfers between devices, per_device(): gathered = jnp.sum(lax.all_to_all(payload, 'dp', 0, 0, tiled=True), axis=0)  16.6 us
    all_to_all x1, waiting for transfers between devices, per_device(): gathered = jnp.sum(lax.all_to_all(payload, 'dp', 0, 0, tiled=True), axis=0)  14.1 us
    all_to_all x1, waiting for transfers between devices, tensor_sum(): mine = jnp.sum(lax.all_to_all(chunks, 'tensor', 0, 0, tiled=True), axis=0)  8.56 us
    all_to_all x1, waiting for transfers between devices, tensor_sum(): whole = lax.all_to_all(spread, 'tensor', 0, 0, tiled=True)  6.1 us
    all_to_all x1, starting transfers between devices, tensor_sum(): mine = jnp.sum(lax.all_to_all(chunks, 'tensor', 0, 0, tiled=True), axis=0)  4.3 us
    dot_general x2, matrix products, project_t(): lax.dot_general(projection, flattened, (((1,), (1,)), ((), ())), preferre...  3.6 us
    all_to_all x1, starting transfers between devices, tensor_sum(): whole = lax.all_to_all(spread, 'tensor', 0, 0, tiled=True)  3.45 us
    convert_element_type x1, other arithmetic, per_device(): right_t = right_t * (token_pos < token_seq).astype(jnp.float32)[None, :]  1.92 us
  transfers between devices with their start and end apart: 3, of which 3 were waited for; matrix products, arithmetic and copies ran while one was open for 6% of the time, Pallas kernels for 0%

profile of v2, /device:TPU:8, one launch (start us, length us, event | category | flops | bytes accessed | tf_op | source)
XLA Modules:
  0.0 67.3 jit_solution(9608383558225744455)
XLA Ops:
  0.6 0.0 copy-start
  0.6 0.0 copy-start.5
  0.7 0.0 copy-start.6
  0.7 1.7 %fusion.22 = f32[64,768]{1,0:T(8,128)S(1)} fusion(bf16[64,512]{1,0:T(8,128)(2,1)} %param.14, bf16[768,512]{1,0:T(8,128)(2,1)} %bitcast.30), kind=kOutput, calls=%fused_computation.43 | convolution fusion | flops 50331648 | bytes 1048576 | tf_op jit(solution)/shard_map/dot_general | solution.py:9
  2.3 0.3 copy-done
  2.7 0.0 copy-start.2
  2.7 0.0 copy-start.3
  2.7 0.0 copy-start.4
  2.7 1.9 %fusion.21 = f32[64,768]{1,0:T(8,128)S(1)} fusion(bf16[64,1792]{1,0:T(8,128)(2,1)} %param.13, bf16[768,1792]{1,0:T(8,128)(2,1)S(1)} %bitcast.29), kind=kOutput, calls=%fused_computation.42 | convolution fusion | flops 176160768 | bytes 3178496 | tf_op jit(solution)/shard_map/dot_general | solution.py:9
  4.6 0.0 copy-start.1
  4.6 0.8 %pad_maximum_fusion = f32[128,768]{1,0:T(8,128)} fusion(f32[64,768]{1,0:T(8,128)S(1)} %fusion.22, f32[64,768]{1,0:T(8,128)S(1)} %fusion.21), kind=kLoop, calls=%fused_computation.4 | loop fusion | flops 98304 | bytes 786432 | tf_op jit(solution)/shard_map/concatenate | solution.py:34
  5.4 4.3 %all-to-all-start = ((f32[8,16,768]{2,1,0:T(8,128)}), f32[8,16,768]{2,1,0:T(8,128)S(1)}, u32[]{:S(2)}, u32[]{:S(2)}) async-start(f32[8,16,768]{2,1,0:T(8,128)} %bitcast.2), calls=%async_computation | async-start | bytes 786432 | tf_op jit(solution)/shard_map/all_to_all | solution.py:18
  9.7 0.0 copy-done.5
  9.7 0.2 convert_reduce_fusion
  9.9 0.0 copy-done.6
  9.9 0.2 select_reduce_fusion
  10.1 8.6 %all-to-all-done = f32[8,16,768]{2,1,0:T(8,128)S(1)} async-done(((f32[8,16,768]{2,1,0:T(8,128)}), f32[8,16,768]{2,1,0:T(8,128)S(1)}, u32[]{:S(2)}, u32[]{:S(2)}) %all-to-all-start) | async-done | bytes 393248 | tf_op jit(solution)/shard_map/all_to_all | solution.py:18
  18.7 0.8 %broadcast_in_dim.4 = f32[8,16,768]{2,1,0:T(8,128)} broadcast(f32[16,768]{1,0:T(8,128)S(1)} %reduce_sum.45), dimensions={1,2} | broadcast | bytes 442368 | tf_op jit(solution)/shard_map/broadcast_in_dim | solution.py:19
  19.4 3.5 %all-to-all-start.1 = ((f32[8,16,768]{2,1,0:T(8,128)}), f32[8,16,768]{2,1,0:T(8,128)S(1)}, u32[]{:S(2)}, u32[]{:S(2)}) async-start(f32[8,16,768]{2,1,0:T(8,128)} %broadcast_in_dim.4), calls=%async_computation.1 | async-start | bytes 786432 | tf_op jit(solution)/shard_map/all_to_all | solution.py:20
  22.9 0.1 convert_reduce_fusion.1
  23.0 0.1 reshape.145
  23.1 0.0 copy-done.2
  23.1 0.6 fusion.20
  23.7 0.0 copy-done.3
  23.7 0.0 copy-done.4
  23.7 1.9 %fusion.14 = f32[768]{0:T(1024)S(1)} fusion(pred[768]{0:T(1024)(128)(4,1)S(1)} %copy-done.3, pred[768]{0:T(1024)(128)(4,1)S(1)} %copy-done.4, s32[]{:T(128)} %bitcast.7, s32[]{:T(128)} %bitcast.5, s32[]{:T(128)} %bitcast.6), kind=kLoop, calls=%fused_computation.27 | loop fusion | flops 7680 | bytes 4620 | tf_op jit(solution)/shard_map/convert_element_type | solution.py:39
  25.7 6.1 %all-to-all-done.1 = f32[8,16,768]{2,1,0:T(8,128)S(1)} async-done(((f32[8,16,768]{2,1,0:T(8,128)}), f32[8,16,768]{2,1,0:T(8,128)S(1)}, u32[]{:S(2)}, u32[]{:S(2)}) %all-to-all-start.1) | async-done | bytes 393248 | tf_op jit(solution)/shard_map/all_to_all | solution.py:20
  31.8 0.2 convolution_bitcast_fusion
  32.0 0.2 convolution_bitcast_fusion.1
  32.2 0.2 convolution_bitcast_fusion.2
  32.4 0.9 %convolution_bitcast_fusion.3 = f32[3,8,64]{2,1,0:T(8,128)S(1)} fusion(f32[64,64]{1,0:T(8,128)} %param.15, s32[]{:T(128)S(6)} %select_n.40, f32[1,64,64]{2,1,0:T(8,128)S(1)} %convolution_bitcast_fusion, f32[1,64,64]{2,1,0:T(8,128)S(1)} %convolution_bitcast_fusion.1, f32[1,64,64]{2,1,0:T(8,128)S(1)} %convolution_bitcast_fusion.2), kind=kOutput, calls=%fused_computation.3 | convolution fusion | flops 1204224 | bytes 59396 | tf_op jit(solution)/shard_map/ik,skj->sij/dot_general | solution.py:53
  33.3 0.0 copy-done.1
  33.3 0.1 fusion.7
  33.5 0.1 reshape.143
  33.6 0.4 fusion.16
  34.0 0.1 reshape.144
  34.1 0.9 %all_to_all.14 = f32[64,1,1152]{2,1,0:T(1,128)} reshape(f32[64,1152]{1,0:T(8,128)S(1)} %select_maximum_fusion) | data formatting | bytes 589824 | tf_op jit(solution)/shard_map/all_to_all | solution.py:81
  35.0 16.6 %all-to-all-start.2 = ((f32[64,1,1152]{2,1,0:T(1,128)}), f32[64,1,1152]{2,1,0:T(1,128)S(1)}, u32[]{:S(2)}, u32[]{:S(2)}) async-start(f32[64,1,1152]{2,1,0:T(1,128)} %all_to_all.14), calls=%async_computation.2 | async-start | bytes 589824 | tf_op jit(solution)/shard_map/all_to_all | solution.py:81
  51.6 0.7 %reshape.142 = f32[3,512]{1,0:T(4,128)} reshape(f32[3,8,64]{2,1,0:T(8,128)S(1)} %constant_dynamic-slice_fusion) | data formatting | bytes 12288 | tf_op jit(solution)/shard_map/reshape | solution.py:55
  52.3 14.1 %all-to-all-done.2 = f32[64,1,1152]{2,1,0:T(1,128)S(1)} async-done(((f32[64,1,1152]{2,1,0:T(1,128)}), f32[64,1,1152]{2,1,0:T(1,128)S(1)}, u32[]{:S(2)}, u32[]{:S(2)}) %all-to-all-start.2) | async-done | bytes 294944 | tf_op jit(solution)/shard_map/all_to_all | solution.py:81
  66.4 0.2 reduce_sum.49
  66.6 0.7 broadcast_divide_fusion
  (10 shorter events, 0.1 us)
Async XLA Ops:
  0.6 2.1 %copy-start = (bf16[3,256,1792]{2,1,0:T(8,128)(2,1)S(1)}, bf16[3,256,1792]{2,1,0:T(8,128)(2,1)}, u32[]{:S(2)}) copy-start(bf16[3,256,1792]{2,1,0:T(8,128)(2,1)} %param.11) | copy-start | bytes 8257540
  0.6 9.1 %copy-start.5 = (s32[100]{0:T(128)S(1)}, s32[100]{0:T(128)}, u32[]{:S(2)}) copy-start(s32[100]{0:T(128)} %param.19) | copy-start | bytes 1204
  0.7 9.2 %copy-start.6 = (s32[3]{0:T(128)S(1)}, s32[3]{0:T(128)}, u32[]{:S(2)}) copy-start(s32[3]{0:T(128)} %param.18) | copy-start | bytes 40
  2.7 20.4 %copy-start.2 = (s32[3]{0:T(128)S(1)}, s32[3]{0:T(128)}, u32[]{:S(2)}) copy-start(s32[3]{0:T(128)} %param.17) | copy-start | bytes 40
  2.7 21.0 %copy-start.3 = (pred[768]{0:T(1024)(128)(4,1)S(1)}, pred[768]{0:T(1024)(128)(4,1)}, u32[]{:S(2)}) copy-start(pred[768]{0:T(1024)(128)(4,1)} %constant.142) | copy-start | bytes 2308
  2.7 21.0 %copy-start.4 = (pred[768]{0:T(1024)(128)(4,1)S(1)}, pred[768]{0:T(1024)(128)(4,1)}, u32[]{:S(2)}) copy-start(pred[768]{0:T(1024)(128)(4,1)} %constant.143) | copy-start | bytes 2308
  4.6 28.7 %copy-start.1 = (f32[64,64]{1,0:T(8,128)S(1)}, f32[64,64]{1,0:T(8,128)}, u32[]{:S(2)}) copy-start(f32[64,64]{1,0:T(8,128)} %param.16) | copy-start | bytes 49156
  5.4 13.2 %all-to-all-start = ((f32[8,16,768]{2,1,0:T(8,128)}), f32[8,16,768]{2,1,0:T(8,128)S(1)}, u32[]{:S(2)}, u32[]{:S(2)}) async-start(f32[8,16,768]{2,1,0:T(8,128)} %bitcast.2), calls=%async_computation | async-start | bytes 786432 | tf_op jit(solution)/shard_map/all_to_all | solution.py:18
  19.4 12.3 %all-to-all-start.1 = ((f32[8,16,768]{2,1,0:T(8,128)}), f32[8,16,768]{2,1,0:T(8,128)S(1)}, u32[]{:S(2)}, u32[]{:S(2)}) async-start(f32[8,16,768]{2,1,0:T(8,128)} %broadcast_in_dim.4), calls=%async_computation.1 | async-start | bytes 786432 | tf_op jit(solution)/shard_map/all_to_all | solution.py:20
  35.0 31.4 %all-to-all-start.2 = ((f32[64,1,1152]{2,1,0:T(1,128)}), f32[64,1,1152]{2,1,0:T(1,128)S(1)}, u32[]{:S(2)}, u32[]{:S(2)}) async-start(f32[64,1,1152]{2,1,0:T(1,128)} %all_to_all.14), calls=%async_computation.2 | async-start | bytes 589824 | tf_op jit(solution)/shard_map/all_to_all | solution.py:81

commit v3 on v0

--- a/solution.py
+++ b/solution.py
@@ -11,6 +11,16 @@
     )
 
 
+def tensor_sum(parts, tensor_size):
+    tokens, feat = parts.shape
+    block = tokens // tensor_size
+    chunks = parts.reshape(tensor_size, block, feat)
+    mine = jnp.sum(lax.all_to_all(chunks, "tensor", 0, 0, tiled=True), axis=0)
+    spread = jnp.broadcast_to(mine[None], (tensor_size, block, feat))
+    whole = lax.all_to_all(spread, "tensor", 0, 0, tiled=True)
+    return whole.reshape(tokens, feat)
+
+
 def per_device(hidden, out_grad, proj_in, proj_out, left_inv, right_inv, lengths, language, owner):
     highest = lax.Precision.HIGHEST
     seq_count = hidden.shape[0]
@@ -19,19 +29,20 @@
     tensor_size = lax.axis_size("tensor")
     row_width = proj_rank // tensor_size
     row_start = lax.axis_index("tensor") * row_width
-    left_part = project(hidden, proj_in)
-    right_part = project(out_grad, proj_out)
     token_mask = (jnp.arange(seq_length, dtype=jnp.int32)[None, :] < lengths[:, None]).astype(
         jnp.float32
     )
-    left_full, right_full = lax.psum((left_part, right_part), "tensor")
-    left_full = left_full.reshape(seq_count, seq_length, proj_rank)
-    right_full = right_full.reshape(seq_count, seq_length, proj_rank) * token_mask[:, :, None]
+    left_part = project(hidden, proj_in)
+    right_part = project(out_grad, proj_out) * token_mask.reshape(-1)[:, None]
+    both = tensor_sum(jnp.concatenate([left_part, right_part], axis=1), tensor_size)
+    both = both.reshape(seq_count, seq_length, 2 * proj_rank)
+    left_full = both[:, :, :proj_rank]
+    right_full = both[:, :, proj_rank:]
     full_grads = jnp.einsum("sti,stj->sij", left_full, right_full, precision=highest)
-    left_done = jnp.einsum("ik,skj->sij", left_inv, full_grads, precision=highest)
-    full_pre = jnp.einsum("sik,kj->sij", left_done, right_inv, precision=highest)
+    inv_rows = lax.dynamic_slice_in_dim(left_inv, row_start, row_width, 0)
     grad_rows = lax.dynamic_slice_in_dim(full_grads, row_start, row_width, 1)
-    pre_rows = lax.dynamic_slice_in_dim(full_pre, row_start, row_width, 1)
+    left_done = jnp.einsum("ik,skj->sij", inv_rows, full_grads, precision=highest)
+    pre_rows = jnp.einsum("sik,kj->sij", left_done, right_inv, precision=highest)
     grad_flat = grad_rows.reshape(seq_count, row_width * proj_rank)
     pre_flat = pre_rows.reshape(seq_count, row_width * proj_rank)
     lang_total = owner.shape[0]
@@ -49,10 +60,21 @@
     )
     slot_table = jnp.dot(place_hot.T, pre_flat, precision=highest)
     slot_counts = jnp.sum(place_hot, axis=0)
-    summed, counted = (
-        lax.psum_scatter(slot_table, "dp", scatter_dimension=0, tiled=True),
-        lax.psum_scatter(slot_counts, "dp", scatter_dimension=0, tiled=True),
+    width = slot_table.shape[1]
+    count_pad = 128
+    payload = jnp.concatenate(
+        [
+            slot_table.reshape(dp_size, 1, slot_count * width),
+            jnp.pad(
+                slot_counts.reshape(dp_size, 1, slot_count),
+                ((0, 0), (0, 0), (0, count_pad - slot_count)),
+            ),
+        ],
+        axis=2,
     )
+    gathered = jnp.sum(lax.all_to_all(payload, "dp", 0, 0, tiled=True), axis=(0, 1))
+    summed = gathered[: slot_count * width].reshape(slot_count, width)
+    counted = gathered[slot_count * width : slot_count * width + slot_count]
     owned_means = summed / jnp.maximum(counted, 1.0)[:, None]
     return (grad_flat, owned_means)
 

time: 253 us -> 68.4 us (0.27)
  the two profiles are of different devices: /device:TPU:6 before, /device:TPU:8 now
where the time goes in v3:
time: 68.4 us; the launch traced here: 68.1 us
  waiting for transfers between devices  31.3 us (46%)
  starting transfers between devices  24.3 us (36%)
  matrix products  4.61 us (7%)
  local copies, waits for them, and re-layouts  3.83 us (6%)
  other arithmetic  3.21 us (5%)
  between operations  0.82 us (1%)
    all_to_all x1, starting transfers between devices, per_device(): lax.all_to_all(payload, 'dp', 0, 0, tiled=True)  16.6 us
    all_to_all x1, waiting for transfers between devices, per_device(): lax.all_to_all(payload, 'dp', 0, 0, tiled=True)  14.1 us
    all_to_all x1, waiting for transfers between devices, tensor_sum(): mine = jnp.sum(lax.all_to_all(chunks, 'tensor', 0, 0, tiled=True), axis=0)  8.76 us
    all_to_all x1, waiting for transfers between devices, tensor_sum(): whole = lax.all_to_all(spread, 'tensor', 0, 0, tiled=True)  8.41 us
    all_to_all x1, starting transfers between devices, tensor_sum(): mine = jnp.sum(lax.all_to_all(chunks, 'tensor', 0, 0, tiled=True), axis=0)  4.3 us
    all_to_all x1, starting transfers between devices, tensor_sum(): whole = lax.all_to_all(spread, 'tensor', 0, 0, tiled=True)  3.45 us
    dot_general x2, matrix products, project(): lax.dot_general(flattened, projection, (((1,), (1,)), ((), ())), preferre...  2.29 us
  transfers between devices with their start and end apart: 3, of which 3 were waited for; matrix products, arithmetic and copies ran while one was open for 2% of the time, Pallas kernels for 0%

profile of v3, /device:TPU:8, one launch (start us, length us, event | category | flops | bytes accessed | tf_op | source)
XLA Modules:
  0.0 68.1 jit_solution(12514140104102803686)
XLA Ops:
  0.6 0.0 copy-start
  0.6 0.0 copy-start.1
  0.7 0.9 %fusion.8 = f32[3,256]{1,0:T(4,128)S(1)} fusion(s32[3]{0:T(128)} %param.15), kind=kLoop, calls=%fused_computation.15 | loop fusion | flops 1536 | bytes 3084 | tf_op jit(solution)/shard_map/convert_element_type | solution.py:32
  1.5 0.9 %copy-done = bf16[3,256,1792]{2,1,0:T(8,128)(2,1)S(1)} copy-done((bf16[3,256,1792]{2,1,0:T(8,128)(2,1)S(1)}, bf16[3,256,1792]{2,1,0:T(8,128)(2,1)}, u32[]{:S(2)}) %copy-start) | copy-done | bytes 2752536
  2.4 0.0 copy-start.2
  2.4 1.9 %fusion.12 = f32[768,64]{0,1:T(8,128)S(1)} fusion(bf16[768,1792]{1,0:T(8,128)(2,1)S(1)} %bitcast.20, bf16[64,1792]{1,0:T(8,128)(2,1)} %param.11), kind=kOutput, calls=%fused_computation.27 | convolution fusion | flops 176160768 | bytes 3178496 | tf_op jit(solution)/shard_map/dot_general | solution.py:9
  4.4 0.0 copy-start.4
  4.4 0.0 copy-start.5
  4.4 0.0 copy-done.1
  4.4 0.0 copy-done.2
  4.4 0.4 convolution_multiply_fusion
  4.8 0.0 copy-start.3
  4.8 0.9 %copy.19 = f32[768,128]{1,0:T(8,128)} copy(f32[768,128]{0,1:T(8,128)S(1)} %pad_maximum_fusion) | data formatting | bytes 786432 | tf_op jit(solution)/shard_map/concatenate | solution.py:37
  5.7 4.3 %all-to-all-start = ((f32[8,96,128]{2,1,0:T(8,128)}), f32[8,96,128]{2,1,0:T(8,128)S(1)}, u32[]{:S(2)}, u32[]{:S(2)}) async-start(f32[8,96,128]{2,1,0:T(8,128)} %bitcast.2), calls=%async_computation | async-start | bytes 786432 | tf_op jit(solution)/shard_map/all_to_all | solution.py:18
  10.0 0.0 copy-done.4
  10.0 0.2 convert_reduce_fusion
  10.2 8.8 %all-to-all-done = f32[8,96,128]{2,1,0:T(8,128)S(1)} async-done(((f32[8,96,128]{2,1,0:T(8,128)}), f32[8,96,128]{2,1,0:T(8,128)S(1)}, u32[]{:S(2)}, u32[]{:S(2)}) %all-to-all-start) | async-done | bytes 393248 | tf_op jit(solution)/shard_map/all_to_all | solution.py:18
  19.0 0.8 %broadcast_in_dim.2 = f32[8,96,128]{2,1,0:T(8,128)} broadcast(f32[96,128]{1,0:T(8,128)S(1)} %reduce_sum.45), dimensions={1,2} | broadcast | bytes 442368 | tf_op jit(solution)/shard_map/broadcast_in_dim | solution.py:19
  19.8 3.5 %all-to-all-start.1 = ((f32[8,96,128]{2,1,0:T(8,128)}), f32[8,96,128]{2,1,0:T(8,128)S(1)}, u32[]{:S(2)}, u32[]{:S(2)}) async-start(f32[8,96,128]{2,1,0:T(8,128)} %broadcast_in_dim.2), calls=%async_computation.1 | async-start | bytes 786432 | tf_op jit(solution)/shard_map/all_to_all | solution.py:20
  23.2 0.0 copy-done.5
  23.2 0.2 select_reduce_fusion
  23.4 0.1 convert_reduce_fusion.1
  23.5 0.1 reshape.59
  23.7 8.4 %all-to-all-done.1 = f32[8,96,128]{2,1,0:T(8,128)S(1)} async-done(((f32[8,96,128]{2,1,0:T(8,128)}), f32[8,96,128]{2,1,0:T(8,128)S(1)}, u32[]{:S(2)}, u32[]{:S(2)}) %all-to-all-start.1) | async-done | bytes 393248 | tf_op jit(solution)/shard_map/all_to_all | solution.py:20
  32.1 0.9 %fusion = f32[3,64,64]{2,1,0:T(8,128)S(1)} fusion(f32[3,256,128]{2,1,0:T(8,128)S(1)} %bitcast.21), kind=kOutput, calls=%fused_computation.2 | convolution fusion | flops 37748736 | bytes 835584 | tf_op jit(solution)/shard_map/sti,stj->sij/dot_general | solution.py:41
  33.0 0.9 %convolution_bitcast_fusion = f32[3,8,64]{2,1,0:T(8,128)S(1)} fusion(f32[3,64,64]{2,1,0:T(8,128)S(1)} %fusion, f32[64,64]{1,0:T(8,128)} %param.13, s32[]{:T(128)S(6)} %select_n.4), kind=kOutput, calls=%fused_computation.1 | convolution fusion | flops 1179648 | bytes 59396 | tf_op jit(solution)/shard_map/ik,skj->sij/dot_general | solution.py:44
  33.9 0.0 copy-done.3
  33.9 0.1 fusion.4
  34.0 0.1 reshape.57
  34.1 0.4 fusion.9
  34.5 0.3 reshape.64
  34.8 1.0 %pad_maximum_fusion.1 = f32[64,1,1152]{2,1,0:T(1,128)} fusion(f32[64,1,128]{2,1,0:T(1,128)S(1)} %bitcast.23, f32[64,1,1024]{2,1,0:T(1,128)S(1)} %reshape.64), kind=kLoop, calls=%fused_computation.6 | loop fusion | flops 73728 | bytes 589824 | tf_op jit(solution)/shard_map/concatenate | solution.py:65
  35.8 16.6 %all-to-all-start.2 = ((f32[64,1,1152]{2,1,0:T(1,128)}), f32[64,1,1152]{2,1,0:T(1,128)S(1)}, u32[]{:S(2)}, u32[]{:S(2)}) async-start(f32[64,1,1152]{2,1,0:T(1,128)} %pad_maximum_fusion.1), calls=%async_computation.2 | async-start | bytes 589824 | tf_op jit(solution)/shard_map/all_to_all | solution.py:75
  52.4 0.7 reshape.56
  53.1 14.1 %all-to-all-done.2 = f32[64,1,1152]{2,1,0:T(1,128)S(1)} async-done(((f32[64,1,1152]{2,1,0:T(1,128)}), f32[64,1,1152]{2,1,0:T(1,128)S(1)}, u32[]{:S(2)}, u32[]{:S(2)}) %all-to-all-start.2) | async-done | bytes 294944 | tf_op jit(solution)/shard_map/all_to_all | solution.py:75
  67.2 0.2 reduce_sum.49
  67.4 0.7 broadcast_divide_fusion
  (9 shorter events, 0.1 us)
Async XLA Ops:
  0.6 1.8 %copy-start = (bf16[3,256,1792]{2,1,0:T(8,128)(2,1)S(1)}, bf16[3,256,1792]{2,1,0:T(8,128)(2,1)}, u32[]{:S(2)}) copy-start(bf16[3,256,1792]{2,1,0:T(8,128)(2,1)} %param.9) | copy-start | bytes 8257540
  0.6 3.7 %copy-start.1 = (bf16[3,256,512]{2,1,0:T(8,128)(2,1)S(1)}, bf16[3,256,512]{2,1,0:T(8,128)(2,1)}, u32[]{:S(2)}) copy-start(bf16[3,256,512]{2,1,0:T(8,128)(2,1)} %param.10) | copy-start | bytes 2359300
  2.4 2.0 %copy-start.2 = (bf16[64,512]{1,0:T(8,128)(2,1)S(1)}, bf16[64,512]{1,0:T(8,128)(2,1)}, u32[]{:S(2)}) copy-start(bf16[64,512]{1,0:T(8,128)(2,1)} %param.12) | copy-start | bytes 196612
  4.4 5.7 %copy-start.4 = (s32[100]{0:T(128)S(1)}, s32[100]{0:T(128)}, u32[]{:S(2)}) copy-start(s32[100]{0:T(128)} %param.17) | copy-start | bytes 1204
  4.4 18.9 %copy-start.5 = (s32[3]{0:T(128)S(1)}, s32[3]{0:T(128)}, u32[]{:S(2)}) copy-start(s32[3]{0:T(128)} %param.16) | copy-start | bytes 40
  4.8 29.1 %copy-start.3 = (f32[64,64]{1,0:T(8,128)S(1)}, f32[64,64]{1,0:T(8,128)}, u32[]{:S(2)}) copy-start(f32[64,64]{1,0:T(8,128)} %param.14) | copy-start | bytes 49156
  5.7 13.2 %all-to-all-start = ((f32[8,96,128]{2,1,0:T(8,128)}), f32[8,96,128]{2,1,0:T(8,128)S(1)}, u32[]{:S(2)}, u32[]{:S(2)}) async-start(f32[8,96,128]{2,1,0:T(8,128)} %bitcast.2), calls=%async_computation | async-start | bytes 786432 | tf_op jit(solution)/shard_map/all_to_all | solution.py:18
  19.8 12.3 %all-to-all-start.1 = ((f32[8,96,128]{2,1,0:T(8,128)}), f32[8,96,128]{2,1,0:T(8,128)S(1)}, u32[]{:S(2)}, u32[]{:S(2)}) async-start(f32[8,96,128]{2,1,0:T(8,128)} %broadcast_in_dim.2), calls=%async_computation.1 | async-start | bytes 786432 | tf_op jit(solution)/shard_map/all_to_all | solution.py:20
  35.8 31.4 %all-to-all-start.2 = ((f32[64,1,1152]{2,1,0:T(1,128)}), f32[64,1,1152]{2,1,0:T(1,128)S(1)}, u32[]{:S(2)}, u32[]{:S(2)}) async-start(f32[64,1,1152]{2,1,0:T(1,128)} %pad_maximum_fusion.1), calls=%async_computation.2 | async-start | bytes 589824 | tf_op jit(solution)/shard_map/all_to_all | solution.py:75

commit v4 on v3

--- a/solution.py
+++ b/solution.py
@@ -11,16 +11,6 @@
     )
 
 
-def tensor_sum(parts, tensor_size):
-    tokens, feat = parts.shape
-    block = tokens // tensor_size
-    chunks = parts.reshape(tensor_size, block, feat)
-    mine = jnp.sum(lax.all_to_all(chunks, "tensor", 0, 0, tiled=True), axis=0)
-    spread = jnp.broadcast_to(mine[None], (tensor_size, block, feat))
-    whole = lax.all_to_all(spread, "tensor", 0, 0, tiled=True)
-    return whole.reshape(tokens, feat)
-
-
 def per_device(hidden, out_grad, proj_in, proj_out, left_inv, right_inv, lengths, language, owner):
     highest = lax.Precision.HIGHEST
     seq_count = hidden.shape[0]
@@ -28,23 +18,28 @@
     proj_rank = proj_in.shape[0]
     tensor_size = lax.axis_size("tensor")
     row_width = proj_rank // tensor_size
-    row_start = lax.axis_index("tensor") * row_width
-    token_mask = (jnp.arange(seq_length, dtype=jnp.int32)[None, :] < lengths[:, None]).astype(
-        jnp.float32
-    )
     left_part = project(hidden, proj_in)
-    right_part = project(out_grad, proj_out) * token_mask.reshape(-1)[:, None]
-    both = tensor_sum(jnp.concatenate([left_part, right_part], axis=1), tensor_size)
-    both = both.reshape(seq_count, seq_length, 2 * proj_rank)
-    left_full = both[:, :, :proj_rank]
-    right_full = both[:, :, proj_rank:]
-    full_grads = jnp.einsum("sti,stj->sij", left_full, right_full, precision=highest)
-    inv_rows = lax.dynamic_slice_in_dim(left_inv, row_start, row_width, 0)
-    grad_rows = lax.dynamic_slice_in_dim(full_grads, row_start, row_width, 1)
-    left_done = jnp.einsum("ik,skj->sij", inv_rows, full_grads, precision=highest)
-    pre_rows = jnp.einsum("sik,kj->sij", left_done, right_inv, precision=highest)
-    grad_flat = grad_rows.reshape(seq_count, row_width * proj_rank)
-    pre_flat = pre_rows.reshape(seq_count, row_width * proj_rank)
+    right_part = project(out_grad, proj_out)
+    parts = jnp.concatenate([left_part, right_part], axis=1)
+    tokens = seq_count * seq_length
+    block = tokens // tensor_size
+    chunks = parts.reshape(tensor_size, block, 2 * proj_rank)
+    mine = jnp.sum(lax.all_to_all(chunks, "tensor", 0, 0, tiled=True), axis=0)
+    token_at = lax.axis_index("tensor") * block + jnp.arange(block, dtype=jnp.int32)
+    token_seq = token_at // seq_length
+    token_pos = token_at % seq_length
+    seq_index = jnp.arange(seq_count, dtype=jnp.int32)
+    weight = (token_seq[None, :] == seq_index[:, None]) & (token_pos[None, :] < lengths[:, None])
+    right_seq = mine[None, :, proj_rank:] * weight.astype(jnp.float32)[:, :, None]
+    grads_part = jnp.einsum("ti,stj->sij", mine[:, :proj_rank], right_seq, precision=highest)
+    left_done = jnp.einsum("ik,skj->sij", left_inv, grads_part, precision=highest)
+    pre_part = jnp.einsum("sik,kj->sij", left_done, right_inv, precision=highest)
+    stacked = jnp.stack([grads_part, pre_part], axis=1)
+    stacked = stacked.reshape(seq_count, 2, tensor_size, row_width, proj_rank)
+    stacked = stacked.transpose(2, 0, 1, 3, 4)
+    rows = jnp.sum(lax.all_to_all(stacked, "tensor", 0, 0, tiled=True), axis=0)
+    grad_flat = rows[:, 0].reshape(seq_count, row_width * proj_rank)
+    pre_flat = rows[:, 1].reshape(seq_count, row_width * proj_rank)
     lang_total = owner.shape[0]
     dp_size = lax.axis_size("dp")
     slot_count = (lang_total + dp_size - 1) // dp_size

time: 68.4 us -> 65.8 us (0.962)
  waiting for transfers between devices: 31.3 us -> 28.1 us
    all_to_all x2, waiting for transfers between devices: 17.2 us -> 13.9 us  [the longest x1 8.46 us: per_device(): mine = jnp.sum(lax.all_to_all(chunks, 'tensor', 0, 0, tiled=True), axis=0)]
    dot_general x2, matrix products: 2.29 us -> 3.58 us  [project(): lax.dot_general(flattened, projection, (((1,), (1,)), ((), ())), preferre...]
    dot_general x2, matrix products: 1.78 us -> 0.49 us  [the longest x1 0.25 us: per_device(): jnp.einsum('ti,stj->sij', mine[:, :proj_rank], right_seq, precision=highest)]
    all_to_all x0 -> x1, other arithmetic: none -> 0.88 us  [per_device(): rows = jnp.sum(lax.all_to_all(stacked, 'tensor', 0, 0, tiled=True), axis=0)]
    convert_element_type x1, other arithmetic: 0.88 us -> 0.07 us  [per_device(): weight.astype(jnp.float32)[:, :, None]]
    broadcast_in_dim x1 -> x0, local copies, waits for them, and re-layouts: 0.76 us -> none  [tensor_sum(): spread = jnp.broadcast_to(mine[None], (tensor_size, block, feat))]
    reshape x2 -> x0, local copies, waits for them, and re-layouts: 0.76 us -> none  [the longest x1 0.68 us: per_device(): grad_flat = grad_rows.reshape(seq_count, row_width * proj_rank)]
    another operation x0 -> x2, local copies, waits for them, and re-layouts: none -> 0.75 us  [the longest x1 0.68 us: per_device(): grad_flat = rows[:, 0].reshape(seq_count, row_width * proj_rank)]
where the time goes in v4:
time: 65.8 us; the launch traced here: 65.4 us
  waiting for transfers between devices  28.1 us (43%)
  starting transfers between devices  24.2 us (37%)
  matrix products  4.79 us (7%)
  local copies, waits for them, and re-layouts  4.16 us (6%)
  other arithmetic  3.33 us (5%)
  between operations  0.83 us (1%)
    all_to_all x1, starting transfers between devices, per_device(): lax.all_to_all(payload, 'dp', 0, 0, tiled=True)  16.6 us
    all_to_all x1, waiting for transfers between devices, per_device(): lax.all_to_all(payload, 'dp', 0, 0, tiled=True)  14.2 us
    all_to_all x1, waiting for transfers between devices, per_device(): mine = jnp.sum(lax.all_to_all(chunks, 'tensor', 0, 0, tiled=True), axis=0)  8.46 us
    all_to_all x1, waiting for transfers between devices, per_device(): rows = jnp.sum(lax.all_to_all(stacked, 'tensor', 0, 0, tiled=True), axis=0)  5.48 us
    all_to_all x1, starting transfers between devices, per_device(): mine = jnp.sum(lax.all_to_all(chunks, 'tensor', 0, 0, tiled=True), axis=0)  4.3 us
    dot_general x2, matrix products, project(): lax.dot_general(flattened, projection, (((1,), (1,)), ((), ())), preferre...  3.58 us
    all_to_all x1, starting transfers between devices, per_device(): rows = jnp.sum(lax.all_to_all(stacked, 'tensor', 0, 0, tiled=True), axis=0)  3.36 us
  transfers between devices with their start and end apart: 3, of which 3 were waited for; matrix products, arithmetic and copies ran while one was open for 2% of the time, Pallas kernels for 0%

profile of v4, /device:TPU:8, one launch (start us, length us, event | category | flops | bytes accessed | tf_op | source)
XLA Modules:
  0.0 65.4 jit_solution(1930306042742182190)
XLA Ops:
  0.6 0.0 copy-start
  0.6 1.6 %fusion.12 = f32[768,64]{0,1:T(8,128)S(1)} fusion(bf16[768,512]{1,0:T(8,128)(2,1)} %bitcast.44, bf16[64,512]{1,0:T(8,128)(2,1)} %param.12), kind=kOutput, calls=%fused_computation.37 | convolution fusion | flops 50331648 | bytes 1048576 | tf_op jit(solution)/shard_map/dot_general | solution.py:9
  2.3 0.4 copy-done
  2.7 0.0 copy-start.4
  2.7 0.0 copy-start.5
  2.7 0.0 copy-start.3
  2.7 1.9 %fusion.11 = f32[768,64]{0,1:T(8,128)S(1)} fusion(bf16[768,1792]{1,0:T(8,128)(2,1)S(1)} %bitcast.43, bf16[64,1792]{1,0:T(8,128)(2,1)} %param.11), kind=kOutput, calls=%fused_computation.36 | convolution fusion | flops 176160768 | bytes 3178496 | tf_op jit(solution)/shard_map/dot_general | solution.py:9
  4.6 0.0 copy-start.1
  4.6 0.0 copy-start.2
  4.7 0.9 %copy.22 = f32[768,128]{1,0:T(8,128)} copy(f32[768,128]{0,1:T(8,128)S(1)} %pad_maximum_fusion) | data formatting | bytes 786432 | tf_op jit(solution)/shard_map/concatenate | solution.py:23
  5.6 4.3 %all-to-all-start = ((f32[8,96,128]{2,1,0:T(8,128)}), f32[8,96,128]{2,1,0:T(8,128)S(1)}, u32[]{:S(2)}, u32[]{:S(2)}) async-start(f32[8,96,128]{2,1,0:T(8,128)} %bitcast.2), calls=%async_computation | async-start | bytes 786432 | tf_op jit(solution)/shard_map/all_to_all | solution.py:27
  9.9 0.0 copy-done.4
  9.9 0.2 convert_reduce_fusion
  10.1 0.0 copy-done.5
  10.1 0.2 select_reduce_fusion
  10.3 0.0 copy-done.3
  10.3 0.1 fusion.8
  10.4 8.5 %all-to-all-done = f32[8,96,128]{2,1,0:T(8,128)S(1)} async-done(((f32[8,96,128]{2,1,0:T(8,128)}), f32[8,96,128]{2,1,0:T(8,128)S(1)}, u32[]{:S(2)}, u32[]{:S(2)}) %all-to-all-start) | async-done | bytes 393248 | tf_op jit(solution)/shard_map/all_to_all | solution.py:27
  18.9 0.1 slice.24
  18.9 0.1 copy.23
  19.0 0.3 convolution_bitcast_fusion.2
  19.3 0.1 copy.25
  19.4 0.0 copy-done.1
  19.4 0.2 convolution_bitcast_fusion.1
  19.6 0.0 copy-done.2
  19.6 0.3 convolution_bitcast_fusion
  20.0 0.8 %reshape.125 = f32[8,1,3072]{2,1,0:T(1,128)} reshape(f32[8,2,3,8,64]{4,3,2,1,0:T(8,128)S(1)} %copy_bitcast_fusion) | data formatting | bytes 196608
  20.8 3.4 %all-to-all-start.1 = ((f32[8,1,3072]{2,1,0:T(1,128)}), f32[8,1,3072]{2,1,0:T(1,128)S(1)}, u32[]{:S(2)}, u32[]{:S(2)}) async-start(f32[8,1,3072]{2,1,0:T(1,128)} %reshape.125), calls=%async_computation.1 | async-start | bytes 196608 | tf_op jit(solution)/shard_map/all_to_all | solution.py:40
  24.1 0.1 convert_reduce_fusion.1
  24.2 0.1 reshape.119
  24.4 5.5 %all-to-all-done.1 = f32[8,1,3072]{2,1,0:T(1,128)S(1)} async-done(((f32[8,1,3072]{2,1,0:T(1,128)}), f32[8,1,3072]{2,1,0:T(1,128)S(1)}, u32[]{:S(2)}, u32[]{:S(2)}) %all-to-all-start.1) | async-done | bytes 98336 | tf_op jit(solution)/shard_map/all_to_all | solution.py:40
  29.9 0.5 broadcast.123
  30.4 0.9 %reduce = f32[8,3072]{1,0:T(8,128)S(1)} reduce(f32[8,1,3072]{2,1,0:T(1,128)S(1)} %all-to-all-done.1, f32[]{:T(128)} %broadcast.123), dimensions={1}, to_apply=%all_to_all.10.reduce_sub_computation | reduce | bytes 196612 | tf_op jit(solution)/shard_map/all_to_all | solution.py:40
  31.2 0.1 reshape.126
  31.4 0.1 reshape_squeeze.7
  31.5 0.4 fusion.6
  31.9 0.3 reshape.124
  32.2 1.0 %pad_maximum_fusion.1 = f32[64,1,1152]{2,1,0:T(1,128)} fusion(f32[64,1,128]{2,1,0:T(1,128)S(1)} %bitcast.46, f32[64,1,1024]{2,1,0:T(1,128)S(1)} %reshape.124), kind=kLoop, calls=%fused_computation.4 | loop fusion | flops 73728 | bytes 589824 | tf_op jit(solution)/shard_map/concatenate | solution.py:60
  33.1 16.6 %all-to-all-start.2 = ((f32[64,1,1152]{2,1,0:T(1,128)}), f32[64,1,1152]{2,1,0:T(1,128)S(1)}, u32[]{:S(2)}, u32[]{:S(2)}) async-start(f32[64,1,1152]{2,1,0:T(1,128)} %pad_maximum_fusion.1), calls=%async_computation.2 | async-start | bytes 589824 | tf_op jit(solution)/shard_map/all_to_all | solution.py:70
  49.7 0.7 %reshape_squeeze.6 = f32[3,512]{1,0:T(4,128)} reshape(f32[3,1,8,64]{3,2,0,1:T(8,128)S(1)} %get-tuple-element.3) | data formatting | bytes 12288 | tf_op jit(solution)/shard_map/reshape;squeeze | solution.py:41
  50.4 14.2 %all-to-all-done.2 = f32[64,1,1152]{2,1,0:T(1,128)S(1)} async-done(((f32[64,1,1152]{2,1,0:T(1,128)}), f32[64,1,1152]{2,1,0:T(1,128)S(1)}, u32[]{:S(2)}, u32[]{:S(2)}) %all-to-all-start.2) | async-done | bytes 294944 | tf_op jit(solution)/shard_map/all_to_all | solution.py:70
  64.6 0.2 reduce_sum.59
  64.8 0.7 %broadcast_divide_fusion = f32[2,512]{1,0:T(2,128)} fusion(f32[2,512]{1,0:T(2,128)S(1)} %reshape.120, f32[2]{0:T(128)S(1)} %slice_maximum_fusion), kind=kLoop, calls=%fused_computation.15 | loop fusion | flops 1024 | bytes 8200 | tf_op jit(solution)/shard_map/div | solution.py:73
  (11 shorter events, 0.1 us)
Async XLA Ops:
  0.6 2.0 %copy-start = (bf16[3,256,1792]{2,1,0:T(8,128)(2,1)S(1)}, bf16[3,256,1792]{2,1,0:T(8,128)(2,1)}, u32[]{:S(2)}) copy-start(bf16[3,256,1792]{2,1,0:T(8,128)(2,1)} %param.9) | copy-start | bytes 8257540
  2.7 7.2 %copy-start.4 = (s32[100]{0:T(128)S(1)}, s32[100]{0:T(128)}, u32[]{:S(2)}) copy-start(s32[100]{0:T(128)} %param.17) | copy-start | bytes 1204
  2.7 7.4 %copy-start.5 = (s32[3]{0:T(128)S(1)}, s32[3]{0:T(128)}, u32[]{:S(2)}) copy-start(s32[3]{0:T(128)} %param.16) | copy-start | bytes 40
  2.7 7.6 %copy-start.3 = (s32[3]{0:T(128)S(1)}, s32[3]{0:T(128)}, u32[]{:S(2)}) copy-start(s32[3]{0:T(128)} %param.15) | copy-start | bytes 40
  4.6 14.7 %copy-start.1 = (f32[64,64]{1,0:T(8,128)S(1)}, f32[64,64]{1,0:T(8,128)}, u32[]{:S(2)}) copy-start(f32[64,64]{1,0:T(8,128)} %param.13) | copy-start | bytes 49156
  4.6 15.0 %copy-start.2 = (f32[64,64]{1,0:T(8,128)S(1)}, f32[64,64]{1,0:T(8,128)}, u32[]{:S(2)}) copy-start(f32[64,64]{1,0:T(8,128)} %param.14) | copy-start | bytes 49156
  5.6 13.2 %all-to-all-start = ((f32[8,96,128]{2,1,0:T(8,128)}), f32[8,96,128]{2,1,0:T(8,128)S(1)}, u32[]{:S(2)}, u32[]{:S(2)}) async-start(f32[8,96,128]{2,1,0:T(8,128)} %bitcast.2), calls=%async_computation | async-start | bytes 786432 | tf_op jit(solution)/shard_map/all_to_all | solution.py:27
  20.8 9.1 %all-to-all-start.1 = ((f32[8,1,3072]{2,1,0:T(1,128)}), f32[8,1,3072]{2,1,0:T(1,128)S(1)}, u32[]{:S(2)}, u32[]{:S(2)}) async-start(f32[8,1,3072]{2,1,0:T(1,128)} %reshape.125), calls=%async_computation.1 | async-start | bytes 196608 | tf_op jit(solution)/shard_map/all_to_all | solution.py:40
  33.1 31.4 %all-to-all-start.2 = ((f32[64,1,1152]{2,1,0:T(1,128)}), f32[64,1,1152]{2,1,0:T(1,128)S(1)}, u32[]{:S(2)}, u32[]{:S(2)}) async-start(f32[64,1,1152]{2,1,0:T(1,128)} %pad_maximum_fusion.1), calls=%async_computation.2 | async-start | bytes 589824 | tf_op jit(solution)/shard_map/all_to_all | solution.py:70

commit v5 on v4

--- a/solution.py
+++ b/solution.py
@@ -34,12 +34,12 @@
     grads_part = jnp.einsum("ti,stj->sij", mine[:, :proj_rank], right_seq, precision=highest)
     left_done = jnp.einsum("ik,skj->sij", left_inv, grads_part, precision=highest)
     pre_part = jnp.einsum("sik,kj->sij", left_done, right_inv, precision=highest)
-    stacked = jnp.stack([grads_part, pre_part], axis=1)
-    stacked = stacked.reshape(seq_count, 2, tensor_size, row_width, proj_rank)
-    stacked = stacked.transpose(2, 0, 1, 3, 4)
+    stacked = jnp.concatenate([grads_part, pre_part], axis=2)
+    stacked = stacked.reshape(seq_count, tensor_size, row_width, 2 * proj_rank)
+    stacked = stacked.transpose(1, 0, 2, 3)
     rows = jnp.sum(lax.all_to_all(stacked, "tensor", 0, 0, tiled=True), axis=0)
-    grad_flat = rows[:, 0].reshape(seq_count, row_width * proj_rank)
-    pre_flat = rows[:, 1].reshape(seq_count, row_width * proj_rank)
+    grad_flat = rows[:, :, :proj_rank].reshape(seq_count, row_width * proj_rank)
+    pre_flat = rows[:, :, proj_rank:].reshape(seq_count, row_width * proj_rank)
     lang_total = owner.shape[0]
     dp_size = lax.axis_size("dp")
     slot_count = (lang_total + dp_size - 1) // dp_size
@@ -50,20 +50,18 @@
     lang_place = owner * slot_count + lang_slot
     lang_hot = (language[:, None] == lang_index[None, :]).astype(jnp.int32)
     seq_place = jnp.sum(lang_hot * lang_place[None, :], axis=1)
-    place_hot = (seq_place[:, None] == jnp.arange(owned_rows, dtype=jnp.int32)[None, :]).astype(
-        jnp.float32
+    slot_index = jnp.arange(owned_rows, dtype=jnp.int32).reshape(dp_size, 1, slot_count)
+    place_match = seq_place[:, None, None, None] == slot_index[None]
+    slot_sums = jnp.sum(
+        jnp.where(place_match[..., None], pre_flat[:, None, None, None, :], 0.0), axis=0
     )
-    slot_table = jnp.dot(place_hot.T, pre_flat, precision=highest)
-    slot_counts = jnp.sum(place_hot, axis=0)
-    width = slot_table.shape[1]
+    slot_counts = jnp.sum(place_match.astype(jnp.float32), axis=0)
+    width = pre_flat.shape[1]
     count_pad = 128
     payload = jnp.concatenate(
         [
-            slot_table.reshape(dp_size, 1, slot_count * width),
-            jnp.pad(
-                slot_counts.reshape(dp_size, 1, slot_count),
-                ((0, 0), (0, 0), (0, count_pad - slot_count)),
-            ),
+            slot_sums.reshape(dp_size, 1, slot_count * width),
+            jnp.pad(slot_counts, ((0, 0), (0, 0), (0, count_pad - slot_count))),
         ],
         axis=2,
     )

time: 65.8 us -> 64.4 us (0.979)
  other arithmetic: 3.33 us -> 2.41 us
    concatenate x0 -> x1, local copies, waits for them, and re-layouts: none -> 1.01 us  [per_device(): jnp.concatenate([slot_sums.reshape(dp_size, 1, slot_count * width), jnp.p...]
    concatenate x1, other arithmetic: 0.97 us -> 0.02 us  [per_device(): jnp.concatenate([slot_sums.reshape(dp_size, 1, slot_count * width), jnp.p...]
    all_to_all x1 -> x0, other arithmetic: 0.88 us -> none  [per_device(): rows = jnp.sum(lax.all_to_all(stacked, 'tensor', 0, 0, tiled=True), axis=0)]
    unnamed x14 -> x12, local copies, waits for them, and re-layouts: 1.29 us -> 0.42 us
    another operation x2 -> x0, local copies, waits for them, and re-layouts: 0.75 us -> none  [the longest x1 0.68 us: per_device(): grad_flat = rows[:, 0].reshape(seq_count, row_width * proj_rank)]
    transpose x0 -> x1, other arithmetic: none -> 0.72 us  [per_device(): stacked = stacked.transpose(1, 0, 2, 3)]
where the time goes in v5:
time: 64.4 us; the launch traced here: 64 us
  waiting for transfers between devices  28.1 us (44%)
  starting transfers between devices  24.2 us (38%)
  matrix products  4.64 us (7%)
  local copies, waits for them, and re-layouts  3.85 us (6%)
  other arithmetic  2.41 us (4%)
  between operations  0.82 us (1%)
    all_to_all x1, starting transfers between devices, per_device(): lax.all_to_all(payload, 'dp', 0, 0, tiled=True)  16.6 us
    all_to_all x1, waiting for transfers between devices, per_device(): lax.all_to_all(payload, 'dp', 0, 0, tiled=True)  14.1 us
    all_to_all x1, waiting for transfers between devices, per_device(): mine = jnp.sum(lax.all_to_all(chunks, 'tensor', 0, 0, tiled=True), axis=0)  8.37 us
    all_to_all x1, waiting for transfers between devices, per_device(): rows = jnp.sum(lax.all_to_all(stacked, 'tensor', 0, 0, tiled=True), axis=0)  5.53 us
    all_to_all x1, starting transfers between devices, per_device(): mine = jnp.sum(lax.all_to_all(chunks, 'tensor', 0, 0, tiled=True), axis=0)  4.3 us
    dot_general x2, matrix products, project(): lax.dot_general(flattened, projection, (((1,), (1,)), ((), ())), preferre...  3.58 us
    all_to_all x1, starting transfers between devices, per_device(): rows = jnp.sum(lax.all_to_all(stacked, 'tensor', 0, 0, tiled=True), axis=0)  3.36 us
  transfers between devices with their start and end apart: 3, of which 3 were waited for; matrix products, arithmetic and copies ran while one was open for 2% of the time, Pallas kernels for 0%

profile of v5, /device:TPU:8, one launch (start us, length us, event | category | flops | bytes accessed | tf_op | source)
XLA Modules:
  0.0 64.0 jit_solution(14824757786903116221)
XLA Ops:
  0.6 0.0 copy-start
  0.6 1.6 %fusion.12 = f32[768,64]{0,1:T(8,128)S(1)} fusion(bf16[768,512]{1,0:T(8,128)(2,1)} %bitcast.30, bf16[64,512]{1,0:T(8,128)(2,1)} %param.12), kind=kOutput, calls=%fused_computation.38 | convolution fusion | flops 50331648 | bytes 1048576 | tf_op jit(solution)/shard_map/dot_general | solution.py:9
  2.3 0.4 copy-done
  2.7 0.0 copy-start.4
  2.7 0.0 copy-start.5
  2.7 0.0 copy-start.3
  2.7 1.9 %fusion.11 = f32[768,64]{0,1:T(8,128)S(1)} fusion(bf16[768,1792]{1,0:T(8,128)(2,1)S(1)} %bitcast.29, bf16[64,1792]{1,0:T(8,128)(2,1)} %param.11), kind=kOutput, calls=%fused_computation.37 | convolution fusion | flops 176160768 | bytes 3178496 | tf_op jit(solution)/shard_map/dot_general | solution.py:9
  4.6 0.0 copy-start.1
  4.6 0.0 copy-start.2
  4.7 0.9 %copy.28 = f32[768,128]{1,0:T(8,128)} copy(f32[768,128]{0,1:T(8,128)S(1)} %pad_maximum_fusion) | data formatting | bytes 786432 | tf_op jit(solution)/shard_map/concatenate | solution.py:23
  5.6 4.3 %all-to-all-start = ((f32[8,96,128]{2,1,0:T(8,128)}), f32[8,96,128]{2,1,0:T(8,128)S(1)}, u32[]{:S(2)}, u32[]{:S(2)}) async-start(f32[8,96,128]{2,1,0:T(8,128)} %bitcast.2), calls=%async_computation | async-start | bytes 786432 | tf_op jit(solution)/shard_map/all_to_all | solution.py:27
  9.9 0.0 copy-done.4
  9.9 0.2 convert_reduce_fusion
  10.1 0.0 copy-done.5
  10.1 0.2 select_reduce_fusion.1
  10.3 0.1 broadcast_compare_fusion
  10.4 0.0 copy-done.3
  10.4 0.1 fusion.9
  10.5 8.4 %all-to-all-done = f32[8,96,128]{2,1,0:T(8,128)S(1)} async-done(((f32[8,96,128]{2,1,0:T(8,128)}), f32[8,96,128]{2,1,0:T(8,128)S(1)}, u32[]{:S(2)}, u32[]{:S(2)}) %all-to-all-start) | async-done | bytes 393248 | tf_op jit(solution)/shard_map/all_to_all | solution.py:27
  18.9 0.1 slice.24
  18.9 0.1 copy.29
  19.0 0.4 convolution_bitcast_fusion.1
  19.4 0.0 copy-done.1
  19.4 0.3 convolution_bitcast_fusion
  19.7 0.0 copy-done.2
  19.8 0.3 fusion.4
  20.1 0.7 %copy_bitcast_fusion = f32[8,3,8,128]{3,2,1,0:T(8,128)} fusion(f32[3,64,64]{2,1,0:T(8,128)S(1)} %fusion.4, f32[3,64,64]{2,1,0:T(8,128)S(1)} %convolution_bitcast_fusion.1), kind=kLoop, calls=%fused_computation.7 | loop fusion | flops 24576 | bytes 196608 | tf_op jit(solution)/shard_map/transpose | solution.py:39
  20.8 3.4 %all-to-all-start.1 = ((f32[8,3,8,128]{3,2,1,0:T(8,128)}), f32[8,3,8,128]{3,2,1,0:T(8,128)S(1)}, u32[]{:S(2)}, u32[]{:S(2)}) async-start(f32[8,3,8,128]{3,2,1,0:T(8,128)} %copy_bitcast_fusion), calls=%async_computation.1 | async-start | bytes 196608 | tf_op jit(solution)/shard_map/all_to_all | solution.py:40
  24.2 0.1 fusion.7
  24.3 0.1 copy.35
  24.4 5.5 %all-to-all-done.1 = f32[8,3,8,128]{3,2,1,0:T(8,128)S(1)} async-done(((f32[8,3,8,128]{3,2,1,0:T(8,128)}), f32[8,3,8,128]{3,2,1,0:T(8,128)S(1)}, u32[]{:S(2)}, u32[]{:S(2)}) %all-to-all-start.1) | async-done | bytes 98336 | tf_op jit(solution)/shard_map/all_to_all | solution.py:40
  29.9 0.1 fusion.10
  30.0 0.1 broadcast_in_dim.16
  30.1 0.1 select_reduce_fusion
  30.2 0.2 copy.34
  30.4 0.2 reshape.156
  30.7 1.0 %copy.36 = f32[64,1,1152]{2,1,0:T(1,128)} copy(f32[64,1,1152]{2,0,1:T(8,128)S(1)} %select_maximum_fusion) | data formatting | bytes 589824 | tf_op jit(solution)/shard_map/concatenate | solution.py:61
  31.7 16.6 %all-to-all-start.2 = ((f32[64,1,1152]{2,1,0:T(1,128)}), f32[64,1,1152]{2,1,0:T(1,128)S(1)}, u32[]{:S(2)}, u32[]{:S(2)}) async-start(f32[64,1,1152]{2,1,0:T(1,128)} %copy.36), calls=%async_computation.2 | async-start | bytes 589824 | tf_op jit(solution)/shard_map/all_to_all | solution.py:68
  48.3 0.7 %reshape.155 = f32[3,512]{1,0:T(4,128)} reshape(f32[3,8,64]{2,1,0:T(8,128)S(1)} %get-tuple-element.3) | data formatting | bytes 12288 | tf_op jit(solution)/shard_map/reshape | solution.py:41
  49.0 14.1 %all-to-all-done.2 = f32[64,1,1152]{2,1,0:T(1,128)S(1)} async-done(((f32[64,1,1152]{2,1,0:T(1,128)}), f32[64,1,1152]{2,1,0:T(1,128)S(1)}, u32[]{:S(2)}, u32[]{:S(2)}) %all-to-all-start.2) | async-done | bytes 294944 | tf_op jit(solution)/shard_map/all_to_all | solution.py:68
  63.1 0.2 reduce_sum.72
  63.3 0.7 %broadcast_divide_fusion = f32[2,512]{1,0:T(2,128)} fusion(f32[2,512]{1,0:T(2,128)S(1)} %reshape.157, f32[2]{0:T(128)S(1)} %slice_maximum_fusion), kind=kLoop, calls=%fused_computation.20 | loop fusion | flops 1024 | bytes 8200 | tf_op jit(solution)/shard_map/div | solution.py:71
  (10 shorter events, 0.1 us)
Async XLA Ops:
  0.6 2.0 %copy-start = (bf16[3,256,1792]{2,1,0:T(8,128)(2,1)S(1)}, bf16[3,256,1792]{2,1,0:T(8,128)(2,1)}, u32[]{:S(2)}) copy-start(bf16[3,256,1792]{2,1,0:T(8,128)(2,1)} %param.9) | copy-start | bytes 8257540
  2.7 7.2 %copy-start.4 = (s32[100]{0:T(128)S(1)}, s32[100]{0:T(128)}, u32[]{:S(2)}) copy-start(s32[100]{0:T(128)} %param.17) | copy-start | bytes 1204
  2.7 7.4 %copy-start.5 = (s32[3]{0:T(128)S(1)}, s32[3]{0:T(128)}, u32[]{:S(2)}) copy-start(s32[3]{0:T(128)} %param.16) | copy-start | bytes 40
  2.7 7.7 %copy-start.3 = (s32[3]{0:T(128)S(1)}, s32[3]{0:T(128)}, u32[]{:S(2)}) copy-start(s32[3]{0:T(128)} %param.15) | copy-start | bytes 40
  4.6 14.8 %copy-start.1 = (f32[64,64]{1,0:T(8,128)S(1)}, f32[64,64]{1,0:T(8,128)}, u32[]{:S(2)}) copy-start(f32[64,64]{1,0:T(8,128)} %param.13) | copy-start | bytes 49156
  4.6 15.1 %copy-start.2 = (f32[64,64]{1,0:T(8,128)S(1)}, f32[64,64]{1,0:T(8,128)}, u32[]{:S(2)}) copy-start(f32[64,64]{1,0:T(8,128)} %param.14) | copy-start | bytes 49156
  5.6 13.2 %all-to-all-start = ((f32[8,96,128]{2,1,0:T(8,128)}), f32[8,96,128]{2,1,0:T(8,128)S(1)}, u32[]{:S(2)}, u32[]{:S(2)}) async-start(f32[8,96,128]{2,1,0:T(8,128)} %bitcast.2), calls=%async_computation | async-start | bytes 786432 | tf_op jit(solution)/shard_map/all_to_all | solution.py:27
  20.8 9.1 %all-to-all-start.1 = ((f32[8,3,8,128]{3,2,1,0:T(8,128)}), f32[8,3,8,128]{3,2,1,0:T(8,128)S(1)}, u32[]{:S(2)}, u32[]{:S(2)}) async-start(f32[8,3,8,128]{3,2,1,0:T(8,128)} %copy_bitcast_fusion), calls=%async_computation.1 | async-start | bytes 196608 | tf_op jit(solution)/shard_map/all_to_all | solution.py:40
  31.7 31.4 %all-to-all-start.2 = ((f32[64,1,1152]{2,1,0:T(1,128)}), f32[64,1,1152]{2,1,0:T(1,128)S(1)}, u32[]{:S(2)}, u32[]{:S(2)}) async-start(f32[64,1,1152]{2,1,0:T(1,128)} %copy.36), calls=%async_computation.2 | async-start | bytes 589824 | tf_op jit(solution)/shard_map/all_to_all | solution.py:68

commit v6 on v5

--- a/solution.py
+++ b/solution.py
@@ -1,14 +1,38 @@
 import jax
 import jax.numpy as jnp
 from jax import lax
+from jax.experimental import pallas as pl
 from jax.sharding import PartitionSpec as P
 
 
-def project(values, projection):
-    flattened = values.reshape(-1, values.shape[-1])
-    return lax.dot_general(
-        flattened, projection, (((1,), (1,)), ((), ())), preferred_element_type=jnp.float32
+def _project_kernel(hidden_ref, grad_ref, proj_in_ref, proj_out_ref, out_ref):
+    contract = (((1,), (1,)), ((), ()))
+    rank = proj_in_ref.shape[0]
+    out_ref[:, :rank] = lax.dot_general(
+        hidden_ref[...], proj_in_ref[...], contract, preferred_element_type=jnp.float32
     )
+    out_ref[:, rank:] = lax.dot_general(
+        grad_ref[...], proj_out_ref[...], contract, preferred_element_type=jnp.float32
+    )
+
+
+def project_both(hidden, out_grad, proj_in, proj_out, tile):
+    hidden = hidden.reshape(-1, hidden.shape[-1])
+    out_grad = out_grad.reshape(-1, out_grad.shape[-1])
+    tokens = hidden.shape[0]
+    rank = proj_in.shape[0]
+    return pl.pallas_call(
+        _project_kernel,
+        grid=(tokens // tile,),
+        in_specs=[
+            pl.BlockSpec((tile, hidden.shape[1]), lambda i: (i, 0)),
+            pl.BlockSpec((tile, out_grad.shape[1]), lambda i: (i, 0)),
+            pl.BlockSpec(proj_in.shape, lambda i: (0, 0)),
+            pl.BlockSpec(proj_out.shape, lambda i: (0, 0)),
+        ],
+        out_specs=pl.BlockSpec((tile, 2 * rank), lambda i: (i, 0)),
+        out_shape=jax.ShapeDtypeStruct((tokens, 2 * rank), jnp.float32),
+    )(hidden, out_grad, proj_in, proj_out)
 
 
 def per_device(hidden, out_grad, proj_in, proj_out, left_inv, right_inv, lengths, language, owner):
@@ -18,9 +42,7 @@
     proj_rank = proj_in.shape[0]
     tensor_size = lax.axis_size("tensor")
     row_width = proj_rank // tensor_size
-    left_part = project(hidden, proj_in)
-    right_part = project(out_grad, proj_out)
-    parts = jnp.concatenate([left_part, right_part], axis=1)
+    parts = project_both(hidden, out_grad, proj_in, proj_out, seq_length)
     tokens = seq_count * seq_length
     block = tokens // tensor_size
     chunks = parts.reshape(tensor_size, block, 2 * proj_rank)

time: 64.4 us -> 63.8 us (level)
  Pallas kernels: 0 us -> 4.3 us
  matrix products: 4.64 us -> 1.06 us
  local copies, waits for them, and re-layouts: 3.85 us -> 2.56 us
    pallas_call x0 -> x1, Pallas kernels: none -> 4.3 us  [project_both(): pl.pallas_call(_project_kernel, grid=(tokens // tile,), in_specs=[pl.Bloc...]
    dot_general x2 -> x0, matrix products: 3.58 us -> none  [project(): lax.dot_general(flattened, projection, (((1,), (1,)), ((), ())), preferre...]
    concatenate x1 -> x0, local copies, waits for them, and re-layouts: 0.91 us -> none  [per_device(): parts = jnp.concatenate([left_part, right_part], axis=1)]
where the time goes in v6:
time: 63.8 us; the launch traced here: 63.4 us
  waiting for transfers between devices  28.1 us (44%)
  starting transfers between devices  24.2 us (38%)
  Pallas kernels  4.3 us (7%)
  local copies, waits for them, and re-layouts  2.56 us (4%)
  other arithmetic  2.38 us (4%)
  matrix products  1.06 us (2%)
  between operations  0.83 us (1%)
    all_to_all x1, starting transfers between devices, per_device(): lax.all_to_all(payload, 'dp', 0, 0, tiled=True)  16.6 us
    all_to_all x1, waiting for transfers between devices, per_device(): lax.all_to_all(payload, 'dp', 0, 0, tiled=True)  14.1 us
    all_to_all x1, waiting for transfers between devices, per_device(): mine = jnp.sum(lax.all_to_all(chunks, 'tensor', 0, 0, tiled=True), axis=0)  8.37 us
    all_to_all x1, waiting for transfers between devices, per_device(): rows = jnp.sum(lax.all_to_all(stacked, 'tensor', 0, 0, tiled=True), axis=0)  5.53 us
    pallas_call x1, Pallas kernels, project_both(): pl.pallas_call(_project_kernel, grid=(tokens // tile,), in_specs=[pl.Bloc...  4.3 us
    all_to_all x1, starting transfers between devices, per_device(): mine = jnp.sum(lax.all_to_all(chunks, 'tensor', 0, 0, tiled=True), axis=0)  4.3 us
    all_to_all x1, starting transfers between devices, per_device(): rows = jnp.sum(lax.all_to_all(stacked, 'tensor', 0, 0, tiled=True), axis=0)  3.36 us
  transfers between devices with their start and end apart: 3, of which 3 were waited for; matrix products, arithmetic and copies ran while one was open for 2% of the time, Pallas kernels for 0%

profile of v6, /device:TPU:8, one launch (start us, length us, event | category | flops | bytes accessed | tf_op | source)
XLA Modules:
  0.0 63.4 jit_solution(17430304393870157825)
XLA Ops:
  0.6 0.0 copy-start
  0.6 0.0 copy-start.3
  0.7 0.0 copy-start.4
  0.7 0.0 copy-start.2
  0.7 0.0 copy-start.1
  0.7 4.3 %shard_map.104 = f32[768,128]{1,0:T(8,128)} custom-call(bf16[768,1792]{1,0:T(8,128)(2,1)} %bitcast.25, bf16[768,512]{1,0:T(8,128)(2,1)} %bitcast.27, bf16[64,1792]{1,0:T(8,128)(2,1)} %proj_in_ref.1, bf16[64,512]{1,0:T(8,128)(2,1)} %proj_out_ref.1), custom_call_target="tpu_custom_call" | custom-call | tf_op jit(solution)/shard_map/pallas_call | solution.py:24
  5.0 4.3 %all-to-all-start = ((f32[8,96,128]{2,1,0:T(8,128)}), f32[8,96,128]{2,1,0:T(8,128)S(1)}, u32[]{:S(2)}, u32[]{:S(2)}) async-start(f32[8,96,128]{2,1,0:T(8,128)} %bitcast.26), calls=%async_computation | async-start | bytes 786432 | tf_op jit(solution)/shard_map/all_to_all | solution.py:49
  9.3 0.0 copy-done.3
  9.3 0.2 convert_reduce_fusion
  9.5 0.0 copy-done.4
  9.5 0.2 select_reduce_fusion.1
  9.7 0.1 broadcast_compare_fusion
  9.8 0.0 copy-done.2
  9.8 0.1 fusion.9
  9.9 8.4 %all-to-all-done = f32[8,96,128]{2,1,0:T(8,128)S(1)} async-done(((f32[8,96,128]{2,1,0:T(8,128)}), f32[8,96,128]{2,1,0:T(8,128)S(1)}, u32[]{:S(2)}, u32[]{:S(2)}) %all-to-all-start) | async-done | bytes 393248 | tf_op jit(solution)/shard_map/all_to_all | solution.py:49
  18.3 0.1 slice.24
  18.3 0.1 copy.22
  18.4 0.4 convolution_bitcast_fusion.1
  18.8 0.0 copy-done
  18.8 0.3 convolution_bitcast_fusion
  19.2 0.0 copy-done.1
  19.2 0.3 fusion.4
  19.5 0.7 %copy_bitcast_fusion = f32[8,3,8,128]{3,2,1,0:T(8,128)} fusion(f32[3,64,64]{2,1,0:T(8,128)S(1)} %fusion.4, f32[3,64,64]{2,1,0:T(8,128)S(1)} %convolution_bitcast_fusion.1), kind=kLoop, calls=%fused_computation.6 | loop fusion | flops 24576 | bytes 196608 | tf_op jit(solution)/shard_map/transpose | solution.py:61
  20.2 3.4 %all-to-all-start.1 = ((f32[8,3,8,128]{3,2,1,0:T(8,128)}), f32[8,3,8,128]{3,2,1,0:T(8,128)S(1)}, u32[]{:S(2)}, u32[]{:S(2)}) async-start(f32[8,3,8,128]{3,2,1,0:T(8,128)} %copy_bitcast_fusion), calls=%async_computation.1 | async-start | bytes 196608 | tf_op jit(solution)/shard_map/all_to_all | solution.py:62
  23.6 0.1 fusion.7
  23.7 0.1 copy.28
  23.8 5.5 %all-to-all-done.1 = f32[8,3,8,128]{3,2,1,0:T(8,128)S(1)} async-done(((f32[8,3,8,128]{3,2,1,0:T(8,128)}), f32[8,3,8,128]{3,2,1,0:T(8,128)S(1)}, u32[]{:S(2)}, u32[]{:S(2)}) %all-to-all-start.1) | async-done | bytes 98336 | tf_op jit(solution)/shard_map/all_to_all | solution.py:62
  29.3 0.1 fusion.10
  29.4 0.1 broadcast_in_dim.16
  29.5 0.1 select_reduce_fusion
  29.6 0.2 copy.27
  29.8 0.2 reshape.156
  30.1 1.0 %copy.29 = f32[64,1,1152]{2,1,0:T(1,128)} copy(f32[64,1,1152]{2,0,1:T(8,128)S(1)} %select_maximum_fusion) | data formatting | bytes 589824 | tf_op jit(solution)/shard_map/concatenate | solution.py:83
  31.1 16.6 %all-to-all-start.2 = ((f32[64,1,1152]{2,1,0:T(1,128)}), f32[64,1,1152]{2,1,0:T(1,128)S(1)}, u32[]{:S(2)}, u32[]{:S(2)}) async-start(f32[64,1,1152]{2,1,0:T(1,128)} %copy.29), calls=%async_computation.2 | async-start | bytes 589824 | tf_op jit(solution)/shard_map/all_to_all | solution.py:90
  47.7 0.7 %reshape.155 = f32[3,512]{1,0:T(4,128)} reshape(f32[3,8,64]{2,1,0:T(8,128)S(1)} %get-tuple-element.3) | data formatting | bytes 12288 | tf_op jit(solution)/shard_map/reshape | solution.py:63
  48.4 14.1 %all-to-all-done.2 = f32[64,1,1152]{2,1,0:T(1,128)S(1)} async-done(((f32[64,1,1152]{2,1,0:T(1,128)}), f32[64,1,1152]{2,1,0:T(1,128)S(1)}, u32[]{:S(2)}, u32[]{:S(2)}) %all-to-all-start.2) | async-done | bytes 294944 | tf_op jit(solution)/shard_map/all_to_all | solution.py:90
  62.5 0.2 reduce_sum.72
  62.8 0.7 %broadcast_divide_fusion = f32[2,512]{1,0:T(2,128)} fusion(f32[2,512]{1,0:T(2,128)S(1)} %reshape.157, f32[2]{0:T(128)S(1)} %slice_maximum_fusion), kind=kLoop, calls=%fused_computation.19 | loop fusion | flops 1024 | bytes 8200 | tf_op jit(solution)/shard_map/div | solution.py:93
  (9 shorter events, 0.1 us)
Async XLA Ops:
  0.6 18.2 %copy-start = (f32[64,64]{1,0:T(8,128)S(1)}, f32[64,64]{1,0:T(8,128)}, u32[]{:S(2)}) copy-start(f32[64,64]{1,0:T(8,128)} %param.13) | copy-start | bytes 49156
  0.6 8.7 %copy-start.3 = (s32[100]{0:T(128)S(1)}, s32[100]{0:T(128)}, u32[]{:S(2)}) copy-start(s32[100]{0:T(128)} %param.17) | copy-start | bytes 1204
  0.7 8.8 %copy-start.4 = (s32[3]{0:T(128)S(1)}, s32[3]{0:T(128)}, u32[]{:S(2)}) copy-start(s32[3]{0:T(128)} %param.16) | copy-start | bytes 40
  0.7 9.1 %copy-start.2 = (s32[3]{0:T(128)S(1)}, s32[3]{0:T(128)}, u32[]{:S(2)}) copy-start(s32[3]{0:T(128)} %param.15) | copy-start | bytes 40
  0.7 18.5 %copy-start.1 = (f32[64,64]{1,0:T(8,128)S(1)}, f32[64,64]{1,0:T(8,128)}, u32[]{:S(2)}) copy-start(f32[64,64]{1,0:T(8,128)} %param.14) | copy-start | bytes 49156
  5.0 13.2 %all-to-all-start = ((f32[8,96,128]{2,1,0:T(8,128)}), f32[8,96,128]{2,1,0:T(8,128)S(1)}, u32[]{:S(2)}, u32[]{:S(2)}) async-start(f32[8,96,128]{2,1,0:T(8,128)} %bitcast.26), calls=%async_computation | async-start | bytes 786432 | tf_op jit(solution)/shard_map/all_to_all | solution.py:49
  20.2 9.1 %all-to-all-start.1 = ((f32[8,3,8,128]{3,2,1,0:T(8,128)}), f32[8,3,8,128]{3,2,1,0:T(8,128)S(1)}, u32[]{:S(2)}, u32[]{:S(2)}) async-start(f32[8,3,8,128]{3,2,1,0:T(8,128)} %copy_bitcast_fusion), calls=%async_computation.1 | async-start | bytes 196608 | tf_op jit(solution)/shard_map/all_to_all | solution.py:62
  31.1 31.4 %all-to-all-start.2 = ((f32[64,1,1152]{2,1,0:T(1,128)}), f32[64,1,1152]{2,1,0:T(1,128)S(1)}, u32[]{:S(2)}, u32[]{:S(2)}) async-start(f32[64,1,1152]{2,1,0:T(1,128)} %copy.29), calls=%async_computation.2 | async-start | bytes 589824 | tf_op jit(solution)/shard_map/all_to_all | solution.py:90

commit v7 on v6

--- a/solution.py
+++ b/solution.py
@@ -36,7 +36,7 @@
 
 
 def per_device(hidden, out_grad, proj_in, proj_out, left_inv, right_inv, lengths, language, owner):
-    highest = lax.Precision.HIGHEST
+    high = lax.Precision.HIGH
     seq_count = hidden.shape[0]
     seq_length = hidden.shape[1]
     proj_rank = proj_in.shape[0]
@@ -53,9 +53,9 @@
     seq_index = jnp.arange(seq_count, dtype=jnp.int32)
     weight = (token_seq[None, :] == seq_index[:, None]) & (token_pos[None, :] < lengths[:, None])
     right_seq = mine[None, :, proj_rank:] * weight.astype(jnp.float32)[:, :, None]
-    grads_part = jnp.einsum("ti,stj->sij", mine[:, :proj_rank], right_seq, precision=highest)
-    left_done = jnp.einsum("ik,skj->sij", left_inv, grads_part, precision=highest)
-    pre_part = jnp.einsum("sik,kj->sij", left_done, right_inv, precision=highest)
+    grads_part = jnp.einsum("ti,stj->sij", mine[:, :proj_rank], right_seq, precision=high)
+    left_done = jnp.einsum("ik,skj->sij", left_inv, grads_part, precision=high)
+    pre_part = jnp.einsum("sik,kj->sij", left_done, right_inv, precision=high)
     stacked = jnp.concatenate([grads_part, pre_part], axis=2)
     stacked = stacked.reshape(seq_count, tensor_size, row_width, 2 * proj_rank)
     stacked = stacked.transpose(1, 0, 2, 3)

time: 63.8 us -> 63.6 us (level)
  no operation moved by 1% of the time
where the time goes in v7:
time: 63.6 us; the launch traced here: 63.2 us
  waiting for transfers between devices  28.1 us (44%)
  starting transfers between devices  24.2 us (38%)
  Pallas kernels  4.3 us (7%)
  local copies, waits for them, and re-layouts  2.56 us (4%)
  other arithmetic  2.38 us (4%)
  matrix products  0.84 us (1%)
  between operations  0.82 us (1%)
    all_to_all x1, starting transfers between devices, per_device(): lax.all_to_all(payload, 'dp', 0, 0, tiled=True)  16.6 us
    all_to_all x1, waiting for transfers between devices, per_device(): lax.all_to_all(payload, 'dp', 0, 0, tiled=True)  14.1 us
    all_to_all x1, waiting for transfers between devices, per_device(): mine = jnp.sum(lax.all_to_all(chunks, 'tensor', 0, 0, tiled=True), axis=0)  8.37 us
    all_to_all x1, waiting for transfers between devices, per_device(): rows = jnp.sum(lax.all_to_all(stacked, 'tensor', 0, 0, tiled=True), axis=0)  5.53 us
    pallas_call x1, Pallas kernels, project_both(): pl.pallas_call(_project_kernel, grid=(tokens // tile,), in_specs=[pl.Bloc...  4.3 us
    all_to_all x1, starting transfers between devices, per_device(): mine = jnp.sum(lax.all_to_all(chunks, 'tensor', 0, 0, tiled=True), axis=0)  4.3 us
    all_to_all x1, starting transfers between devices, per_device(): rows = jnp.sum(lax.all_to_all(stacked, 'tensor', 0, 0, tiled=True), axis=0)  3.36 us
  transfers between devices with their start and end apart: 3, of which 3 were waited for; matrix products, arithmetic and copies ran while one was open for 2% of the time, Pallas kernels for 0%

profile of v7, /device:TPU:8, one launch (start us, length us, event | category | flops | bytes accessed | tf_op | source)
XLA Modules:
  0.0 63.2 jit_solution(3003264296635886995)
XLA Ops:
  0.6 0.0 copy-start
  0.6 0.0 copy-start.3
  0.7 0.0 copy-start.4
  0.7 0.0 copy-start.2
  0.7 0.0 copy-start.1
  0.7 4.3 %shard_map.104 = f32[768,128]{1,0:T(8,128)} custom-call(bf16[768,1792]{1,0:T(8,128)(2,1)} %bitcast.25, bf16[768,512]{1,0:T(8,128)(2,1)} %bitcast.27, bf16[64,1792]{1,0:T(8,128)(2,1)} %proj_in_ref.1, bf16[64,512]{1,0:T(8,128)(2,1)} %proj_out_ref.1), custom_call_target="tpu_custom_call" | custom-call | tf_op jit(solution)/shard_map/pallas_call | solution.py:24
  5.0 4.3 %all-to-all-start = ((f32[8,96,128]{2,1,0:T(8,128)}), f32[8,96,128]{2,1,0:T(8,128)S(1)}, u32[]{:S(2)}, u32[]{:S(2)}) async-start(f32[8,96,128]{2,1,0:T(8,128)} %bitcast.26), calls=%async_computation | async-start | bytes 786432 | tf_op jit(solution)/shard_map/all_to_all | solution.py:49
  9.3 0.0 copy-done.3
  9.3 0.2 convert_reduce_fusion
  9.5 0.0 copy-done.4
  9.5 0.2 select_reduce_fusion.1
  9.7 0.1 broadcast_compare_fusion
  9.8 0.0 copy-done.2
  9.8 0.1 fusion.9
  9.9 8.4 %all-to-all-done = f32[8,96,128]{2,1,0:T(8,128)S(1)} async-done(((f32[8,96,128]{2,1,0:T(8,128)}), f32[8,96,128]{2,1,0:T(8,128)S(1)}, u32[]{:S(2)}, u32[]{:S(2)}) %all-to-all-start) | async-done | bytes 393248 | tf_op jit(solution)/shard_map/all_to_all | solution.py:49
  18.3 0.1 slice.24
  18.3 0.1 copy.22
  18.4 0.3 convolution_bitcast_fusion.1
  18.7 0.0 copy-done
  18.7 0.3 convolution_bitcast_fusion
  19.0 0.0 copy-done.1
  19.0 0.3 fusion.4
  19.3 0.7 %copy_bitcast_fusion = f32[8,3,8,128]{3,2,1,0:T(8,128)} fusion(f32[3,64,64]{2,1,0:T(8,128)S(1)} %fusion.4, f32[3,64,64]{2,1,0:T(8,128)S(1)} %convolution_bitcast_fusion.1), kind=kLoop, calls=%fused_computation.6 | loop fusion | flops 24576 | bytes 196608 | tf_op jit(solution)/shard_map/transpose | solution.py:61
  20.0 3.4 %all-to-all-start.1 = ((f32[8,3,8,128]{3,2,1,0:T(8,128)}), f32[8,3,8,128]{3,2,1,0:T(8,128)S(1)}, u32[]{:S(2)}, u32[]{:S(2)}) async-start(f32[8,3,8,128]{3,2,1,0:T(8,128)} %copy_bitcast_fusion), calls=%async_computation.1 | async-start | bytes 196608 | tf_op jit(solution)/shard_map/all_to_all | solution.py:62
  23.4 0.1 fusion.7
  23.5 0.1 copy.28
  23.6 5.5 %all-to-all-done.1 = f32[8,3,8,128]{3,2,1,0:T(8,128)S(1)} async-done(((f32[8,3,8,128]{3,2,1,0:T(8,128)}), f32[8,3,8,128]{3,2,1,0:T(8,128)S(1)}, u32[]{:S(2)}, u32[]{:S(2)}) %all-to-all-start.1) | async-done | bytes 98336 | tf_op jit(solution)/shard_map/all_to_all | solution.py:62
  29.1 0.1 fusion.10
  29.2 0.1 broadcast_in_dim.16
  29.3 0.1 select_reduce_fusion
  29.4 0.2 copy.27
  29.6 0.2 reshape.156
  29.9 1.0 %copy.29 = f32[64,1,1152]{2,1,0:T(1,128)} copy(f32[64,1,1152]{2,0,1:T(8,128)S(1)} %select_maximum_fusion) | data formatting | bytes 589824 | tf_op jit(solution)/shard_map/concatenate | solution.py:83
  30.9 16.6 %all-to-all-start.2 = ((f32[64,1,1152]{2,1,0:T(1,128)}), f32[64,1,1152]{2,1,0:T(1,128)S(1)}, u32[]{:S(2)}, u32[]{:S(2)}) async-start(f32[64,1,1152]{2,1,0:T(1,128)} %copy.29), calls=%async_computation.2 | async-start | bytes 589824 | tf_op jit(solution)/shard_map/all_to_all | solution.py:90
  47.5 0.7 %reshape.155 = f32[3,512]{1,0:T(4,128)} reshape(f32[3,8,64]{2,1,0:T(8,128)S(1)} %get-tuple-element.3) | data formatting | bytes 12288 | tf_op jit(solution)/shard_map/reshape | solution.py:63
  48.2 14.1 %all-to-all-done.2 = f32[64,1,1152]{2,1,0:T(1,128)S(1)} async-done(((f32[64,1,1152]{2,1,0:T(1,128)}), f32[64,1,1152]{2,1,0:T(1,128)S(1)}, u32[]{:S(2)}, u32[]{:S(2)}) %all-to-all-start.2) | async-done | bytes 294944 | tf_op jit(solution)/shard_map/all_to_all | solution.py:90
  62.3 0.2 reduce_sum.72
  62.5 0.7 %broadcast_divide_fusion = f32[2,512]{1,0:T(2,128)} fusion(f32[2,512]{1,0:T(2,128)S(1)} %reshape.157, f32[2]{0:T(128)S(1)} %slice_maximum_fusion), kind=kLoop, calls=%fused_computation.19 | loop fusion | flops 1024 | bytes 8200 | tf_op jit(solution)/shard_map/div | solution.py:93
  (9 shorter events, 0.1 us)
Async XLA Ops:
  0.6 18.1 %copy-start = (f32[64,64]{1,0:T(8,128)S(1)}, f32[64,64]{1,0:T(8,128)}, u32[]{:S(2)}) copy-start(f32[64,64]{1,0:T(8,128)} %param.13) | copy-start | bytes 49156
  0.6 8.7 %copy-start.3 = (s32[100]{0:T(128)S(1)}, s32[100]{0:T(128)}, u32[]{:S(2)}) copy-start(s32[100]{0:T(128)} %param.17) | copy-start | bytes 1204
  0.7 8.8 %copy-start.4 = (s32[3]{0:T(128)S(1)}, s32[3]{0:T(128)}, u32[]{:S(2)}) copy-start(s32[3]{0:T(128)} %param.16) | copy-start | bytes 40
  0.7 9.1 %copy-start.2 = (s32[3]{0:T(128)S(1)}, s32[3]{0:T(128)}, u32[]{:S(2)}) copy-start(s32[3]{0:T(128)} %param.15) | copy-start | bytes 40
  0.7 18.3 %copy-start.1 = (f32[64,64]{1,0:T(8,128)S(1)}, f32[64,64]{1,0:T(8,128)}, u32[]{:S(2)}) copy-start(f32[64,64]{1,0:T(8,128)} %param.14) | copy-start | bytes 49156
  5.0 13.2 %all-to-all-start = ((f32[8,96,128]{2,1,0:T(8,128)}), f32[8,96,128]{2,1,0:T(8,128)S(1)}, u32[]{:S(2)}, u32[]{:S(2)}) async-start(f32[8,96,128]{2,1,0:T(8,128)} %bitcast.26), calls=%async_computation | async-start | bytes 786432 | tf_op jit(solution)/shard_map/all_to_all | solution.py:49
  20.0 9.1 %all-to-all-start.1 = ((f32[8,3,8,128]{3,2,1,0:T(8,128)}), f32[8,3,8,128]{3,2,1,0:T(8,128)S(1)}, u32[]{:S(2)}, u32[]{:S(2)}) async-start(f32[8,3,8,128]{3,2,1,0:T(8,128)} %copy_bitcast_fusion), calls=%async_computation.1 | async-start | bytes 196608 | tf_op jit(solution)/shard_map/all_to_all | solution.py:62
  30.9 31.4 %all-to-all-start.2 = ((f32[64,1,1152]{2,1,0:T(1,128)}), f32[64,1,1152]{2,1,0:T(1,128)S(1)}, u32[]{:S(2)}, u32[]{:S(2)}) async-start(f32[64,1,1152]{2,1,0:T(1,128)} %copy.29), calls=%async_computation.2 | async-start | bytes 589824 | tf_op jit(solution)/shard_map/all_to_all | solution.py:90

commit v8 on v7

--- a/solution.py
+++ b/solution.py
@@ -72,25 +72,18 @@
     lang_place = owner * slot_count + lang_slot
     lang_hot = (language[:, None] == lang_index[None, :]).astype(jnp.int32)
     seq_place = jnp.sum(lang_hot * lang_place[None, :], axis=1)
-    slot_index = jnp.arange(owned_rows, dtype=jnp.int32).reshape(dp_size, 1, slot_count)
-    place_match = seq_place[:, None, None, None] == slot_index[None]
-    slot_sums = jnp.sum(
-        jnp.where(place_match[..., None], pre_flat[:, None, None, None, :], 0.0), axis=0
-    )
+    slot_index = jnp.arange(owned_rows, dtype=jnp.int32).reshape(dp_size, slot_count)
+    place_match = seq_place[:, None, None] == slot_index[None]
+    slot_sums = jnp.sum(jnp.where(place_match[..., None], pre_flat[:, None, None, :], 0.0), axis=0)
     slot_counts = jnp.sum(place_match.astype(jnp.float32), axis=0)
-    width = pre_flat.shape[1]
     count_pad = 128
     payload = jnp.concatenate(
-        [
-            slot_sums.reshape(dp_size, 1, slot_count * width),
-            jnp.pad(slot_counts, ((0, 0), (0, 0), (0, count_pad - slot_count))),
-        ],
+        [slot_sums, jnp.pad(slot_counts[:, :, None], ((0, 0), (0, 0), (0, count_pad - 1)))],
         axis=2,
     )
-    gathered = jnp.sum(lax.all_to_all(payload, "dp", 0, 0, tiled=True), axis=(0, 1))
-    summed = gathered[: slot_count * width].reshape(slot_count, width)
-    counted = gathered[slot_count * width : slot_count * width + slot_count]
-    owned_means = summed / jnp.maximum(counted, 1.0)[:, None]
+    gathered = jnp.sum(lax.all_to_all(payload, "dp", 0, 0, tiled=True), axis=0)
+    width = pre_flat.shape[1]
+    owned_means = gathered[:, :width] / jnp.maximum(gathered[:, width], 1.0)[:, None]
     return (grad_flat, owned_means)
 
 

time: 63.6 us -> 63.8 us (level)
  no operation moved by 1% of the time
where the time goes in v8:
time: 63.8 us; the launch traced here: 63.4 us
  waiting for transfers between devices  28.7 us (45%)
  starting transfers between devices  24.2 us (38%)
  Pallas kernels  4.3 us (7%)
  other arithmetic  2.36 us (4%)
  local copies, waits for them, and re-layouts  2.07 us (3%)
  matrix products  0.84 us (1%)
  between operations  0.8 us (1%)
    all_to_all x1, starting transfers between devices, per_device(): gathered = jnp.sum(lax.all_to_all(payload, 'dp', 0, 0, tiled=True), axis=0)  16.6 us
    all_to_all x1, waiting for transfers between devices, per_device(): gathered = jnp.sum(lax.all_to_all(payload, 'dp', 0, 0, tiled=True), axis=0)  14.8 us
    all_to_all x1, waiting for transfers between devices, per_device(): mine = jnp.sum(lax.all_to_all(chunks, 'tensor', 0, 0, tiled=True), axis=0)  8.45 us
    all_to_all x1, waiting for transfers between devices, per_device(): rows = jnp.sum(lax.all_to_all(stacked, 'tensor', 0, 0, tiled=True), axis=0)  5.52 us
    pallas_call x1, Pallas kernels, project_both(): pl.pallas_call(_project_kernel, grid=(tokens // tile,), in_specs=[pl.Bloc...  4.3 us
    all_to_all x1, starting transfers between devices, per_device(): mine = jnp.sum(lax.all_to_all(chunks, 'tensor', 0, 0, tiled=True), axis=0)  4.3 us
    all_to_all x1, starting transfers between devices, per_device(): rows = jnp.sum(lax.all_to_all(stacked, 'tensor', 0, 0, tiled=True), axis=0)  3.36 us
  transfers between devices with their start and end apart: 3, of which 3 were waited for; matrix products, arithmetic and copies ran while one was open for 2% of the time, Pallas kernels for 0%

profile of v8, /device:TPU:8, one launch (start us, length us, event | category | flops | bytes accessed | tf_op | source)
XLA Modules:
  0.0 63.4 jit_solution(7610630108721674902)
XLA Ops:
  0.6 0.0 copy-start
  0.6 0.0 copy-start.3
  0.7 0.0 copy-start.4
  0.7 0.0 copy-start.2
  0.7 0.0 copy-start.1
  0.7 4.3 %shard_map.104 = f32[768,128]{1,0:T(8,128)} custom-call(bf16[768,1792]{1,0:T(8,128)(2,1)} %bitcast.25, bf16[768,512]{1,0:T(8,128)(2,1)} %bitcast.27, bf16[64,1792]{1,0:T(8,128)(2,1)} %proj_in_ref.1, bf16[64,512]{1,0:T(8,128)(2,1)} %proj_out_ref.1), custom_call_target="tpu_custom_call" | custom-call | tf_op jit(solution)/shard_map/pallas_call | solution.py:24
  5.0 4.3 %all-to-all-start = ((f32[8,96,128]{2,1,0:T(8,128)}), f32[8,96,128]{2,1,0:T(8,128)S(1)}, u32[]{:S(2)}, u32[]{:S(2)}) async-start(f32[8,96,128]{2,1,0:T(8,128)} %bitcast.26), calls=%async_computation | async-start | bytes 786432 | tf_op jit(solution)/shard_map/all_to_all | solution.py:49
  9.3 0.0 copy-done.3
  9.3 0.2 convert_reduce_fusion
  9.5 0.0 copy-done.4
  9.5 0.2 select_reduce_fusion.1
  9.7 0.0 copy-done.2
  9.7 0.1 fusion.8
  9.8 8.5 %all-to-all-done = f32[8,96,128]{2,1,0:T(8,128)S(1)} async-done(((f32[8,96,128]{2,1,0:T(8,128)}), f32[8,96,128]{2,1,0:T(8,128)S(1)}, u32[]{:S(2)}, u32[]{:S(2)}) %all-to-all-start) | async-done | bytes 393248 | tf_op jit(solution)/shard_map/all_to_all | solution.py:49
  18.3 0.1 slice.24
  18.3 0.1 copy.28
  18.4 0.3 convolution_bitcast_fusion.1
  18.7 0.0 copy-done
  18.7 0.3 convolution_bitcast_fusion
  19.0 0.0 copy-done.1
  19.0 0.3 fusion.4
  19.3 0.7 %copy_bitcast_fusion = f32[8,3,8,128]{3,2,1,0:T(8,128)} fusion(f32[3,64,64]{2,1,0:T(8,128)S(1)} %fusion.4, f32[3,64,64]{2,1,0:T(8,128)S(1)} %convolution_bitcast_fusion.1), kind=kLoop, calls=%fused_computation.6 | loop fusion | flops 24576 | bytes 196608 | tf_op jit(solution)/shard_map/transpose | solution.py:61
  20.0 3.4 %all-to-all-start.1 = ((f32[8,3,8,128]{3,2,1,0:T(8,128)}), f32[8,3,8,128]{3,2,1,0:T(8,128)S(1)}, u32[]{:S(2)}, u32[]{:S(2)}) async-start(f32[8,3,8,128]{3,2,1,0:T(8,128)} %copy_bitcast_fusion), calls=%async_computation.1 | async-start | bytes 196608 | tf_op jit(solution)/shard_map/all_to_all | solution.py:62
  23.4 0.1 convert_reduce_fusion.1
  23.5 0.1 copy.33
  23.6 5.5 %all-to-all-done.1 = f32[8,3,8,128]{3,2,1,0:T(8,128)S(1)} async-done(((f32[8,3,8,128]{3,2,1,0:T(8,128)}), f32[8,3,8,128]{3,2,1,0:T(8,128)S(1)}, u32[]{:S(2)}, u32[]{:S(2)}) %all-to-all-start.1) | async-done | bytes 98336 | tf_op jit(solution)/shard_map/all_to_all | solution.py:62
  29.1 0.1 fusion.10
  29.2 0.1 broadcast_in_dim.18
  29.3 0.1 select_reduce_fusion
  29.4 1.0 %copy.34 = f32[64,2,640]{2,1,0:T(2,128)} copy(f32[64,2,640]{2,0,1:T(8,128)S(1)} %select_maximum_fusion) | data formatting | bytes 655360 | tf_op jit(solution)/shard_map/concatenate | solution.py:80
  30.4 16.6 %all-to-all-start.2 = ((f32[64,2,640]{2,1,0:T(2,128)}), f32[64,2,640]{2,1,0:T(2,128)S(1)}, u32[]{:S(2)}, u32[]{:S(2)}) async-start(f32[64,2,640]{2,1,0:T(2,128)} %copy.34), calls=%async_computation.2 | async-start | bytes 655360 | tf_op jit(solution)/shard_map/all_to_all | solution.py:84
  47.0 0.7 %reshape.122 = f32[3,512]{1,0:T(4,128)} reshape(f32[3,8,64]{2,1,0:T(8,128)S(1)} %get-tuple-element.5) | data formatting | bytes 12288 | tf_op jit(solution)/shard_map/reshape | solution.py:63
  47.7 14.8 %all-to-all-done.2 = f32[64,2,640]{2,1,0:T(2,128)S(1)} async-done(((f32[64,2,640]{2,1,0:T(2,128)}), f32[64,2,640]{2,1,0:T(2,128)S(1)}, u32[]{:S(2)}, u32[]{:S(2)}) %all-to-all-start.2) | async-done | bytes 327712 | tf_op jit(solution)/shard_map/all_to_all | solution.py:84
  62.4 0.1 reduce_sum.69
  62.6 0.1 fusion.9
  62.7 0.7 %slice_divide_fusion = f32[2,512]{1,0:T(2,128)} fusion(f32[2,640]{1,0:T(2,128)S(1)} %reduce_sum.69, f32[2]{0:T(128)S(1)} %fusion.9), kind=kLoop, calls=%fused_computation.17 | loop fusion | flops 1024 | bytes 8200 | tf_op jit(solution)/shard_map/div | solution.py:86
  (6 shorter events, 0.1 us)
Async XLA Ops:
  0.6 18.1 %copy-start = (f32[64,64]{1,0:T(8,128)S(1)}, f32[64,64]{1,0:T(8,128)}, u32[]{:S(2)}) copy-start(f32[64,64]{1,0:T(8,128)} %param.13) | copy-start | bytes 49156
  0.6 8.7 %copy-start.3 = (s32[100]{0:T(128)S(1)}, s32[100]{0:T(128)}, u32[]{:S(2)}) copy-start(s32[100]{0:T(128)} %param.17) | copy-start | bytes 1204
  0.7 8.9 %copy-start.4 = (s32[3]{0:T(128)S(1)}, s32[3]{0:T(128)}, u32[]{:S(2)}) copy-start(s32[3]{0:T(128)} %param.16) | copy-start | bytes 40
  0.7 9.0 %copy-start.2 = (s32[3]{0:T(128)S(1)}, s32[3]{0:T(128)}, u32[]{:S(2)}) copy-start(s32[3]{0:T(128)} %param.15) | copy-start | bytes 40
  0.7 18.3 %copy-start.1 = (f32[64,64]{1,0:T(8,128)S(1)}, f32[64,64]{1,0:T(8,128)}, u32[]{:S(2)}) copy-start(f32[64,64]{1,0:T(8,128)} %param.14) | copy-start | bytes 49156
  5.0 13.2 %all-to-all-start = ((f32[8,96,128]{2,1,0:T(8,128)}), f32[8,96,128]{2,1,0:T(8,128)S(1)}, u32[]{:S(2)}, u32[]{:S(2)}) async-start(f32[8,96,128]{2,1,0:T(8,128)} %bitcast.26), calls=%async_computation | async-start | bytes 786432 | tf_op jit(solution)/shard_map/all_to_all | solution.py:49
  20.0 9.1 %all-to-all-start.1 = ((f32[8,3,8,128]{3,2,1,0:T(8,128)}), f32[8,3,8,128]{3,2,1,0:T(8,128)S(1)}, u32[]{:S(2)}, u32[]{:S(2)}) async-start(f32[8,3,8,128]{3,2,1,0:T(8,128)} %copy_bitcast_fusion), calls=%async_computation.1 | async-start | bytes 196608 | tf_op jit(solution)/shard_map/all_to_all | solution.py:62
  30.4 32.0 %all-to-all-start.2 = ((f32[64,2,640]{2,1,0:T(2,128)}), f32[64,2,640]{2,1,0:T(2,128)S(1)}, u32[]{:S(2)}, u32[]{:S(2)}) async-start(f32[64,2,640]{2,1,0:T(2,128)} %copy.34), calls=%async_computation.2 | async-start | bytes 655360 | tf_op jit(solution)/shard_map/all_to_all | solution.py:84

commit v9 on v8

--- a/solution.py
+++ b/solution.py
@@ -35,8 +35,40 @@
     )(hidden, out_grad, proj_in, proj_out)
 
 
+def _block_kernel(recv_ref, weight_ref, left_inv_ref, right_inv_ref, out_ref):
+    peers, _, double = recv_ref.shape
+    rank = double // 2
+    _, seqs, width, _ = out_ref.shape
+    total = recv_ref[0]
+    for peer in range(1, peers):
+        total = total + recv_ref[peer]
+    left = total[:, :rank]
+    right = total[:, rank:]
+    highest = lax.Precision.HIGHEST
+    for s in range(seqs):
+        right_s = right * weight_ref[:, s : s + 1]
+        grads = lax.dot_general(
+            left, right_s, (((0,), (0,)), ((), ())), precision=highest,
+            preferred_element_type=jnp.float32,
+        )
+        left_done = jnp.dot(left_inv_ref[...], grads, precision=highest,
+                            preferred_element_type=jnp.float32)
+        pre = jnp.dot(left_done, right_inv_ref[...], precision=highest,
+                      preferred_element_type=jnp.float32)
+        for k in range(peers):
+            out_ref[k, s, :, :rank] = grads[k * width : (k + 1) * width, :]
+            out_ref[k, s, :, rank:] = pre[k * width : (k + 1) * width, :]
+
+
+def block_shares(recv, weight_t, left_inv, right_inv, seqs, width):
+    peers, tokens, double = recv.shape
+    return pl.pallas_call(
+        _block_kernel,
+        out_shape=jax.ShapeDtypeStruct((peers, seqs, width, double), jnp.float32),
+    )(recv, weight_t, left_inv, right_inv)
+
+
 def per_device(hidden, out_grad, proj_in, proj_out, left_inv, right_inv, lengths, language, owner):
-    high = lax.Precision.HIGH
     seq_count = hidden.shape[0]
     seq_length = hidden.shape[1]
     proj_rank = proj_in.shape[0]
@@ -46,19 +78,15 @@
     tokens = seq_count * seq_length
     block = tokens // tensor_size
     chunks = parts.reshape(tensor_size, block, 2 * proj_rank)
-    mine = jnp.sum(lax.all_to_all(chunks, "tensor", 0, 0, tiled=True), axis=0)
+    recv = lax.all_to_all(chunks, "tensor", 0, 0, tiled=True)
     token_at = lax.axis_index("tensor") * block + jnp.arange(block, dtype=jnp.int32)
     token_seq = token_at // seq_length
     token_pos = token_at % seq_length
     seq_index = jnp.arange(seq_count, dtype=jnp.int32)
-    weight = (token_seq[None, :] == seq_index[:, None]) & (token_pos[None, :] < lengths[:, None])
-    right_seq = mine[None, :, proj_rank:] * weight.astype(jnp.float32)[:, :, None]
-    grads_part = jnp.einsum("ti,stj->sij", mine[:, :proj_rank], right_seq, precision=high)
-    left_done = jnp.einsum("ik,skj->sij", left_inv, grads_part, precision=high)
-    pre_part = jnp.einsum("sik,kj->sij", left_done, right_inv, precision=high)
-    stacked = jnp.concatenate([grads_part, pre_part], axis=2)
-    stacked = stacked.reshape(seq_count, tensor_size, row_width, 2 * proj_rank)
-    stacked = stacked.transpose(1, 0, 2, 3)
+    weight = (token_seq[:, None] == seq_index[None, :]) & (token_pos[:, None] < lengths[None, :])
+    stacked = block_shares(
+        recv, weight.astype(jnp.float32), left_inv, right_inv, seq_count, row_width
+    )
     rows = jnp.sum(lax.all_to_all(stacked, "tensor", 0, 0, tiled=True), axis=0)
     grad_flat = rows[:, :, :proj_rank].reshape(seq_count, row_width * proj_rank)
     pre_flat = rows[:, :, proj_rank:].reshape(seq_count, row_width * proj_rank)

time: 63.8 us -> 65.7 us (1.030)
  Pallas kernels: 4.3 us -> 7.27 us
  matrix products: 0.84 us -> 0 us
    pallas_call x0 -> x1, Pallas kernels: none -> 2.97 us  [block_shares(): pl.pallas_call(_block_kernel, out_shape=jax.ShapeDtypeStruct((peers, seqs...]
    dot_general x3 -> x0, matrix products: 0.84 us -> none  [the longest x1 0.3 us: per_device(): jnp.einsum('ti,stj->sij', mine[:, :proj_rank], right_seq, precision=high)]
    unnamed x10 -> x8, local copies, waits for them, and re-layouts: 0.03 us -> 0.75 us
    transpose x1 -> x0, other arithmetic: 0.72 us -> none  [per_device(): stacked = stacked.transpose(1, 0, 2, 3)]
  transfers between devices with their start and end apart: 3 -> 3, of which waited for: 3 -> 3; matrix products, arithmetic and copies ran while one was open for 2% -> 3% of each run, Pallas kernels for 0% -> 0%
where the time goes in v9:
time: 65.7 us; the launch traced here: 65.3 us
  waiting for transfers between devices  28.1 us (43%)
  starting transfers between devices  24.2 us (37%)
  Pallas kernels  7.27 us (11%)
  local copies, waits for them, and re-layouts  2.65 us (4%)
  other arithmetic  2.25 us (3%)
  between operations  0.74 us (1%)
    all_to_all x1, starting transfers between devices, per_device(): gathered = jnp.sum(lax.all_to_all(payload, 'dp', 0, 0, tiled=True), axis=0)  16.6 us
    all_to_all x1, waiting for transfers between devices, per_device(): gathered = jnp.sum(lax.all_to_all(payload, 'dp', 0, 0, tiled=True), axis=0)  14.8 us
    all_to_all x1, waiting for transfers between devices, per_device(): recv = lax.all_to_all(chunks, 'tensor', 0, 0, tiled=True)  7.82 us
    all_to_all x1, waiting for transfers between devices, per_device(): rows = jnp.sum(lax.all_to_all(stacked, 'tensor', 0, 0, tiled=True), axis=0)  5.52 us
    all_to_all x1, starting transfers between devices, per_device(): recv = lax.all_to_all(chunks, 'tensor', 0, 0, tiled=True)  4.3 us
    pallas_call x1, Pallas kernels, project_both(): pl.pallas_call(_project_kernel, grid=(tokens // tile,), in_specs=[pl.Bloc...  4.29 us
    all_to_all x1, starting transfers between devices, per_device(): rows = jnp.sum(lax.all_to_all(stacked, 'tensor', 0, 0, tiled=True), axis=0)  3.36 us
    pallas_call x1, Pallas kernels, block_shares(): pl.pallas_call(_block_kernel, out_shape=jax.ShapeDtypeStruct((peers, seqs...  2.97 us
  transfers between devices with their start and end apart: 3, of which 3 were waited for; matrix products, arithmetic and copies ran while one was open for 3% of the time, Pallas kernels for 0%

profile of v9, /device:TPU:8, one launch (start us, length us, event | category | flops | bytes accessed | tf_op | source)
XLA Modules:
  0.0 65.3 jit_solution(1457724717319051214)
XLA Ops:
  0.6 0.0 copy-start.2
  0.6 0.0 copy-start.3
  0.7 0.0 copy-start.1
  0.7 4.3 %shard_map.104 = f32[768,128]{1,0:T(8,128)} custom-call(bf16[768,1792]{1,0:T(8,128)(2,1)} %bitcast.4, bf16[768,512]{1,0:T(8,128)(2,1)} %bitcast.6, bf16[64,1792]{1,0:T(8,128)(2,1)} %proj_in_ref.1, bf16[64,512]{1,0:T(8,128)(2,1)} %proj_out_ref.1), custom_call_target="tpu_custom_call" | custom-call | tf_op jit(solution)/shard_map/pallas_call | solution.py:24
  5.0 4.3 %all-to-all-start = ((f32[8,96,128]{2,1,0:T(8,128)}), f32[8,96,128]{2,1,0:T(8,128)S(1)}, u32[]{:S(2)}, u32[]{:S(2)}) async-start(f32[8,96,128]{2,1,0:T(8,128)} %bitcast.5), calls=%async_computation | async-start | bytes 786432 | tf_op jit(solution)/shard_map/all_to_all | solution.py:81
  9.3 0.0 copy-done.2
  9.3 0.2 convert_reduce_fusion
  9.5 0.0 copy-done.3
  9.5 0.2 select_reduce_fusion.1
  9.7 0.0 copy-done.1
  9.7 0.7 %fusion.2.weight_ref = f32[96,3]{1,0:T(8,128)} fusion(s32[96]{0:T(128)S(1)} %get-tuple-element.7, s32[3]{0:T(128)S(1)} %copy-done.1, s32[96]{0:T(128)S(1)} %get-tuple-element.6), kind=kLoop, calls=%fused_computation.8 | loop fusion | flops 1152 | bytes 1932 | tf_op jit(solution)/shard_map/convert_element_type | solution.py:88
  10.4 7.8 %all-to-all-done.recv_ref = f32[8,96,128]{2,1,0:T(8,128)S(1)} async-done(((f32[8,96,128]{2,1,0:T(8,128)}), f32[8,96,128]{2,1,0:T(8,128)S(1)}, u32[]{:S(2)}, u32[]{:S(2)}) %all-to-all-start) | async-done | bytes 393248 | tf_op jit(solution)/shard_map/all_to_all | solution.py:81
  18.2 0.0 copy-start
  18.2 0.7 %copy-done = f32[8,96,128]{2,1,0:T(8,128)} copy-done((f32[8,96,128]{2,1,0:T(8,128)}, f32[8,96,128]{2,1,0:T(8,128)S(1)}, u32[]{:S(2)}) %copy-start) | copy-done | bytes 393240
  18.9 3.0 %shard_map.105 = f32[8,3,8,128]{3,2,1,0:T(8,128)} custom-call(f32[8,96,128]{2,1,0:T(8,128)} %copy-done, f32[96,3]{1,0:T(8,128)} %fusion.2.weight_ref, f32[64,64]{1,0:T(8,128)} %left_inv_ref.1, f32[64,64]{1,0:T(8,128)} %right_inv_ref.1), custom_call_target="tpu_custom_call" | custom-call | tf_op jit(solution)/shard_map/pallas_call | solution.py:65
  21.9 3.4 %all-to-all-start.1 = ((f32[8,3,8,128]{3,2,1,0:T(8,128)}), f32[8,3,8,128]{3,2,1,0:T(8,128)S(1)}, u32[]{:S(2)}, u32[]{:S(2)}) async-start(f32[8,3,8,128]{3,2,1,0:T(8,128)} %shard_map.105), calls=%async_computation.1 | async-start | bytes 196608 | tf_op jit(solution)/shard_map/all_to_all | solution.py:90
  25.3 0.1 convert_reduce_fusion.1
  25.4 0.1 copy.18
  25.5 5.5 %all-to-all-done.1 = f32[8,3,8,128]{3,2,1,0:T(8,128)S(1)} async-done(((f32[8,3,8,128]{3,2,1,0:T(8,128)}), f32[8,3,8,128]{3,2,1,0:T(8,128)S(1)}, u32[]{:S(2)}, u32[]{:S(2)}) %all-to-all-start.1) | async-done | bytes 98336 | tf_op jit(solution)/shard_map/all_to_all | solution.py:90
  31.0 0.1 fusion.4
  31.1 0.1 broadcast_in_dim.18
  31.2 0.1 select_reduce_fusion
  31.3 1.0 %copy.19 = f32[64,2,640]{2,1,0:T(2,128)} copy(f32[64,2,640]{2,0,1:T(8,128)S(1)} %select_maximum_fusion) | data formatting | bytes 655360 | tf_op jit(solution)/shard_map/concatenate | solution.py:108
  32.3 16.6 %all-to-all-start.2 = ((f32[64,2,640]{2,1,0:T(2,128)}), f32[64,2,640]{2,1,0:T(2,128)S(1)}, u32[]{:S(2)}, u32[]{:S(2)}) async-start(f32[64,2,640]{2,1,0:T(2,128)} %copy.19), calls=%async_computation.2 | async-start | bytes 655360 | tf_op jit(solution)/shard_map/all_to_all | solution.py:112
  48.9 0.7 %reshape.69 = f32[3,512]{1,0:T(4,128)} reshape(f32[3,8,64]{2,1,0:T(8,128)S(1)} %get-tuple-element.5) | data formatting | bytes 12288 | tf_op jit(solution)/shard_map/reshape | solution.py:91
  49.6 14.8 %all-to-all-done.2 = f32[64,2,640]{2,1,0:T(2,128)S(1)} async-done(((f32[64,2,640]{2,1,0:T(2,128)}), f32[64,2,640]{2,1,0:T(2,128)S(1)}, u32[]{:S(2)}, u32[]{:S(2)}) %all-to-all-start.2) | async-done | bytes 327712 | tf_op jit(solution)/shard_map/all_to_all | solution.py:112
  64.3 0.1 reduce_sum.59
  64.5 0.1 fusion.3
  64.6 0.7 %slice_divide_fusion = f32[2,512]{1,0:T(2,128)} fusion(f32[2,640]{1,0:T(2,128)S(1)} %reduce_sum.59, f32[2]{0:T(128)S(1)} %fusion.3), kind=kLoop, calls=%fused_computation.9 | loop fusion | flops 1024 | bytes 8200 | tf_op jit(solution)/shard_map/div | solution.py:114
  (5 shorter events, 0.1 us)
Async XLA Ops:
  0.6 8.6 %copy-start.2 = (s32[100]{0:T(128)S(1)}, s32[100]{0:T(128)}, u32[]{:S(2)}) copy-start(s32[100]{0:T(128)} %param.17) | copy-start | bytes 1204
  0.6 8.8 %copy-start.3 = (s32[3]{0:T(128)S(1)}, s32[3]{0:T(128)}, u32[]{:S(2)}) copy-start(s32[3]{0:T(128)} %param.16) | copy-start | bytes 40
  0.7 9.0 %copy-start.1 = (s32[3]{0:T(128)S(1)}, s32[3]{0:T(128)}, u32[]{:S(2)}) copy-start(s32[3]{0:T(128)} %param.15) | copy-start | bytes 40
  5.0 13.2 %all-to-all-start = ((f32[8,96,128]{2,1,0:T(8,128)}), f32[8,96,128]{2,1,0:T(8,128)S(1)}, u32[]{:S(2)}, u32[]{:S(2)}) async-start(f32[8,96,128]{2,1,0:T(8,128)} %bitcast.5), calls=%async_computation | async-start | bytes 786432 | tf_op jit(solution)/shard_map/all_to_all | solution.py:81
  18.2 0.7 %copy-start = (f32[8,96,128]{2,1,0:T(8,128)}, f32[8,96,128]{2,1,0:T(8,128)S(1)}, u32[]{:S(2)}) copy-start(f32[8,96,128]{2,1,0:T(8,128)S(1)} %all-to-all-done.recv_ref) | copy-start | bytes 1179652
  21.9 9.1 %all-to-all-start.1 = ((f32[8,3,8,128]{3,2,1,0:T(8,128)}), f32[8,3,8,128]{3,2,1,0:T(8,128)S(1)}, u32[]{:S(2)}, u32[]{:S(2)}) async-start(f32[8,3,8,128]{3,2,1,0:T(8,128)} %shard_map.105), calls=%async_computation.1 | async-start | bytes 196608 | tf_op jit(solution)/shard_map/all_to_all | solution.py:90
  32.3 32.0 %all-to-all-start.2 = ((f32[64,2,640]{2,1,0:T(2,128)}), f32[64,2,640]{2,1,0:T(2,128)S(1)}, u32[]{:S(2)}, u32[]{:S(2)}) async-start(f32[64,2,640]{2,1,0:T(2,128)} %copy.19), calls=%async_computation.2 | async-start | bytes 655360 | tf_op jit(solution)/shard_map/all_to_all | solution.py:112

commit v10 on v8

--- a/solution.py
+++ b/solution.py
@@ -42,7 +42,7 @@
     proj_rank = proj_in.shape[0]
     tensor_size = lax.axis_size("tensor")
     row_width = proj_rank // tensor_size
-    parts = project_both(hidden, out_grad, proj_in, proj_out, seq_length)
+    parts = project_both(hidden, out_grad, proj_in, proj_out, seq_count * seq_length)
     tokens = seq_count * seq_length
     block = tokens // tensor_size
     chunks = parts.reshape(tensor_size, block, 2 * proj_rank)

time: 63.8 us -> 63.3 us (level)
  no operation moved by 1% of the time
where the time goes in v10:
time: 63.3 us; the launch traced here: 63 us
  waiting for transfers between devices  28.7 us (45%)
  starting transfers between devices  24.2 us (38%)
  Pallas kernels  3.9 us (6%)
  other arithmetic  2.36 us (4%)
  local copies, waits for them, and re-layouts  2.07 us (3%)
  matrix products  0.85 us (1%)
  between operations  0.8 us (1%)
    all_to_all x1, starting transfers between devices, per_device(): gathered = jnp.sum(lax.all_to_all(payload, 'dp', 0, 0, tiled=True), axis=0)  16.6 us
    all_to_all x1, waiting for transfers between devices, per_device(): gathered = jnp.sum(lax.all_to_all(payload, 'dp', 0, 0, tiled=True), axis=0)  14.8 us
    all_to_all x1, waiting for transfers between devices, per_device(): mine = jnp.sum(lax.all_to_all(chunks, 'tensor', 0, 0, tiled=True), axis=0)  8.45 us
    all_to_all x1, waiting for transfers between devices, per_device(): rows = jnp.sum(lax.all_to_all(stacked, 'tensor', 0, 0, tiled=True), axis=0)  5.52 us
    all_to_all x1, starting transfers between devices, per_device(): mine = jnp.sum(lax.all_to_all(chunks, 'tensor', 0, 0, tiled=True), axis=0)  4.3 us
    pallas_call x1, Pallas kernels, project_both(): pl.pallas_call(_project_kernel, grid=(tokens // tile,), in_specs=[pl.Bloc...  3.9 us
    all_to_all x1, starting transfers between devices, per_device(): rows = jnp.sum(lax.all_to_all(stacked, 'tensor', 0, 0, tiled=True), axis=0)  3.36 us
  transfers between devices with their start and end apart: 3, of which 3 were waited for; matrix products, arithmetic and copies ran while one was open for 2% of the time, Pallas kernels for 0%

profile of v10, /device:TPU:8, one launch (start us, length us, event | category | flops | bytes accessed | tf_op | source)
XLA Modules:
  0.0 63.0 jit_solution(12489025529277368622)
XLA Ops:
  0.6 0.0 copy-start
  0.6 0.0 copy-start.3
  0.7 0.0 copy-start.4
  0.7 0.0 copy-start.2
  0.7 0.0 copy-start.1
  0.7 3.9 %shard_map.104 = f32[768,128]{1,0:T(8,128)} custom-call(bf16[768,1792]{1,0:T(8,128)(2,1)} %bitcast.25, bf16[768,512]{1,0:T(8,128)(2,1)} %bitcast.27, bf16[64,1792]{1,0:T(8,128)(2,1)} %proj_in_ref.1, bf16[64,512]{1,0:T(8,128)(2,1)} %proj_out_ref.1), custom_call_target="tpu_custom_call" | custom-call | tf_op jit(solution)/shard_map/pallas_call | solution.py:24
  4.6 4.3 %all-to-all-start = ((f32[8,96,128]{2,1,0:T(8,128)}), f32[8,96,128]{2,1,0:T(8,128)S(1)}, u32[]{:S(2)}, u32[]{:S(2)}) async-start(f32[8,96,128]{2,1,0:T(8,128)} %bitcast.26), calls=%async_computation | async-start | bytes 786432 | tf_op jit(solution)/shard_map/all_to_all | solution.py:49
  8.9 0.0 copy-done.3
  8.9 0.2 convert_reduce_fusion
  9.1 0.0 copy-done.4
  9.1 0.2 select_reduce_fusion.1
  9.3 0.0 copy-done.2
  9.3 0.1 fusion.8
  9.4 8.5 %all-to-all-done = f32[8,96,128]{2,1,0:T(8,128)S(1)} async-done(((f32[8,96,128]{2,1,0:T(8,128)}), f32[8,96,128]{2,1,0:T(8,128)S(1)}, u32[]{:S(2)}, u32[]{:S(2)}) %all-to-all-start) | async-done | bytes 393248 | tf_op jit(solution)/shard_map/all_to_all | solution.py:49
  17.9 0.1 slice.24
  17.9 0.1 copy.28
  18.0 0.3 convolution_bitcast_fusion.1
  18.3 0.0 copy-done
  18.3 0.3 convolution_bitcast_fusion
  18.6 0.0 copy-done.1
  18.6 0.3 fusion.4
  18.9 0.7 %copy_bitcast_fusion = f32[8,3,8,128]{3,2,1,0:T(8,128)} fusion(f32[3,64,64]{2,1,0:T(8,128)S(1)} %fusion.4, f32[3,64,64]{2,1,0:T(8,128)S(1)} %convolution_bitcast_fusion.1), kind=kLoop, calls=%fused_computation.6 | loop fusion | flops 24576 | bytes 196608 | tf_op jit(solution)/shard_map/transpose | solution.py:61
  19.6 3.4 %all-to-all-start.1 = ((f32[8,3,8,128]{3,2,1,0:T(8,128)}), f32[8,3,8,128]{3,2,1,0:T(8,128)S(1)}, u32[]{:S(2)}, u32[]{:S(2)}) async-start(f32[8,3,8,128]{3,2,1,0:T(8,128)} %copy_bitcast_fusion), calls=%async_computation.1 | async-start | bytes 196608 | tf_op jit(solution)/shard_map/all_to_all | solution.py:62
  23.0 0.1 convert_reduce_fusion.1
  23.1 0.1 copy.33
  23.2 5.5 %all-to-all-done.1 = f32[8,3,8,128]{3,2,1,0:T(8,128)S(1)} async-done(((f32[8,3,8,128]{3,2,1,0:T(8,128)}), f32[8,3,8,128]{3,2,1,0:T(8,128)S(1)}, u32[]{:S(2)}, u32[]{:S(2)}) %all-to-all-start.1) | async-done | bytes 98336 | tf_op jit(solution)/shard_map/all_to_all | solution.py:62
  28.7 0.1 fusion.10
  28.8 0.1 broadcast_in_dim.18
  28.9 0.1 select_reduce_fusion
  29.0 1.0 %copy.34 = f32[64,2,640]{2,1,0:T(2,128)} copy(f32[64,2,640]{2,0,1:T(8,128)S(1)} %select_maximum_fusion) | data formatting | bytes 655360 | tf_op jit(solution)/shard_map/concatenate | solution.py:80
  30.0 16.6 %all-to-all-start.2 = ((f32[64,2,640]{2,1,0:T(2,128)}), f32[64,2,640]{2,1,0:T(2,128)S(1)}, u32[]{:S(2)}, u32[]{:S(2)}) async-start(f32[64,2,640]{2,1,0:T(2,128)} %copy.34), calls=%async_computation.2 | async-start | bytes 655360 | tf_op jit(solution)/shard_map/all_to_all | solution.py:84
  46.6 0.7 %reshape.122 = f32[3,512]{1,0:T(4,128)} reshape(f32[3,8,64]{2,1,0:T(8,128)S(1)} %get-tuple-element.5) | data formatting | bytes 12288 | tf_op jit(solution)/shard_map/reshape | solution.py:63
  47.3 14.8 %all-to-all-done.2 = f32[64,2,640]{2,1,0:T(2,128)S(1)} async-done(((f32[64,2,640]{2,1,0:T(2,128)}), f32[64,2,640]{2,1,0:T(2,128)S(1)}, u32[]{:S(2)}, u32[]{:S(2)}) %all-to-all-start.2) | async-done | bytes 327712 | tf_op jit(solution)/shard_map/all_to_all | solution.py:84
  62.0 0.1 reduce_sum.69
  62.2 0.1 fusion.9
  62.3 0.7 %slice_divide_fusion = f32[2,512]{1,0:T(2,128)} fusion(f32[2,640]{1,0:T(2,128)S(1)} %reduce_sum.69, f32[2]{0:T(128)S(1)} %fusion.9), kind=kLoop, calls=%fused_computation.17 | loop fusion | flops 1024 | bytes 8200 | tf_op jit(solution)/shard_map/div | solution.py:86
  (6 shorter events, 0.1 us)
Async XLA Ops:
  0.6 17.7 %copy-start = (f32[64,64]{1,0:T(8,128)S(1)}, f32[64,64]{1,0:T(8,128)}, u32[]{:S(2)}) copy-start(f32[64,64]{1,0:T(8,128)} %param.13) | copy-start | bytes 49156
  0.6 8.3 %copy-start.3 = (s32[100]{0:T(128)S(1)}, s32[100]{0:T(128)}, u32[]{:S(2)}) copy-start(s32[100]{0:T(128)} %param.17) | copy-start | bytes 1204
  0.7 8.5 %copy-start.4 = (s32[3]{0:T(128)S(1)}, s32[3]{0:T(128)}, u32[]{:S(2)}) copy-start(s32[3]{0:T(128)} %param.16) | copy-start | bytes 40
  0.7 8.6 %copy-start.2 = (s32[3]{0:T(128)S(1)}, s32[3]{0:T(128)}, u32[]{:S(2)}) copy-start(s32[3]{0:T(128)} %param.15) | copy-start | bytes 40
  0.7 17.9 %copy-start.1 = (f32[64,64]{1,0:T(8,128)S(1)}, f32[64,64]{1,0:T(8,128)}, u32[]{:S(2)}) copy-start(f32[64,64]{1,0:T(8,128)} %param.14) | copy-start | bytes 49156
  4.6 13.2 %all-to-all-start = ((f32[8,96,128]{2,1,0:T(8,128)}), f32[8,96,128]{2,1,0:T(8,128)S(1)}, u32[]{:S(2)}, u32[]{:S(2)}) async-start(f32[8,96,128]{2,1,0:T(8,128)} %bitcast.26), calls=%async_computation | async-start | bytes 786432 | tf_op jit(solution)/shard_map/all_to_all | solution.py:49
  19.6 9.1 %all-to-all-start.1 = ((f32[8,3,8,128]{3,2,1,0:T(8,128)}), f32[8,3,8,128]{3,2,1,0:T(8,128)S(1)}, u32[]{:S(2)}, u32[]{:S(2)}) async-start(f32[8,3,8,128]{3,2,1,0:T(8,128)} %copy_bitcast_fusion), calls=%async_computation.1 | async-start | bytes 196608 | tf_op jit(solution)/shard_map/all_to_all | solution.py:62
  30.0 32.0 %all-to-all-start.2 = ((f32[64,2,640]{2,1,0:T(2,128)}), f32[64,2,640]{2,1,0:T(2,128)S(1)}, u32[]{:S(2)}, u32[]{:S(2)}) async-start(f32[64,2,640]{2,1,0:T(2,128)} %copy.34), calls=%async_computation.2 | async-start | bytes 655360 | tf_op jit(solution)/shard_map/all_to_all | solution.py:84

commit v11 on v10

--- a/solution.py
+++ b/solution.py
@@ -42,7 +42,7 @@
     proj_rank = proj_in.shape[0]
     tensor_size = lax.axis_size("tensor")
     row_width = proj_rank // tensor_size
-    parts = project_both(hidden, out_grad, proj_in, proj_out, seq_count * seq_length)
+    parts = project_both(hidden, out_grad, proj_in, proj_out, seq_count * seq_length // 2)
     tokens = seq_count * seq_length
     block = tokens // tensor_size
     chunks = parts.reshape(tensor_size, block, 2 * proj_rank)

time: 63.3 us -> 63 us (level)
  no operation moved by 1% of the time
where the time goes in v11:
time: 63 us; the launch traced here: 62.6 us
  waiting for transfers between devices  28.7 us (46%)
  starting transfers between devices  24.3 us (39%)
  Pallas kernels  3.54 us (6%)
  other arithmetic  2.36 us (4%)
  local copies, waits for them, and re-layouts  2.07 us (3%)
  matrix products  0.84 us (1%)
  between operations  0.8 us (1%)
    all_to_all x1, starting transfers between devices, per_device(): gathered = jnp.sum(lax.all_to_all(payload, 'dp', 0, 0, tiled=True), axis=0)  16.6 us
    all_to_all x1, waiting for transfers between devices, per_device(): gathered = jnp.sum(lax.all_to_all(payload, 'dp', 0, 0, tiled=True), axis=0)  14.8 us
    all_to_all x1, waiting for transfers between devices, per_device(): mine = jnp.sum(lax.all_to_all(chunks, 'tensor', 0, 0, tiled=True), axis=0)  8.45 us
    all_to_all x1, waiting for transfers between devices, per_device(): rows = jnp.sum(lax.all_to_all(stacked, 'tensor', 0, 0, tiled=True), axis=0)  5.52 us
    all_to_all x1, starting transfers between devices, per_device(): mine = jnp.sum(lax.all_to_all(chunks, 'tensor', 0, 0, tiled=True), axis=0)  4.3 us
    pallas_call x1, Pallas kernels, project_both(): pl.pallas_call(_project_kernel, grid=(tokens // tile,), in_specs=[pl.Bloc...  3.54 us
    all_to_all x1, starting transfers between devices, per_device(): rows = jnp.sum(lax.all_to_all(stacked, 'tensor', 0, 0, tiled=True), axis=0)  3.36 us
  transfers between devices with their start and end apart: 3, of which 3 were waited for; matrix products, arithmetic and copies ran while one was open for 2% of the time, Pallas kernels for 0%

profile of v11, /device:TPU:8, one launch (start us, length us, event | category | flops | bytes accessed | tf_op | source)
XLA Modules:
  0.0 62.6 jit_solution(9517927234216417461)
XLA Ops:
  0.6 0.0 copy-start
  0.6 0.0 copy-start.3
  0.7 0.0 copy-start.4
  0.7 0.0 copy-start.2
  0.7 0.0 copy-start.1
  0.7 3.5 %shard_map.104 = f32[768,128]{1,0:T(8,128)} custom-call(bf16[768,1792]{1,0:T(8,128)(2,1)} %bitcast.25, bf16[768,512]{1,0:T(8,128)(2,1)} %bitcast.27, bf16[64,1792]{1,0:T(8,128)(2,1)} %proj_in_ref.1, bf16[64,512]{1,0:T(8,128)(2,1)} %proj_out_ref.1), custom_call_target="tpu_custom_call" | custom-call | tf_op jit(solution)/shard_map/pallas_call | solution.py:24
  4.2 4.3 %all-to-all-start = ((f32[8,96,128]{2,1,0:T(8,128)}), f32[8,96,128]{2,1,0:T(8,128)S(1)}, u32[]{:S(2)}, u32[]{:S(2)}) async-start(f32[8,96,128]{2,1,0:T(8,128)} %bitcast.26), calls=%async_computation | async-start | bytes 786432 | tf_op jit(solution)/shard_map/all_to_all | solution.py:49
  8.5 0.0 copy-done.3
  8.6 0.2 convert_reduce_fusion
  8.8 0.0 copy-done.4
  8.8 0.2 select_reduce_fusion.1
  9.0 0.0 copy-done.2
  9.0 0.1 fusion.8
  9.0 8.5 %all-to-all-done = f32[8,96,128]{2,1,0:T(8,128)S(1)} async-done(((f32[8,96,128]{2,1,0:T(8,128)}), f32[8,96,128]{2,1,0:T(8,128)S(1)}, u32[]{:S(2)}, u32[]{:S(2)}) %all-to-all-start) | async-done | bytes 393248 | tf_op jit(solution)/shard_map/all_to_all | solution.py:49
  17.5 0.1 slice.24
  17.6 0.1 copy.28
  17.7 0.3 convolution_bitcast_fusion.1
  18.0 0.0 copy-done
  18.0 0.3 convolution_bitcast_fusion
  18.3 0.0 copy-done.1
  18.3 0.3 fusion.4
  18.5 0.7 %copy_bitcast_fusion = f32[8,3,8,128]{3,2,1,0:T(8,128)} fusion(f32[3,64,64]{2,1,0:T(8,128)S(1)} %fusion.4, f32[3,64,64]{2,1,0:T(8,128)S(1)} %convolution_bitcast_fusion.1), kind=kLoop, calls=%fused_computation.6 | loop fusion | flops 24576 | bytes 196608 | tf_op jit(solution)/shard_map/transpose | solution.py:61
  19.3 3.4 %all-to-all-start.1 = ((f32[8,3,8,128]{3,2,1,0:T(8,128)}), f32[8,3,8,128]{3,2,1,0:T(8,128)S(1)}, u32[]{:S(2)}, u32[]{:S(2)}) async-start(f32[8,3,8,128]{3,2,1,0:T(8,128)} %copy_bitcast_fusion), calls=%async_computation.1 | async-start | bytes 196608 | tf_op jit(solution)/shard_map/all_to_all | solution.py:62
  22.6 0.1 convert_reduce_fusion.1
  22.7 0.1 copy.33
  22.8 5.5 %all-to-all-done.1 = f32[8,3,8,128]{3,2,1,0:T(8,128)S(1)} async-done(((f32[8,3,8,128]{3,2,1,0:T(8,128)}), f32[8,3,8,128]{3,2,1,0:T(8,128)S(1)}, u32[]{:S(2)}, u32[]{:S(2)}) %all-to-all-start.1) | async-done | bytes 98336 | tf_op jit(solution)/shard_map/all_to_all | solution.py:62
  28.4 0.1 fusion.10
  28.4 0.1 broadcast_in_dim.18
  28.5 0.1 select_reduce_fusion
  28.7 1.0 %copy.34 = f32[64,2,640]{2,1,0:T(2,128)} copy(f32[64,2,640]{2,0,1:T(8,128)S(1)} %select_maximum_fusion) | data formatting | bytes 655360 | tf_op jit(solution)/shard_map/concatenate | solution.py:80
  29.6 16.6 %all-to-all-start.2 = ((f32[64,2,640]{2,1,0:T(2,128)}), f32[64,2,640]{2,1,0:T(2,128)S(1)}, u32[]{:S(2)}, u32[]{:S(2)}) async-start(f32[64,2,640]{2,1,0:T(2,128)} %copy.34), calls=%async_computation.2 | async-start | bytes 655360 | tf_op jit(solution)/shard_map/all_to_all | solution.py:84
  46.2 0.7 %reshape.122 = f32[3,512]{1,0:T(4,128)} reshape(f32[3,8,64]{2,1,0:T(8,128)S(1)} %get-tuple-element.5) | data formatting | bytes 12288 | tf_op jit(solution)/shard_map/reshape | solution.py:63
  46.9 14.8 %all-to-all-done.2 = f32[64,2,640]{2,1,0:T(2,128)S(1)} async-done(((f32[64,2,640]{2,1,0:T(2,128)}), f32[64,2,640]{2,1,0:T(2,128)S(1)}, u32[]{:S(2)}, u32[]{:S(2)}) %all-to-all-start.2) | async-done | bytes 327712 | tf_op jit(solution)/shard_map/all_to_all | solution.py:84
  61.7 0.1 reduce_sum.69
  61.8 0.1 fusion.9
  61.9 0.7 %slice_divide_fusion = f32[2,512]{1,0:T(2,128)} fusion(f32[2,640]{1,0:T(2,128)S(1)} %reduce_sum.69, f32[2]{0:T(128)S(1)} %fusion.9), kind=kLoop, calls=%fused_computation.17 | loop fusion | flops 1024 | bytes 8200 | tf_op jit(solution)/shard_map/div | solution.py:86
  (6 shorter events, 0.1 us)
Async XLA Ops:
  0.6 17.3 %copy-start = (f32[64,64]{1,0:T(8,128)S(1)}, f32[64,64]{1,0:T(8,128)}, u32[]{:S(2)}) copy-start(f32[64,64]{1,0:T(8,128)} %param.13) | copy-start | bytes 49156
  0.6 7.9 %copy-start.3 = (s32[100]{0:T(128)S(1)}, s32[100]{0:T(128)}, u32[]{:S(2)}) copy-start(s32[100]{0:T(128)} %param.17) | copy-start | bytes 1204
  0.7 8.1 %copy-start.4 = (s32[3]{0:T(128)S(1)}, s32[3]{0:T(128)}, u32[]{:S(2)}) copy-start(s32[3]{0:T(128)} %param.16) | copy-start | bytes 40
  0.7 8.3 %copy-start.2 = (s32[3]{0:T(128)S(1)}, s32[3]{0:T(128)}, u32[]{:S(2)}) copy-start(s32[3]{0:T(128)} %param.15) | copy-start | bytes 40
  0.7 17.6 %copy-start.1 = (f32[64,64]{1,0:T(8,128)S(1)}, f32[64,64]{1,0:T(8,128)}, u32[]{:S(2)}) copy-start(f32[64,64]{1,0:T(8,128)} %param.14) | copy-start | bytes 49156
  4.2 13.2 %all-to-all-start = ((f32[8,96,128]{2,1,0:T(8,128)}), f32[8,96,128]{2,1,0:T(8,128)S(1)}, u32[]{:S(2)}, u32[]{:S(2)}) async-start(f32[8,96,128]{2,1,0:T(8,128)} %bitcast.26), calls=%async_computation | async-start | bytes 786432 | tf_op jit(solution)/shard_map/all_to_all | solution.py:49
  19.3 9.1 %all-to-all-start.1 = ((f32[8,3,8,128]{3,2,1,0:T(8,128)}), f32[8,3,8,128]{3,2,1,0:T(8,128)S(1)}, u32[]{:S(2)}, u32[]{:S(2)}) async-start(f32[8,3,8,128]{3,2,1,0:T(8,128)} %copy_bitcast_fusion), calls=%async_computation.1 | async-start | bytes 196608 | tf_op jit(solution)/shard_map/all_to_all | solution.py:62
  29.6 32.0 %all-to-all-start.2 = ((f32[64,2,640]{2,1,0:T(2,128)}), f32[64,2,640]{2,1,0:T(2,128)S(1)}, u32[]{:S(2)}, u32[]{:S(2)}) async-start(f32[64,2,640]{2,1,0:T(2,128)} %copy.34), calls=%async_computation.2 | async-start | bytes 655360 | tf_op jit(solution)/shard_map/all_to_all | solution.py:84

commit v12 on v11

--- a/solution.py
+++ b/solution.py
@@ -42,7 +42,7 @@
     proj_rank = proj_in.shape[0]
     tensor_size = lax.axis_size("tensor")
     row_width = proj_rank // tensor_size
-    parts = project_both(hidden, out_grad, proj_in, proj_out, seq_count * seq_length // 2)
+    parts = project_both(hidden, out_grad, proj_in, proj_out, seq_count * seq_length // 4)
     tokens = seq_count * seq_length
     block = tokens // tensor_size
     chunks = parts.reshape(tensor_size, block, 2 * proj_rank)

time: 63 us -> 64.1 us (1.017)
  Pallas kernels: 3.54 us -> 4.6 us
    pallas_call x1, Pallas kernels: 3.54 us -> 4.6 us  [project_both(): pl.pallas_call(_project_kernel, grid=(tokens // tile,), in_specs=[pl.Bloc...]
where the time goes in v12:
time: 64.1 us; the launch traced here: 63.6 us
  waiting for transfers between devices  28.7 us (45%)
  starting transfers between devices  24.2 us (38%)
  Pallas kernels  4.6 us (7%)
  other arithmetic  2.36 us (4%)
  local copies, waits for them, and re-layouts  2.07 us (3%)
  matrix products  0.84 us (1%)
  between operations  0.8 us (1%)
    all_to_all x1, starting transfers between devices, per_device(): gathered = jnp.sum(lax.all_to_all(payload, 'dp', 0, 0, tiled=True), axis=0)  16.6 us
    all_to_all x1, waiting for transfers between devices, per_device(): gathered = jnp.sum(lax.all_to_all(payload, 'dp', 0, 0, tiled=True), axis=0)  14.8 us
    all_to_all x1, waiting for transfers between devices, per_device(): mine = jnp.sum(lax.all_to_all(chunks, 'tensor', 0, 0, tiled=True), axis=0)  8.45 us
    all_to_all x1, waiting for transfers between devices, per_device(): rows = jnp.sum(lax.all_to_all(stacked, 'tensor', 0, 0, tiled=True), axis=0)  5.52 us
    pallas_call x1, Pallas kernels, project_both(): pl.pallas_call(_project_kernel, grid=(tokens // tile,), in_specs=[pl.Bloc...  4.6 us
    all_to_all x1, starting transfers between devices, per_device(): mine = jnp.sum(lax.all_to_all(chunks, 'tensor', 0, 0, tiled=True), axis=0)  4.28 us
    all_to_all x1, starting transfers between devices, per_device(): rows = jnp.sum(lax.all_to_all(stacked, 'tensor', 0, 0, tiled=True), axis=0)  3.36 us
  transfers between devices with their start and end apart: 3, of which 3 were waited for; matrix products, arithmetic and copies ran while one was open for 2% of the time, Pallas kernels for 0%

profile of v12, /device:TPU:8, one launch (start us, length us, event | category | flops | bytes accessed | tf_op | source)
XLA Modules:
  0.0 63.6 jit_solution(14697568162241756578)
XLA Ops:
  0.6 0.0 copy-start
  0.6 0.0 copy-start.3
  0.7 0.0 copy-start.4
  0.7 0.0 copy-start.2
  0.7 0.0 copy-start.1
  0.7 4.6 %shard_map.104 = f32[768,128]{1,0:T(8,128)} custom-call(bf16[768,1792]{1,0:T(8,128)(2,1)} %bitcast.25, bf16[768,512]{1,0:T(8,128)(2,1)} %bitcast.27, bf16[64,1792]{1,0:T(8,128)(2,1)} %proj_in_ref.1, bf16[64,512]{1,0:T(8,128)(2,1)} %proj_out_ref.1), custom_call_target="tpu_custom_call" | custom-call | tf_op jit(solution)/shard_map/pallas_call | solution.py:24
  5.3 4.3 %all-to-all-start = ((f32[8,96,128]{2,1,0:T(8,128)}), f32[8,96,128]{2,1,0:T(8,128)S(1)}, u32[]{:S(2)}, u32[]{:S(2)}) async-start(f32[8,96,128]{2,1,0:T(8,128)} %bitcast.26), calls=%async_computation | async-start | bytes 786432 | tf_op jit(solution)/shard_map/all_to_all | solution.py:49
  9.6 0.0 copy-done.3
  9.6 0.2 convert_reduce_fusion
  9.8 0.0 copy-done.4
  9.8 0.2 select_reduce_fusion.1
  10.0 0.0 copy-done.2
  10.0 0.1 fusion.8
  10.1 8.5 %all-to-all-done = f32[8,96,128]{2,1,0:T(8,128)S(1)} async-done(((f32[8,96,128]{2,1,0:T(8,128)}), f32[8,96,128]{2,1,0:T(8,128)S(1)}, u32[]{:S(2)}, u32[]{:S(2)}) %all-to-all-start) | async-done | bytes 393248 | tf_op jit(solution)/shard_map/all_to_all | solution.py:49
  18.5 0.1 slice.24
  18.6 0.1 copy.28
  18.7 0.3 convolution_bitcast_fusion.1
  19.0 0.0 copy-done
  19.0 0.3 convolution_bitcast_fusion
  19.3 0.0 copy-done.1
  19.3 0.3 fusion.4
  19.6 0.7 %copy_bitcast_fusion = f32[8,3,8,128]{3,2,1,0:T(8,128)} fusion(f32[3,64,64]{2,1,0:T(8,128)S(1)} %fusion.4, f32[3,64,64]{2,1,0:T(8,128)S(1)} %convolution_bitcast_fusion.1), kind=kLoop, calls=%fused_computation.6 | loop fusion | flops 24576 | bytes 196608 | tf_op jit(solution)/shard_map/transpose | solution.py:61
  20.3 3.4 %all-to-all-start.1 = ((f32[8,3,8,128]{3,2,1,0:T(8,128)}), f32[8,3,8,128]{3,2,1,0:T(8,128)S(1)}, u32[]{:S(2)}, u32[]{:S(2)}) async-start(f32[8,3,8,128]{3,2,1,0:T(8,128)} %copy_bitcast_fusion), calls=%async_computation.1 | async-start | bytes 196608 | tf_op jit(solution)/shard_map/all_to_all | solution.py:62
  23.7 0.1 convert_reduce_fusion.1
  23.7 0.1 copy.33
  23.9 5.5 %all-to-all-done.1 = f32[8,3,8,128]{3,2,1,0:T(8,128)S(1)} async-done(((f32[8,3,8,128]{3,2,1,0:T(8,128)}), f32[8,3,8,128]{3,2,1,0:T(8,128)S(1)}, u32[]{:S(2)}, u32[]{:S(2)}) %all-to-all-start.1) | async-done | bytes 98336 | tf_op jit(solution)/shard_map/all_to_all | solution.py:62
  29.4 0.1 fusion.10
  29.5 0.1 broadcast_in_dim.18
  29.5 0.1 select_reduce_fusion
  29.7 1.0 %copy.34 = f32[64,2,640]{2,1,0:T(2,128)} copy(f32[64,2,640]{2,0,1:T(8,128)S(1)} %select_maximum_fusion) | data formatting | bytes 655360 | tf_op jit(solution)/shard_map/concatenate | solution.py:80
  30.7 16.6 %all-to-all-start.2 = ((f32[64,2,640]{2,1,0:T(2,128)}), f32[64,2,640]{2,1,0:T(2,128)S(1)}, u32[]{:S(2)}, u32[]{:S(2)}) async-start(f32[64,2,640]{2,1,0:T(2,128)} %copy.34), calls=%async_computation.2 | async-start | bytes 655360 | tf_op jit(solution)/shard_map/all_to_all | solution.py:84
  47.3 0.7 %reshape.122 = f32[3,512]{1,0:T(4,128)} reshape(f32[3,8,64]{2,1,0:T(8,128)S(1)} %get-tuple-element.5) | data formatting | bytes 12288 | tf_op jit(solution)/shard_map/reshape | solution.py:63
  47.9 14.8 %all-to-all-done.2 = f32[64,2,640]{2,1,0:T(2,128)S(1)} async-done(((f32[64,2,640]{2,1,0:T(2,128)}), f32[64,2,640]{2,1,0:T(2,128)S(1)}, u32[]{:S(2)}, u32[]{:S(2)}) %all-to-all-start.2) | async-done | bytes 327712 | tf_op jit(solution)/shard_map/all_to_all | solution.py:84
  62.7 0.1 reduce_sum.69
  62.8 0.1 fusion.9
  63.0 0.7 %slice_divide_fusion = f32[2,512]{1,0:T(2,128)} fusion(f32[2,640]{1,0:T(2,128)S(1)} %reduce_sum.69, f32[2]{0:T(128)S(1)} %fusion.9), kind=kLoop, calls=%fused_computation.17 | loop fusion | flops 1024 | bytes 8200 | tf_op jit(solution)/shard_map/div | solution.py:86
  (6 shorter events, 0.1 us)
Async XLA Ops:
  0.6 18.4 %copy-start = (f32[64,64]{1,0:T(8,128)S(1)}, f32[64,64]{1,0:T(8,128)}, u32[]{:S(2)}) copy-start(f32[64,64]{1,0:T(8,128)} %param.13) | copy-start | bytes 49156
  0.6 8.9 %copy-start.3 = (s32[100]{0:T(128)S(1)}, s32[100]{0:T(128)}, u32[]{:S(2)}) copy-start(s32[100]{0:T(128)} %param.17) | copy-start | bytes 1204
  0.7 9.1 %copy-start.4 = (s32[3]{0:T(128)S(1)}, s32[3]{0:T(128)}, u32[]{:S(2)}) copy-start(s32[3]{0:T(128)} %param.16) | copy-start | bytes 40
  0.7 9.3 %copy-start.2 = (s32[3]{0:T(128)S(1)}, s32[3]{0:T(128)}, u32[]{:S(2)}) copy-start(s32[3]{0:T(128)} %param.15) | copy-start | bytes 40
  0.7 18.6 %copy-start.1 = (f32[64,64]{1,0:T(8,128)S(1)}, f32[64,64]{1,0:T(8,128)}, u32[]{:S(2)}) copy-start(f32[64,64]{1,0:T(8,128)} %param.14) | copy-start | bytes 49156
  5.3 13.2 %all-to-all-start = ((f32[8,96,128]{2,1,0:T(8,128)}), f32[8,96,128]{2,1,0:T(8,128)S(1)}, u32[]{:S(2)}, u32[]{:S(2)}) async-start(f32[8,96,128]{2,1,0:T(8,128)} %bitcast.26), calls=%async_computation | async-start | bytes 786432 | tf_op jit(solution)/shard_map/all_to_all | solution.py:49
  20.3 9.1 %all-to-all-start.1 = ((f32[8,3,8,128]{3,2,1,0:T(8,128)}), f32[8,3,8,128]{3,2,1,0:T(8,128)S(1)}, u32[]{:S(2)}, u32[]{:S(2)}) async-start(f32[8,3,8,128]{3,2,1,0:T(8,128)} %copy_bitcast_fusion), calls=%async_computation.1 | async-start | bytes 196608 | tf_op jit(solution)/shard_map/all_to_all | solution.py:62
  30.7 32.0 %all-to-all-start.2 = ((f32[64,2,640]{2,1,0:T(2,128)}), f32[64,2,640]{2,1,0:T(2,128)S(1)}, u32[]{:S(2)}, u32[]{:S(2)}) async-start(f32[64,2,640]{2,1,0:T(2,128)} %copy.34), calls=%async_computation.2 | async-start | bytes 655360 | tf_op jit(solution)/shard_map/all_to_all | solution.py:84

commit v13 on v11

--- a/solution.py
+++ b/solution.py
@@ -52,16 +52,18 @@
     token_pos = token_at % seq_length
     seq_index = jnp.arange(seq_count, dtype=jnp.int32)
     weight = (token_seq[None, :] == seq_index[:, None]) & (token_pos[None, :] < lengths[:, None])
-    right_seq = mine[None, :, proj_rank:] * weight.astype(jnp.float32)[:, :, None]
+    upper = (jnp.arange(2 * proj_rank, dtype=jnp.int32) >= proj_rank).astype(jnp.float32)
+    right_seq = mine[None, :, :] * (weight.astype(jnp.float32)[:, :, None] * upper[None, None, :])
     grads_part = jnp.einsum("ti,stj->sij", mine[:, :proj_rank], right_seq, precision=high)
     left_done = jnp.einsum("ik,skj->sij", left_inv, grads_part, precision=high)
-    pre_part = jnp.einsum("sik,kj->sij", left_done, right_inv, precision=high)
-    stacked = jnp.concatenate([grads_part, pre_part], axis=2)
-    stacked = stacked.reshape(seq_count, tensor_size, row_width, 2 * proj_rank)
+    to_lower = jnp.zeros((2 * proj_rank, 2 * proj_rank), jnp.float32)
+    to_lower = to_lower.at[proj_rank:, :proj_rank].set(right_inv)
+    pre_part = jnp.einsum("sik,kj->sij", left_done, to_lower, precision=high)
+    stacked = (grads_part + pre_part).reshape(seq_count, tensor_size, row_width, 2 * proj_rank)
     stacked = stacked.transpose(1, 0, 2, 3)
     rows = jnp.sum(lax.all_to_all(stacked, "tensor", 0, 0, tiled=True), axis=0)
-    grad_flat = rows[:, :, :proj_rank].reshape(seq_count, row_width * proj_rank)
-    pre_flat = rows[:, :, proj_rank:].reshape(seq_count, row_width * proj_rank)
+    grad_flat = rows[:, :, proj_rank:].reshape(seq_count, row_width * proj_rank)
+    pre_flat = rows[:, :, :proj_rank].reshape(seq_count, row_width * proj_rank)
     lang_total = owner.shape[0]
     dp_size = lax.axis_size("dp")
     slot_count = (lang_total + dp_size - 1) // dp_size

time: 63 us -> 62.5 us (level)
  other arithmetic: 2.36 us -> 1.65 us
    transpose x1 -> x0, other arithmetic: 0.72 us -> none  [per_device(): stacked = stacked.transpose(1, 0, 2, 3)]
    reshape x1 -> x2, local copies, waits for them, and re-layouts: 0.68 us -> 1.31 us  [the longest x1 0.68 us: per_device(): grad_flat = rows[:, :, proj_rank:].reshape(seq_count, row_width * proj_rank)]
where the time goes in v13:
time: 62.5 us; the launch traced here: 62.2 us
  waiting for transfers between devices  28.7 us (46%)
  starting transfers between devices  24.3 us (39%)
  Pallas kernels  3.54 us (6%)
  local copies, waits for them, and re-layouts  2.55 us (4%)
  other arithmetic  1.65 us (3%)
  between operations  0.8 us (1%)
  matrix products  0.66 us (1%)
    all_to_all x1, starting transfers between devices, per_device(): gathered = jnp.sum(lax.all_to_all(payload, 'dp', 0, 0, tiled=True), axis=0)  16.6 us
    all_to_all x1, waiting for transfers between devices, per_device(): gathered = jnp.sum(lax.all_to_all(payload, 'dp', 0, 0, tiled=True), axis=0)  14.8 us
    all_to_all x1, waiting for transfers between devices, per_device(): mine = jnp.sum(lax.all_to_all(chunks, 'tensor', 0, 0, tiled=True), axis=0)  8.44 us
    all_to_all x1, waiting for transfers between devices, per_device(): rows = jnp.sum(lax.all_to_all(stacked, 'tensor', 0, 0, tiled=True), axis=0)  5.52 us
    all_to_all x1, starting transfers between devices, per_device(): mine = jnp.sum(lax.all_to_all(chunks, 'tensor', 0, 0, tiled=True), axis=0)  4.3 us
    pallas_call x1, Pallas kernels, project_both(): pl.pallas_call(_project_kernel, grid=(tokens // tile,), in_specs=[pl.Bloc...  3.54 us
    all_to_all x1, starting transfers between devices, per_device(): rows = jnp.sum(lax.all_to_all(stacked, 'tensor', 0, 0, tiled=True), axis=0)  3.36 us
  transfers between devices with their start and end apart: 3, of which 3 were waited for; matrix products, arithmetic and copies ran while one was open for 2% of the time, Pallas kernels for 0%

profile of v13, /device:TPU:8, one launch (start us, length us, event | category | flops | bytes accessed | tf_op | source)
XLA Modules:
  0.0 62.2 jit_solution(16686401805137325889)
XLA Ops:
  0.6 0.0 copy-start
  0.6 0.0 copy-start.3
  0.7 0.0 copy-start.4
  0.7 0.0 copy-start.2
  0.7 0.0 copy-start.1
  0.7 3.5 %shard_map.104 = f32[768,128]{1,0:T(8,128)} custom-call(bf16[768,1792]{1,0:T(8,128)(2,1)} %bitcast.25, bf16[768,512]{1,0:T(8,128)(2,1)} %bitcast.27, bf16[64,1792]{1,0:T(8,128)(2,1)} %proj_in_ref.1, bf16[64,512]{1,0:T(8,128)(2,1)} %proj_out_ref.1), custom_call_target="tpu_custom_call" | custom-call | tf_op jit(solution)/shard_map/pallas_call | solution.py:24
  4.2 4.3 %all-to-all-start = ((f32[8,96,128]{2,1,0:T(8,128)}), f32[8,96,128]{2,1,0:T(8,128)S(1)}, u32[]{:S(2)}, u32[]{:S(2)}) async-start(f32[8,96,128]{2,1,0:T(8,128)} %bitcast.26), calls=%async_computation | async-start | bytes 786432 | tf_op jit(solution)/shard_map/all_to_all | solution.py:49
  8.6 0.0 copy-done.3
  8.6 0.2 convert_reduce_fusion
  8.8 0.0 copy-done.4
  8.8 0.2 select_reduce_fusion.1
  9.0 0.0 copy-done.2
  9.0 0.1 fusion.11
  9.0 8.4 %all-to-all-done = f32[8,96,128]{2,1,0:T(8,128)S(1)} async-done(((f32[8,96,128]{2,1,0:T(8,128)}), f32[8,96,128]{2,1,0:T(8,128)S(1)}, u32[]{:S(2)}, u32[]{:S(2)}) %all-to-all-start) | async-done | bytes 393248 | tf_op jit(solution)/shard_map/all_to_all | solution.py:49
  17.5 0.3 convolution_bitcast_fusion.1
  17.8 0.0 copy-done
  17.8 0.2 convolution_bitcast_fusion
  18.0 0.0 copy-done.1
  18.0 0.2 fusion
  18.2 0.6 %copy.32 = f32[3,8,8,128]{3,2,0,1:T(8,128)} copy(f32[3,8,8,128]{3,2,1,0:T(8,128)S(1)} %fusion) | data formatting | bytes 196608 | tf_op jit(solution)/shard_map/reshape | solution.py:62
  18.8 3.4 %all-to-all-start.1 = ((f32[8,3,8,128]{3,2,1,0:T(8,128)}), f32[8,3,8,128]{3,2,1,0:T(8,128)S(1)}, u32[]{:S(2)}, u32[]{:S(2)}) async-start(f32[8,3,8,128]{3,2,1,0:T(8,128)} %bitcast.24), calls=%async_computation.1 | async-start | bytes 196608 | tf_op jit(solution)/shard_map/all_to_all | solution.py:64
  22.2 0.1 convert_reduce_fusion.1
  22.3 0.1 copy.24
  22.4 5.5 %all-to-all-done.1 = f32[8,3,8,128]{3,2,1,0:T(8,128)S(1)} async-done(((f32[8,3,8,128]{3,2,1,0:T(8,128)}), f32[8,3,8,128]{3,2,1,0:T(8,128)S(1)}, u32[]{:S(2)}, u32[]{:S(2)}) %all-to-all-start.1) | async-done | bytes 98336 | tf_op jit(solution)/shard_map/all_to_all | solution.py:64
  27.9 0.1 fusion.14
  28.0 0.1 broadcast_in_dim.18
  28.1 0.1 select_reduce_fusion
  28.2 1.0 %copy.25 = f32[64,2,640]{2,1,0:T(2,128)} copy(f32[64,2,640]{2,0,1:T(8,128)S(1)} %select_maximum_fusion) | data formatting | bytes 655360 | tf_op jit(solution)/shard_map/concatenate | solution.py:82
  29.2 16.6 %all-to-all-start.2 = ((f32[64,2,640]{2,1,0:T(2,128)}), f32[64,2,640]{2,1,0:T(2,128)S(1)}, u32[]{:S(2)}, u32[]{:S(2)}) async-start(f32[64,2,640]{2,1,0:T(2,128)} %copy.25), calls=%async_computation.2 | async-start | bytes 655360 | tf_op jit(solution)/shard_map/all_to_all | solution.py:86
  45.8 0.7 %reshape.160 = f32[3,512]{1,0:T(4,128)} reshape(f32[3,8,64]{2,1,0:T(8,128)S(1)} %get-tuple-element.17) | data formatting | bytes 12288 | tf_op jit(solution)/shard_map/reshape | solution.py:65
  46.5 14.8 %all-to-all-done.2 = f32[64,2,640]{2,1,0:T(2,128)S(1)} async-done(((f32[64,2,640]{2,1,0:T(2,128)}), f32[64,2,640]{2,1,0:T(2,128)S(1)}, u32[]{:S(2)}, u32[]{:S(2)}) %all-to-all-start.2) | async-done | bytes 327712 | tf_op jit(solution)/shard_map/all_to_all | solution.py:86
  61.3 0.1 reduce_sum.69
  61.4 0.1 fusion.12
  61.5 0.7 %slice_divide_fusion = f32[2,512]{1,0:T(2,128)} fusion(f32[2,640]{1,0:T(2,128)S(1)} %reduce_sum.69, f32[2]{0:T(128)S(1)} %fusion.12), kind=kLoop, calls=%fused_computation.20 | loop fusion | flops 1024 | bytes 8200 | tf_op jit(solution)/shard_map/div | solution.py:88
  (7 shorter events, 0.1 us)
Async XLA Ops:
  0.6 17.2 %copy-start = (f32[64,64]{1,0:T(8,128)S(1)}, f32[64,64]{1,0:T(8,128)}, u32[]{:S(2)}) copy-start(f32[64,64]{1,0:T(8,128)} %param.15) | copy-start | bytes 49156
  0.6 7.9 %copy-start.3 = (s32[100]{0:T(128)S(1)}, s32[100]{0:T(128)}, u32[]{:S(2)}) copy-start(s32[100]{0:T(128)} %param.19) | copy-start | bytes 1204
  0.7 8.1 %copy-start.4 = (s32[3]{0:T(128)S(1)}, s32[3]{0:T(128)}, u32[]{:S(2)}) copy-start(s32[3]{0:T(128)} %param.18) | copy-start | bytes 40
  0.7 8.3 %copy-start.2 = (s32[3]{0:T(128)S(1)}, s32[3]{0:T(128)}, u32[]{:S(2)}) copy-start(s32[3]{0:T(128)} %param.17) | copy-start | bytes 40
  0.7 17.3 %copy-start.1 = (f32[64,64]{1,0:T(8,128)S(1)}, f32[64,64]{1,0:T(8,128)}, u32[]{:S(2)}) copy-start(f32[64,64]{1,0:T(8,128)} %param.16) | copy-start | bytes 49156
  4.2 13.2 %all-to-all-start = ((f32[8,96,128]{2,1,0:T(8,128)}), f32[8,96,128]{2,1,0:T(8,128)S(1)}, u32[]{:S(2)}, u32[]{:S(2)}) async-start(f32[8,96,128]{2,1,0:T(8,128)} %bitcast.26), calls=%async_computation | async-start | bytes 786432 | tf_op jit(solution)/shard_map/all_to_all | solution.py:49
  18.8 9.1 %all-to-all-start.1 = ((f32[8,3,8,128]{3,2,1,0:T(8,128)}), f32[8,3,8,128]{3,2,1,0:T(8,128)S(1)}, u32[]{:S(2)}, u32[]{:S(2)}) async-start(f32[8,3,8,128]{3,2,1,0:T(8,128)} %bitcast.24), calls=%async_computation.1 | async-start | bytes 196608 | tf_op jit(solution)/shard_map/all_to_all | solution.py:64
  29.2 32.0 %all-to-all-start.2 = ((f32[64,2,640]{2,1,0:T(2,128)}), f32[64,2,640]{2,1,0:T(2,128)S(1)}, u32[]{:S(2)}, u32[]{:S(2)}) async-start(f32[64,2,640]{2,1,0:T(2,128)} %copy.25), calls=%async_computation.2 | async-start | bytes 655360 | tf_op jit(solution)/shard_map/all_to_all | solution.py:86

commit v14 on v13

--- a/solution.py
+++ b/solution.py
@@ -52,16 +52,21 @@
     token_pos = token_at % seq_length
     seq_index = jnp.arange(seq_count, dtype=jnp.int32)
     weight = (token_seq[None, :] == seq_index[:, None]) & (token_pos[None, :] < lengths[:, None])
-    upper = (jnp.arange(2 * proj_rank, dtype=jnp.int32) >= proj_rank).astype(jnp.float32)
-    right_seq = mine[None, :, :] * (weight.astype(jnp.float32)[:, :, None] * upper[None, None, :])
-    grads_part = jnp.einsum("ti,stj->sij", mine[:, :proj_rank], right_seq, precision=high)
-    left_done = jnp.einsum("ik,skj->sij", left_inv, grads_part, precision=high)
-    to_lower = jnp.zeros((2 * proj_rank, 2 * proj_rank), jnp.float32)
+    double = 2 * proj_rank
+    upper = (jnp.arange(double, dtype=jnp.int32) >= proj_rank).astype(jnp.float32)
+    right_seq = mine[:, None, :] * (weight.T.astype(jnp.float32)[:, :, None] * upper[None, None, :])
+    right_seq = right_seq.reshape(block, seq_count * double)
+    grads_part = lax.dot_general(
+        mine[:, :proj_rank], right_seq, (((0,), (0,)), ((), ())), precision=high
+    )
+    left_done = jnp.dot(left_inv, grads_part, precision=high)
+    to_lower = jnp.zeros((double, double), jnp.float32)
     to_lower = to_lower.at[proj_rank:, :proj_rank].set(right_inv)
-    pre_part = jnp.einsum("sik,kj->sij", left_done, to_lower, precision=high)
-    stacked = (grads_part + pre_part).reshape(seq_count, tensor_size, row_width, 2 * proj_rank)
-    stacked = stacked.transpose(1, 0, 2, 3)
+    to_lower = jnp.kron(jnp.eye(seq_count, dtype=jnp.float32), to_lower)
+    pre_part = jnp.dot(left_done, to_lower, precision=high)
+    stacked = (grads_part + pre_part).reshape(tensor_size, row_width, seq_count * double)
     rows = jnp.sum(lax.all_to_all(stacked, "tensor", 0, 0, tiled=True), axis=0)
+    rows = rows.reshape(row_width, seq_count, double).transpose(1, 0, 2)
     grad_flat = rows[:, :, proj_rank:].reshape(seq_count, row_width * proj_rank)
     pre_flat = rows[:, :, :proj_rank].reshape(seq_count, row_width * proj_rank)
     lang_total = owner.shape[0]

time: 62.5 us -> 62.8 us (level)
  matrix products: 0.66 us -> 1.35 us
    dot_general x3, matrix products: 0.66 us -> 1.35 us  [the longest x1 0.93 us: per_device(): pre_part = jnp.dot(left_done, to_lower, precision=high)]
    reshape x1 -> x0, local copies, waits for them, and re-layouts: 0.63 us -> none  [per_device(): (grads_part + pre_part).reshape(seq_count, tensor_size, row_width, 2 * pr...]
  transfers between devices with their start and end apart: 3 -> 3, of which waited for: 3 -> 3; matrix products, arithmetic and copies ran while one was open for 2% -> 3% of each run, Pallas kernels for 0% -> 0%
where the time goes in v14:
time: 62.8 us; the launch traced here: 62.4 us
  waiting for transfers between devices  28.4 us (45%)
  starting transfers between devices  24.3 us (39%)
  Pallas kernels  3.54 us (6%)
  local copies, waits for them, and re-layouts  2.23 us (4%)
  other arithmetic  1.82 us (3%)
  matrix products  1.35 us (2%)
  between operations  0.83 us (1%)
    all_to_all x1, starting transfers between devices, per_device(): gathered = jnp.sum(lax.all_to_all(payload, 'dp', 0, 0, tiled=True), axis=0)  16.6 us
    all_to_all x1, waiting for transfers between devices, per_device(): gathered = jnp.sum(lax.all_to_all(payload, 'dp', 0, 0, tiled=True), axis=0)  14.8 us
    all_to_all x1, waiting for transfers between devices, per_device(): mine = jnp.sum(lax.all_to_all(chunks, 'tensor', 0, 0, tiled=True), axis=0)  8.11 us
    all_to_all x1, waiting for transfers between devices, per_device(): rows = jnp.sum(lax.all_to_all(stacked, 'tensor', 0, 0, tiled=True), axis=0)  5.52 us
    all_to_all x1, starting transfers between devices, per_device(): mine = jnp.sum(lax.all_to_all(chunks, 'tensor', 0, 0, tiled=True), axis=0)  4.3 us
    pallas_call x1, Pallas kernels, project_both(): pl.pallas_call(_project_kernel, grid=(tokens // tile,), in_specs=[pl.Bloc...  3.54 us
    all_to_all x1, starting transfers between devices, per_device(): rows = jnp.sum(lax.all_to_all(stacked, 'tensor', 0, 0, tiled=True), axis=0)  3.36 us
  transfers between devices with their start and end apart: 3, of which 3 were waited for; matrix products, arithmetic and copies ran while one was open for 3% of the time, Pallas kernels for 0%

profile of v14, /device:TPU:8, one launch (start us, length us, event | category | flops | bytes accessed | tf_op | source)
XLA Modules:
  0.0 62.4 jit_solution(14088928180943869035)
XLA Ops:
  0.6 0.0 copy-start
  0.6 0.0 copy-start.2
  0.7 0.0 copy-start.3
  0.7 0.0 copy-start.1
  0.7 0.0 copy-start.4
  0.7 3.5 %shard_map.104 = f32[768,128]{1,0:T(8,128)} custom-call(bf16[768,1792]{1,0:T(8,128)(2,1)} %bitcast.31, bf16[768,512]{1,0:T(8,128)(2,1)} %bitcast.34, bf16[64,1792]{1,0:T(8,128)(2,1)} %proj_in_ref.1, bf16[64,512]{1,0:T(8,128)(2,1)} %proj_out_ref.1), custom_call_target="tpu_custom_call" | custom-call | tf_op jit(solution)/shard_map/pallas_call | solution.py:24
  4.2 4.3 %all-to-all-start = ((f32[8,96,128]{2,1,0:T(8,128)}), f32[8,96,128]{2,1,0:T(8,128)S(1)}, u32[]{:S(2)}, u32[]{:S(2)}) async-start(f32[8,96,128]{2,1,0:T(8,128)} %bitcast.33), calls=%async_computation | async-start | bytes 786432 | tf_op jit(solution)/shard_map/all_to_all | solution.py:49
  8.6 0.0 copy-done.2
  8.6 0.1 fusion.13
  8.7 0.1 copy.18
  8.8 0.0 copy-done.3
  8.8 0.2 convert_reduce_fusion
  9.0 0.0 copy-done.1
  9.0 0.0 copy-done.4
  9.0 0.2 select_reduce_fusion.1
  9.2 0.2 broadcast_multiply_fusion
  9.4 8.1 %all-to-all-done = f32[8,96,128]{2,1,0:T(8,128)S(1)} async-done(((f32[8,96,128]{2,1,0:T(8,128)}), f32[8,96,128]{2,1,0:T(8,128)S(1)}, u32[]{:S(2)}, u32[]{:S(2)}) %all-to-all-start) | async-done | bytes 393248 | tf_op jit(solution)/shard_map/all_to_all | solution.py:49
  17.5 0.2 mul.75
  17.7 0.2 fusion.4
  18.0 0.0 copy-done
  18.0 0.2 fusion.17
  18.1 0.9 %fusion = f32[8,8,384]{2,1,0:T(8,128)} fusion(f32[64,384]{1,0:T(8,128)S(1)} %fusion.4, f32[384,64]{0,1:T(8,128)S(1)} %fusion.17, f32[48,8,3,128]{3,2,1,0:T(4,128)S(1)} %bitcast.32), kind=kOutput, calls=%fused_computation.1 | convolution fusion | flops 56647680 | bytes 884736 | tf_op jit(solution)/shard_map/dot_general | solution.py:66
  19.1 3.4 %all-to-all-start.1 = ((f32[8,8,384]{2,1,0:T(8,128)}), f32[8,8,384]{2,1,0:T(8,128)S(1)}, u32[]{:S(2)}, u32[]{:S(2)}) async-start(f32[8,8,384]{2,1,0:T(8,128)} %fusion), calls=%async_computation.1 | async-start | bytes 196608 | tf_op jit(solution)/shard_map/all_to_all | solution.py:68
  22.4 0.1 convert_reduce_fusion.1
  22.5 0.1 copy.19
  22.6 5.5 %all-to-all-done.1 = f32[8,8,384]{2,1,0:T(8,128)S(1)} async-done(((f32[8,8,384]{2,1,0:T(8,128)}), f32[8,8,384]{2,1,0:T(8,128)S(1)}, u32[]{:S(2)}, u32[]{:S(2)}) %all-to-all-start.1) | async-done | bytes 98336 | tf_op jit(solution)/shard_map/all_to_all | solution.py:68
  28.2 0.1 fusion.16
  28.3 0.1 broadcast_in_dim.22
  28.3 0.1 select_reduce_fusion
  28.5 1.0 %copy.20 = f32[64,2,640]{2,1,0:T(2,128)} copy(f32[64,2,640]{2,0,1:T(8,128)S(1)} %select_maximum_fusion) | data formatting | bytes 655360 | tf_op jit(solution)/shard_map/concatenate | solution.py:87
  29.5 16.6 %all-to-all-start.2 = ((f32[64,2,640]{2,1,0:T(2,128)}), f32[64,2,640]{2,1,0:T(2,128)S(1)}, u32[]{:S(2)}, u32[]{:S(2)}) async-start(f32[64,2,640]{2,1,0:T(2,128)} %copy.20), calls=%async_computation.2 | async-start | bytes 655360 | tf_op jit(solution)/shard_map/all_to_all | solution.py:91
  46.1 0.7 %reshape.186 = f32[3,512]{1,0:T(4,128)} reshape(f32[3,8,64]{2,1,0:T(8,128)S(1)} %get-tuple-element.17) | data formatting | bytes 12288 | tf_op jit(solution)/shard_map/reshape | solution.py:70
  46.7 14.8 %all-to-all-done.2 = f32[64,2,640]{2,1,0:T(2,128)S(1)} async-done(((f32[64,2,640]{2,1,0:T(2,128)}), f32[64,2,640]{2,1,0:T(2,128)S(1)}, u32[]{:S(2)}, u32[]{:S(2)}) %all-to-all-start.2) | async-done | bytes 327712 | tf_op jit(solution)/shard_map/all_to_all | solution.py:91
  61.5 0.1 reduce_sum.69
  61.6 0.1 fusion.15
  61.8 0.7 %slice_divide_fusion = f32[2,512]{1,0:T(2,128)} fusion(f32[2,640]{1,0:T(2,128)S(1)} %reduce_sum.69, f32[2]{0:T(128)S(1)} %fusion.15), kind=kLoop, calls=%fused_computation.19 | loop fusion | flops 1024 | bytes 8200 | tf_op jit(solution)/shard_map/div | solution.py:93
  (11 shorter events, 0.1 us)
Async XLA Ops:
  0.6 17.3 %copy-start = (f32[64,64]{1,0:T(8,128)S(1)}, f32[64,64]{1,0:T(8,128)}, u32[]{:S(2)}) copy-start(f32[64,64]{1,0:T(8,128)} %param.15) | copy-start | bytes 49156
  0.6 7.9 %copy-start.2 = (s32[3]{0:T(128)S(1)}, s32[3]{0:T(128)}, u32[]{:S(2)}) copy-start(s32[3]{0:T(128)} %param.17) | copy-start | bytes 40
  0.7 8.1 %copy-start.3 = (s32[100]{0:T(128)S(1)}, s32[100]{0:T(128)}, u32[]{:S(2)}) copy-start(s32[100]{0:T(128)} %param.19) | copy-start | bytes 1204
  0.7 8.3 %copy-start.1 = (f32[64,64]{1,0:T(8,128)S(1)}, f32[64,64]{1,0:T(8,128)}, u32[]{:S(2)}) copy-start(f32[64,64]{1,0:T(8,128)} %param.16) | copy-start | bytes 49156
  0.7 8.3 %copy-start.4 = (s32[3]{0:T(128)S(1)}, s32[3]{0:T(128)}, u32[]{:S(2)}) copy-start(s32[3]{0:T(128)} %param.18) | copy-start | bytes 40
  4.2 13.2 %all-to-all-start = ((f32[8,96,128]{2,1,0:T(8,128)}), f32[8,96,128]{2,1,0:T(8,128)S(1)}, u32[]{:S(2)}, u32[]{:S(2)}) async-start(f32[8,96,128]{2,1,0:T(8,128)} %bitcast.33), calls=%async_computation | async-start | bytes 786432 | tf_op jit(solution)/shard_map/all_to_all | solution.py:49
  19.1 9.1 %all-to-all-start.1 = ((f32[8,8,384]{2,1,0:T(8,128)}), f32[8,8,384]{2,1,0:T(8,128)S(1)}, u32[]{:S(2)}, u32[]{:S(2)}) async-start(f32[8,8,384]{2,1,0:T(8,128)} %fusion), calls=%async_computation.1 | async-start | bytes 196608 | tf_op jit(solution)/shard_map/all_to_all | solution.py:68
  29.5 32.0 %all-to-all-start.2 = ((f32[64,2,640]{2,1,0:T(2,128)}), f32[64,2,640]{2,1,0:T(2,128)S(1)}, u32[]{:S(2)}, u32[]{:S(2)}) async-start(f32[64,2,640]{2,1,0:T(2,128)} %copy.20), calls=%async_computation.2 | async-start | bytes 655360 | tf_op jit(solution)/shard_map/all_to_all | solution.py:91

commit v15 on v14

--- a/solution.py
+++ b/solution.py
@@ -53,18 +53,17 @@
     seq_index = jnp.arange(seq_count, dtype=jnp.int32)
     weight = (token_seq[None, :] == seq_index[:, None]) & (token_pos[None, :] < lengths[:, None])
     double = 2 * proj_rank
-    upper = (jnp.arange(double, dtype=jnp.int32) >= proj_rank).astype(jnp.float32)
-    right_seq = mine[:, None, :] * (weight.T.astype(jnp.float32)[:, :, None] * upper[None, None, :])
+    right_blk = mine[:, proj_rank:]
+    right_both = jnp.concatenate([jnp.dot(right_blk, right_inv, precision=high), right_blk], axis=1)
+    right_seq = right_both[:, None, :] * weight.T.astype(jnp.float32)[:, :, None]
     right_seq = right_seq.reshape(block, seq_count * double)
     grads_part = lax.dot_general(
         mine[:, :proj_rank], right_seq, (((0,), (0,)), ((), ())), precision=high
     )
     left_done = jnp.dot(left_inv, grads_part, precision=high)
-    to_lower = jnp.zeros((double, double), jnp.float32)
-    to_lower = to_lower.at[proj_rank:, :proj_rank].set(right_inv)
-    to_lower = jnp.kron(jnp.eye(seq_count, dtype=jnp.float32), to_lower)
-    pre_part = jnp.dot(left_done, to_lower, precision=high)
-    stacked = (grads_part + pre_part).reshape(tensor_size, row_width, seq_count * double)
+    lane = jnp.arange(seq_count * double, dtype=jnp.int32) % double
+    shares = jnp.where(lane[None, :] < proj_rank, left_done, grads_part)
+    stacked = shares.reshape(tensor_size, row_width, seq_count * double)
     rows = jnp.sum(lax.all_to_all(stacked, "tensor", 0, 0, tiled=True), axis=0)
     rows = rows.reshape(row_width, seq_count, double).transpose(1, 0, 2)
     grad_flat = rows[:, :, proj_rank:].reshape(seq_count, row_width * proj_rank)

time: 62.8 us -> 63 us (level)
    dot_general x1, matrix products: 0.93 us -> 0.25 us  [per_device(): jnp.dot(right_blk, right_inv, precision=high)]
  transfers between devices with their start and end apart: 3 -> 3, of which waited for: 3 -> 3; matrix products, arithmetic and copies ran while one was open for 3% -> 2% of each run, Pallas kernels for 0% -> 0%
where the time goes in v15:
time: 63 us; the launch traced here: 62.6 us
  waiting for transfers between devices  28.6 us (45%)
  starting transfers between devices  24.3 us (39%)
  Pallas kernels  3.54 us (6%)
  local copies, waits for them, and re-layouts  2.26 us (4%)
  other arithmetic  1.83 us (3%)
  matrix products  1.29 us (2%)
  between operations  0.82 us (1%)
    all_to_all x1, starting transfers between devices, per_device(): gathered = jnp.sum(lax.all_to_all(payload, 'dp', 0, 0, tiled=True), axis=0)  16.6 us
    all_to_all x1, waiting for transfers between devices, per_device(): gathered = jnp.sum(lax.all_to_all(payload, 'dp', 0, 0, tiled=True), axis=0)  14.8 us
    all_to_all x1, waiting for transfers between devices, per_device(): mine = jnp.sum(lax.all_to_all(chunks, 'tensor', 0, 0, tiled=True), axis=0)  8.34 us
    all_to_all x1, waiting for transfers between devices, per_device(): rows = jnp.sum(lax.all_to_all(stacked, 'tensor', 0, 0, tiled=True), axis=0)  5.52 us
    all_to_all x1, starting transfers between devices, per_device(): mine = jnp.sum(lax.all_to_all(chunks, 'tensor', 0, 0, tiled=True), axis=0)  4.3 us
    pallas_call x1, Pallas kernels, project_both(): pl.pallas_call(_project_kernel, grid=(tokens // tile,), in_specs=[pl.Bloc...  3.54 us
    all_to_all x1, starting transfers between devices, per_device(): rows = jnp.sum(lax.all_to_all(stacked, 'tensor', 0, 0, tiled=True), axis=0)  3.36 us
  transfers between devices with their start and end apart: 3, of which 3 were waited for; matrix products, arithmetic and copies ran while one was open for 2% of the time, Pallas kernels for 0%

profile of v15, /device:TPU:8, one launch (start us, length us, event | category | flops | bytes accessed | tf_op | source)
XLA Modules:
  0.0 62.6 jit_solution(16353801688135928029)
XLA Ops:
  0.6 0.0 copy-start
  0.6 0.0 copy-start.3
  0.7 0.0 copy-start.2
  0.7 0.0 copy-start.4
  0.7 0.0 copy-start.1
  0.7 3.5 %shard_map.104 = f32[768,128]{1,0:T(8,128)} custom-call(bf16[768,1792]{1,0:T(8,128)(2,1)} %bitcast.22, bf16[768,512]{1,0:T(8,128)(2,1)} %bitcast.24, bf16[64,1792]{1,0:T(8,128)(2,1)} %proj_in_ref.1, bf16[64,512]{1,0:T(8,128)(2,1)} %proj_out_ref.1), custom_call_target="tpu_custom_call" | custom-call | tf_op jit(solution)/shard_map/pallas_call | solution.py:24
  4.2 4.3 %all-to-all-start = ((f32[8,96,128]{2,1,0:T(8,128)}), f32[8,96,128]{2,1,0:T(8,128)S(1)}, u32[]{:S(2)}, u32[]{:S(2)}) async-start(f32[8,96,128]{2,1,0:T(8,128)} %bitcast.23), calls=%async_computation | async-start | bytes 786432 | tf_op jit(solution)/shard_map/all_to_all | solution.py:49
  8.6 0.0 copy-done.3
  8.6 0.2 convert_reduce_fusion
  8.7 0.0 copy-done.2
  8.8 0.1 fusion.12
  8.8 0.1 copy.31
  8.9 0.0 copy-done.4
  9.0 0.2 select_reduce_fusion.1
  9.1 8.3 %all-to-all-done = f32[8,96,128]{2,1,0:T(8,128)S(1)} async-done(((f32[8,96,128]{2,1,0:T(8,128)}), f32[8,96,128]{2,1,0:T(8,128)S(1)}, u32[]{:S(2)}, u32[]{:S(2)}) %all-to-all-start) | async-done | bytes 393248 | tf_op jit(solution)/shard_map/all_to_all | solution.py:49
  17.5 0.1 slice.25
  17.6 0.1 copy.36
  17.7 0.0 copy-done.1
  17.7 0.2 fusion.14
  17.9 0.1 copy.30
  18.0 0.2 broadcast_multiply_fusion
  18.2 0.2 fusion.2
  18.5 0.0 copy-done
  18.5 0.8 %fusion.1 = f32[8,8,384]{2,1,0:T(8,128)} fusion(f32[64,384]{1,0:T(8,128)S(1)} %fusion.2, f32[64,64]{1,0:T(8,128)S(1)} %copy-done, pred[384]{0:T(512)(128)(4,1)S(1)} %fusion.7), kind=kOutput, calls=%fused_computation.2 | convolution fusion | flops 9461760 | bytes 213376 | tf_op jit(solution)/shard_map/dot_general | solution.py:63
  19.3 3.4 %all-to-all-start.1 = ((f32[8,8,384]{2,1,0:T(8,128)}), f32[8,8,384]{2,1,0:T(8,128)S(1)}, u32[]{:S(2)}, u32[]{:S(2)}) async-start(f32[8,8,384]{2,1,0:T(8,128)} %fusion.1), calls=%async_computation.1 | async-start | bytes 196608 | tf_op jit(solution)/shard_map/all_to_all | solution.py:67
  22.6 0.1 convert_reduce_fusion.1
  22.7 0.1 copy.32
  22.8 5.5 %all-to-all-done.1 = f32[8,8,384]{2,1,0:T(8,128)S(1)} async-done(((f32[8,8,384]{2,1,0:T(8,128)}), f32[8,8,384]{2,1,0:T(8,128)S(1)}, u32[]{:S(2)}, u32[]{:S(2)}) %all-to-all-start.1) | async-done | bytes 98336 | tf_op jit(solution)/shard_map/all_to_all | solution.py:67
  28.4 0.1 fusion.16
  28.4 0.1 broadcast_in_dim.27
  28.5 0.1 select_reduce_fusion
  28.7 1.0 %copy.33 = f32[64,2,640]{2,1,0:T(2,128)} copy(f32[64,2,640]{2,0,1:T(8,128)S(1)} %select_maximum_fusion) | data formatting | bytes 655360 | tf_op jit(solution)/shard_map/concatenate | solution.py:86
  29.7 16.6 %all-to-all-start.2 = ((f32[64,2,640]{2,1,0:T(2,128)}), f32[64,2,640]{2,1,0:T(2,128)S(1)}, u32[]{:S(2)}, u32[]{:S(2)}) async-start(f32[64,2,640]{2,1,0:T(2,128)} %copy.33), calls=%async_computation.2 | async-start | bytes 655360 | tf_op jit(solution)/shard_map/all_to_all | solution.py:90
  46.3 0.7 %reshape.140 = f32[3,512]{1,0:T(4,128)} reshape(f32[3,8,64]{2,1,0:T(8,128)S(1)} %get-tuple-element.5) | data formatting | bytes 12288 | tf_op jit(solution)/shard_map/reshape | solution.py:69
  46.9 14.8 %all-to-all-done.2 = f32[64,2,640]{2,1,0:T(2,128)S(1)} async-done(((f32[64,2,640]{2,1,0:T(2,128)}), f32[64,2,640]{2,1,0:T(2,128)S(1)}, u32[]{:S(2)}, u32[]{:S(2)}) %all-to-all-start.2) | async-done | bytes 327712 | tf_op jit(solution)/shard_map/all_to_all | solution.py:90
  61.7 0.1 reduce_sum.69
  61.8 0.1 fusion.13
  62.0 0.7 %slice_divide_fusion = f32[2,512]{1,0:T(2,128)} fusion(f32[2,640]{1,0:T(2,128)S(1)} %reduce_sum.69, f32[2]{0:T(128)S(1)} %fusion.13), kind=kLoop, calls=%fused_computation.15 | loop fusion | flops 1024 | bytes 8200 | tf_op jit(solution)/shard_map/div | solution.py:92
  (8 shorter events, 0.1 us)
Async XLA Ops:
  0.6 17.8 %copy-start = (f32[64,64]{1,0:T(8,128)S(1)}, f32[64,64]{1,0:T(8,128)}, u32[]{:S(2)}) copy-start(f32[64,64]{1,0:T(8,128)} %param.13) | copy-start | bytes 49156
  0.6 7.9 %copy-start.3 = (s32[100]{0:T(128)S(1)}, s32[100]{0:T(128)}, u32[]{:S(2)}) copy-start(s32[100]{0:T(128)} %param.17) | copy-start | bytes 1204
  0.7 8.1 %copy-start.2 = (s32[3]{0:T(128)S(1)}, s32[3]{0:T(128)}, u32[]{:S(2)}) copy-start(s32[3]{0:T(128)} %param.15) | copy-start | bytes 40
  0.7 8.3 %copy-start.4 = (s32[3]{0:T(128)S(1)}, s32[3]{0:T(128)}, u32[]{:S(2)}) copy-start(s32[3]{0:T(128)} %param.16) | copy-start | bytes 40
  0.7 17.0 %copy-start.1 = (f32[64,64]{1,0:T(8,128)S(1)}, f32[64,64]{1,0:T(8,128)}, u32[]{:S(2)}) copy-start(f32[64,64]{1,0:T(8,128)} %param.14) | copy-start | bytes 49156
  4.2 13.2 %all-to-all-start = ((f32[8,96,128]{2,1,0:T(8,128)}), f32[8,96,128]{2,1,0:T(8,128)S(1)}, u32[]{:S(2)}, u32[]{:S(2)}) async-start(f32[8,96,128]{2,1,0:T(8,128)} %bitcast.23), calls=%async_computation | async-start | bytes 786432 | tf_op jit(solution)/shard_map/all_to_all | solution.py:49
  19.3 9.1 %all-to-all-start.1 = ((f32[8,8,384]{2,1,0:T(8,128)}), f32[8,8,384]{2,1,0:T(8,128)S(1)}, u32[]{:S(2)}, u32[]{:S(2)}) async-start(f32[8,8,384]{2,1,0:T(8,128)} %fusion.1), calls=%async_computation.1 | async-start | bytes 196608 | tf_op jit(solution)/shard_map/all_to_all | solution.py:67
  29.7 32.0 %all-to-all-start.2 = ((f32[64,2,640]{2,1,0:T(2,128)}), f32[64,2,640]{2,1,0:T(2,128)S(1)}, u32[]{:S(2)}, u32[]{:S(2)}) async-start(f32[64,2,640]{2,1,0:T(2,128)} %copy.33), calls=%async_computation.2 | async-start | bytes 655360 | tf_op jit(solution)/shard_map/all_to_all | solution.py:90

commit v16 on v14

--- a/solution.py
+++ b/solution.py
@@ -62,8 +62,13 @@
     left_done = jnp.dot(left_inv, grads_part, precision=high)
     to_lower = jnp.zeros((double, double), jnp.float32)
     to_lower = to_lower.at[proj_rank:, :proj_rank].set(right_inv)
-    to_lower = jnp.kron(jnp.eye(seq_count, dtype=jnp.float32), to_lower)
-    pre_part = jnp.dot(left_done, to_lower, precision=high)
+    pre_part = jnp.concatenate(
+        [
+            jnp.dot(left_done[:, s * double : (s + 1) * double], to_lower, precision=high)
+            for s in range(seq_count)
+        ],
+        axis=1,
+    )
     stacked = (grads_part + pre_part).reshape(tensor_size, row_width, seq_count * double)
     rows = jnp.sum(lax.all_to_all(stacked, "tensor", 0, 0, tiled=True), axis=0)
     rows = rows.reshape(row_width, seq_count, double).transpose(1, 0, 2)

time: 62.8 us -> 63 us (level)
    reshape x0 -> x1, other arithmetic: none -> 0.64 us  [per_device(): (grads_part + pre_part).reshape(tensor_size, row_width, seq_count * double)]
  transfers between devices with their start and end apart: 3 -> 3, of which waited for: 3 -> 3; matrix products, arithmetic and copies ran while one was open for 3% -> 2% of each run, Pallas kernels for 0% -> 0%
where the time goes in v16:
time: 63 us; the launch traced here: 62.7 us
  waiting for transfers between devices  28.6 us (45%)
  starting transfers between devices  24.3 us (39%)
  Pallas kernels  3.54 us (6%)
  other arithmetic  2.28 us (4%)
  local copies, waits for them, and re-layouts  2.22 us (4%)
  matrix products  0.9 us (1%)
  between operations  0.83 us (1%)
    all_to_all x1, starting transfers between devices, per_device(): gathered = jnp.sum(lax.all_to_all(payload, 'dp', 0, 0, tiled=True), axis=0)  16.6 us
    all_to_all x1, waiting for transfers between devices, per_device(): gathered = jnp.sum(lax.all_to_all(payload, 'dp', 0, 0, tiled=True), axis=0)  14.8 us
    all_to_all x1, waiting for transfers between devices, per_device(): mine = jnp.sum(lax.all_to_all(chunks, 'tensor', 0, 0, tiled=True), axis=0)  8.34 us
    all_to_all x1, waiting for transfers between devices, per_device(): rows = jnp.sum(lax.all_to_all(stacked, 'tensor', 0, 0, tiled=True), axis=0)  5.52 us
    all_to_all x1, starting transfers between devices, per_device(): mine = jnp.sum(lax.all_to_all(chunks, 'tensor', 0, 0, tiled=True), axis=0)  4.3 us
    pallas_call x1, Pallas kernels, project_both(): pl.pallas_call(_project_kernel, grid=(tokens // tile,), in_specs=[pl.Bloc...  3.54 us
    all_to_all x1, starting transfers between devices, per_device(): rows = jnp.sum(lax.all_to_all(stacked, 'tensor', 0, 0, tiled=True), axis=0)  3.36 us
  transfers between devices with their start and end apart: 3, of which 3 were waited for; matrix products, arithmetic and copies ran while one was open for 2% of the time, Pallas kernels for 0%

profile of v16, /device:TPU:8, one launch (start us, length us, event | category | flops | bytes accessed | tf_op | source)
XLA Modules:
  0.0 62.7 jit_solution(1574318995100282017)
XLA Ops:
  0.6 0.0 copy-start
  0.6 0.0 copy-start.3
  0.7 0.0 copy-start.2
  0.7 0.0 copy-start.4
  0.7 0.0 copy-start.1
  0.7 3.5 %shard_map.104 = f32[768,128]{1,0:T(8,128)} custom-call(bf16[768,1792]{1,0:T(8,128)(2,1)} %bitcast.27, bf16[768,512]{1,0:T(8,128)(2,1)} %bitcast.29, bf16[64,1792]{1,0:T(8,128)(2,1)} %proj_in_ref.1, bf16[64,512]{1,0:T(8,128)(2,1)} %proj_out_ref.1), custom_call_target="tpu_custom_call" | custom-call | tf_op jit(solution)/shard_map/pallas_call | solution.py:24
  4.2 4.3 %all-to-all-start = ((f32[8,96,128]{2,1,0:T(8,128)}), f32[8,96,128]{2,1,0:T(8,128)S(1)}, u32[]{:S(2)}, u32[]{:S(2)}) async-start(f32[8,96,128]{2,1,0:T(8,128)} %bitcast.28), calls=%async_computation | async-start | bytes 786432 | tf_op jit(solution)/shard_map/all_to_all | solution.py:49
  8.6 0.0 copy-done.3
  8.6 0.2 convert_reduce_fusion
  8.8 0.0 copy-done.2
  8.8 0.1 fusion.20
  8.8 0.1 copy.18
  9.0 0.0 copy-done.4
  9.0 0.2 select_reduce_fusion.1
  9.1 8.3 %all-to-all-done = f32[8,96,128]{2,1,0:T(8,128)S(1)} async-done(((f32[8,96,128]{2,1,0:T(8,128)}), f32[8,96,128]{2,1,0:T(8,128)S(1)}, u32[]{:S(2)}, u32[]{:S(2)}) %all-to-all-start) | async-done | bytes 393248 | tf_op jit(solution)/shard_map/all_to_all | solution.py:49
  17.5 0.2 mul.51
  17.7 0.2 fusion.1
  18.0 0.0 copy-done
  18.0 0.2 convolution_bitcast_fusion
  18.1 0.0 copy-done.1
  18.2 0.2 fusion.11
  18.3 0.2 fusion.7
  18.5 0.2 fusion.9
  18.7 0.6 %fusion.6 = f32[8,8,384]{2,1,0:T(8,128)} fusion(f32[64,384]{1,0:T(8,128)S(1)} %fusion.1, f32[64,128]{1,0:T(8,128)S(1)} %fusion.7, f32[64,128]{1,0:T(8,128)S(1)} %fusion.9, f32[64,128]{1,0:T(8,128)S(1)} %fusion.11), kind=kLoop, calls=%fused_computation.11 | loop fusion | flops 73728 | bytes 294912 | tf_op jit(solution)/shard_map/reshape | solution.py:72
  19.3 3.4 %all-to-all-start.1 = ((f32[8,8,384]{2,1,0:T(8,128)}), f32[8,8,384]{2,1,0:T(8,128)S(1)}, u32[]{:S(2)}, u32[]{:S(2)}) async-start(f32[8,8,384]{2,1,0:T(8,128)} %fusion.6), calls=%async_computation.1 | async-start | bytes 196608 | tf_op jit(solution)/shard_map/all_to_all | solution.py:73
  22.7 0.1 convert_reduce_fusion.1
  22.8 0.1 copy.19
  22.9 5.5 %all-to-all-done.1 = f32[8,8,384]{2,1,0:T(8,128)S(1)} async-done(((f32[8,8,384]{2,1,0:T(8,128)}), f32[8,8,384]{2,1,0:T(8,128)S(1)}, u32[]{:S(2)}, u32[]{:S(2)}) %all-to-all-start.1) | async-done | bytes 98336 | tf_op jit(solution)/shard_map/all_to_all | solution.py:73
  28.4 0.1 fusion.25
  28.5 0.1 broadcast_in_dim.18
  28.6 0.1 select_reduce_fusion
  28.7 1.0 %copy.20 = f32[64,2,640]{2,1,0:T(2,128)} copy(f32[64,2,640]{2,0,1:T(8,128)S(1)} %select_maximum_fusion) | data formatting | bytes 655360 | tf_op jit(solution)/shard_map/concatenate | solution.py:92
  29.7 16.6 %all-to-all-start.2 = ((f32[64,2,640]{2,1,0:T(2,128)}), f32[64,2,640]{2,1,0:T(2,128)S(1)}, u32[]{:S(2)}, u32[]{:S(2)}) async-start(f32[64,2,640]{2,1,0:T(2,128)} %copy.20), calls=%async_computation.2 | async-start | bytes 655360 | tf_op jit(solution)/shard_map/all_to_all | solution.py:96
  46.3 0.7 %reshape.167 = f32[3,512]{1,0:T(4,128)} reshape(f32[3,8,64]{2,1,0:T(8,128)S(1)} %get-tuple-element.17) | data formatting | bytes 12288 | tf_op jit(solution)/shard_map/reshape | solution.py:75
  47.0 14.8 %all-to-all-done.2 = f32[64,2,640]{2,1,0:T(2,128)S(1)} async-done(((f32[64,2,640]{2,1,0:T(2,128)}), f32[64,2,640]{2,1,0:T(2,128)S(1)}, u32[]{:S(2)}, u32[]{:S(2)}) %all-to-all-start.2) | async-done | bytes 327712 | tf_op jit(solution)/shard_map/all_to_all | solution.py:96
  61.7 0.1 reduce_sum.69
  61.9 0.1 fusion.21
  62.0 0.7 %slice_divide_fusion = f32[2,512]{1,0:T(2,128)} fusion(f32[2,640]{1,0:T(2,128)S(1)} %reduce_sum.69, f32[2]{0:T(128)S(1)} %fusion.21), kind=kLoop, calls=%fused_computation.26 | loop fusion | flops 1024 | bytes 8200 | tf_op jit(solution)/shard_map/div | solution.py:98
  (9 shorter events, 0.1 us)
Async XLA Ops:
  0.6 17.3 %copy-start = (f32[64,64]{1,0:T(8,128)S(1)}, f32[64,64]{1,0:T(8,128)}, u32[]{:S(2)}) copy-start(f32[64,64]{1,0:T(8,128)} %param.15) | copy-start | bytes 49156
  0.6 7.9 %copy-start.3 = (s32[100]{0:T(128)S(1)}, s32[100]{0:T(128)}, u32[]{:S(2)}) copy-start(s32[100]{0:T(128)} %param.19) | copy-start | bytes 1204
  0.7 8.1 %copy-start.2 = (s32[3]{0:T(128)S(1)}, s32[3]{0:T(128)}, u32[]{:S(2)}) copy-start(s32[3]{0:T(128)} %param.17) | copy-start | bytes 40
  0.7 8.3 %copy-start.4 = (s32[3]{0:T(128)S(1)}, s32[3]{0:T(128)}, u32[]{:S(2)}) copy-start(s32[3]{0:T(128)} %param.18) | copy-start | bytes 40
  0.7 17.5 %copy-start.1 = (f32[64,64]{1,0:T(8,128)S(1)}, f32[64,64]{1,0:T(8,128)}, u32[]{:S(2)}) copy-start(f32[64,64]{1,0:T(8,128)} %param.16) | copy-start | bytes 49156
  4.2 13.2 %all-to-all-start = ((f32[8,96,128]{2,1,0:T(8,128)}), f32[8,96,128]{2,1,0:T(8,128)S(1)}, u32[]{:S(2)}, u32[]{:S(2)}) async-start(f32[8,96,128]{2,1,0:T(8,128)} %bitcast.28), calls=%async_computation | async-start | bytes 786432 | tf_op jit(solution)/shard_map/all_to_all | solution.py:49
  19.3 9.1 %all-to-all-start.1 = ((f32[8,8,384]{2,1,0:T(8,128)}), f32[8,8,384]{2,1,0:T(8,128)S(1)}, u32[]{:S(2)}, u32[]{:S(2)}) async-start(f32[8,8,384]{2,1,0:T(8,128)} %fusion.6), calls=%async_computation.1 | async-start | bytes 196608 | tf_op jit(solution)/shard_map/all_to_all | solution.py:73
  29.7 32.0 %all-to-all-start.2 = ((f32[64,2,640]{2,1,0:T(2,128)}), f32[64,2,640]{2,1,0:T(2,128)S(1)}, u32[]{:S(2)}, u32[]{:S(2)}) async-start(f32[64,2,640]{2,1,0:T(2,128)} %copy.20), calls=%async_computation.2 | async-start | bytes 655360 | tf_op jit(solution)/shard_map/all_to_all | solution.py:96

commit v17 on v15

--- a/solution.py
+++ b/solution.py
@@ -53,8 +53,10 @@
     seq_index = jnp.arange(seq_count, dtype=jnp.int32)
     weight = (token_seq[None, :] == seq_index[:, None]) & (token_pos[None, :] < lengths[:, None])
     double = 2 * proj_rank
-    right_blk = mine[:, proj_rank:]
-    right_both = jnp.concatenate([jnp.dot(right_blk, right_inv, precision=high), right_blk], axis=1)
+    spread = jnp.zeros((double, double), jnp.float32)
+    spread = spread.at[proj_rank:, :proj_rank].set(right_inv)
+    spread = spread.at[proj_rank:, proj_rank:].set(jnp.eye(proj_rank, dtype=jnp.float32))
+    right_both = jnp.dot(mine, spread, precision=lax.Precision.HIGHEST)
     right_seq = right_both[:, None, :] * weight.T.astype(jnp.float32)[:, :, None]
     right_seq = right_seq.reshape(block, seq_count * double)
     grads_part = lax.dot_general(

time: 63 us -> 62.6 us (level)
  waiting for transfers between devices: 28.6 us -> 27.6 us
  local copies, waits for them, and re-layouts: 2.26 us -> 3 us
    all_to_all x1, waiting for transfers between devices: 8.34 us -> 7.33 us  [per_device(): mine = jnp.sum(lax.all_to_all(chunks, 'tensor', 0, 0, tiled=True), axis=0)]
    scatter x0 -> x2, local copies, waits for them, and re-layouts: none -> 0.97 us  [the longest x1 0.96 us: per_device(): spread.at[proj_rank:, proj_rank:].set(jnp.eye(proj_rank, dtype=jnp.float32))]
  transfers between devices with their start and end apart: 3 -> 3, of which waited for: 3 -> 3; matrix products, arithmetic and copies ran while one was open for 2% -> 4% of each run, Pallas kernels for 0% -> 0%
where the time goes in v17:
time: 62.6 us; the launch traced here: 62.3 us
  waiting for transfers between devices  27.6 us (44%)
  starting transfers between devices  24.3 us (39%)
  Pallas kernels  3.54 us (6%)
  local copies, waits for them, and re-layouts  3 us (5%)
  other arithmetic  1.82 us (3%)
  matrix products  1.24 us (2%)
  between operations  0.82 us (1%)
    all_to_all x1, starting transfers between devices, per_device(): gathered = jnp.sum(lax.all_to_all(payload, 'dp', 0, 0, tiled=True), axis=0)  16.6 us
    all_to_all x1, waiting for transfers between devices, per_device(): gathered = jnp.sum(lax.all_to_all(payload, 'dp', 0, 0, tiled=True), axis=0)  14.8 us
    all_to_all x1, waiting for transfers between devices, per_device(): mine = jnp.sum(lax.all_to_all(chunks, 'tensor', 0, 0, tiled=True), axis=0)  7.33 us
    all_to_all x1, waiting for transfers between devices, per_device(): rows = jnp.sum(lax.all_to_all(stacked, 'tensor', 0, 0, tiled=True), axis=0)  5.52 us
    all_to_all x1, starting transfers between devices, per_device(): mine = jnp.sum(lax.all_to_all(chunks, 'tensor', 0, 0, tiled=True), axis=0)  4.3 us
    pallas_call x1, Pallas kernels, project_both(): pl.pallas_call(_project_kernel, grid=(tokens // tile,), in_specs=[pl.Bloc...  3.54 us
    all_to_all x1, starting transfers between devices, per_device(): rows = jnp.sum(lax.all_to_all(stacked, 'tensor', 0, 0, tiled=True), axis=0)  3.36 us
  transfers between devices with their start and end apart: 3, of which 3 were waited for; matrix products, arithmetic and copies ran while one was open for 4% of the time, Pallas kernels for 0%

profile of v17, /device:TPU:8, one launch (start us, length us, event | category | flops | bytes accessed | tf_op | source)
XLA Modules:
  0.0 62.3 jit_solution(1133981792463058605)
XLA Ops:
  0.6 0.0 copy-start
  0.6 0.0 copy-start.3
  0.7 0.0 copy-start.2
  0.7 0.0 copy-start.1
  0.7 0.0 copy-start.4
  0.7 3.5 %shard_map.104 = f32[768,128]{1,0:T(8,128)} custom-call(bf16[768,1792]{1,0:T(8,128)(2,1)} %bitcast.23, bf16[768,512]{1,0:T(8,128)(2,1)} %bitcast.25, bf16[64,1792]{1,0:T(8,128)(2,1)} %proj_in_ref.1, bf16[64,512]{1,0:T(8,128)(2,1)} %proj_out_ref.1), custom_call_target="tpu_custom_call" | custom-call | tf_op jit(solution)/shard_map/pallas_call | solution.py:24
  4.2 4.3 %all-to-all-start = ((f32[8,96,128]{2,1,0:T(8,128)}), f32[8,96,128]{2,1,0:T(8,128)S(1)}, u32[]{:S(2)}, u32[]{:S(2)}) async-start(f32[8,96,128]{2,1,0:T(8,128)} %bitcast.24), calls=%async_computation | async-start | bytes 786432 | tf_op jit(solution)/shard_map/all_to_all | solution.py:49
  8.6 0.0 copy-done.3
  8.6 0.2 convert_reduce_fusion
  8.8 0.0 copy-done.2
  8.8 0.1 fusion.13
  8.9 0.1 copy.18
  9.0 0.0 copy-done.1
  9.0 1.0 %scatter.9 = f32[128,128]{1,0:T(8,128)S(1)} dynamic-update-slice(f32[128,128]{1,0:T(8,128)S(1)} %scatter.6, f32[64,64]{1,0:T(8,128)S(1)} %fusion.7, s32[]{:T(128)} %constant.104.clone.1, s32[]{:T(128)} %constant.104.clone.1) | dynamic-update-slice | bytes 32772 | tf_op jit(solution)/shard_map/scatter | solution.py:58
  10.0 0.0 copy-done.4
  10.0 0.2 select_reduce_fusion.1
  10.2 7.3 %all-to-all-done = f32[8,96,128]{2,1,0:T(8,128)S(1)} async-done(((f32[8,96,128]{2,1,0:T(8,128)}), f32[8,96,128]{2,1,0:T(8,128)S(1)}, u32[]{:S(2)}, u32[]{:S(2)}) %all-to-all-start) | async-done | bytes 393248 | tf_op jit(solution)/shard_map/all_to_all | solution.py:49
  17.5 0.2 fusion.16
  17.7 0.2 broadcast_multiply_fusion
  17.9 0.2 fusion.2
  18.1 0.0 copy-done
  18.1 0.8 %fusion.1 = f32[8,8,384]{2,1,0:T(8,128)} fusion(f32[64,384]{1,0:T(8,128)S(1)} %fusion.2, f32[64,64]{1,0:T(8,128)S(1)} %copy-done, pred[384]{0:T(512)(128)(4,1)S(1)} %fusion.8), kind=kOutput, calls=%fused_computation.2 | convolution fusion | flops 9461760 | bytes 213376 | tf_op jit(solution)/shard_map/dot_general | solution.py:65
  18.9 3.4 %all-to-all-start.1 = ((f32[8,8,384]{2,1,0:T(8,128)}), f32[8,8,384]{2,1,0:T(8,128)S(1)}, u32[]{:S(2)}, u32[]{:S(2)}) async-start(f32[8,8,384]{2,1,0:T(8,128)} %fusion.1), calls=%async_computation.1 | async-start | bytes 196608 | tf_op jit(solution)/shard_map/all_to_all | solution.py:69
  22.3 0.1 convert_reduce_fusion.1
  22.4 0.1 copy.19
  22.5 5.5 %all-to-all-done.1 = f32[8,8,384]{2,1,0:T(8,128)S(1)} async-done(((f32[8,8,384]{2,1,0:T(8,128)}), f32[8,8,384]{2,1,0:T(8,128)S(1)}, u32[]{:S(2)}, u32[]{:S(2)}) %all-to-all-start.1) | async-done | bytes 98336 | tf_op jit(solution)/shard_map/all_to_all | solution.py:69
  28.0 0.1 fusion.15
  28.1 0.1 broadcast_in_dim.27
  28.2 0.1 select_reduce_fusion
  28.4 1.0 %copy.20 = f32[64,2,640]{2,1,0:T(2,128)} copy(f32[64,2,640]{2,0,1:T(8,128)S(1)} %select_maximum_fusion) | data formatting | bytes 655360 | tf_op jit(solution)/shard_map/concatenate | solution.py:88
  29.3 16.6 %all-to-all-start.2 = ((f32[64,2,640]{2,1,0:T(2,128)}), f32[64,2,640]{2,1,0:T(2,128)S(1)}, u32[]{:S(2)}, u32[]{:S(2)}) async-start(f32[64,2,640]{2,1,0:T(2,128)} %copy.20), calls=%async_computation.2 | async-start | bytes 655360 | tf_op jit(solution)/shard_map/all_to_all | solution.py:92
  45.9 0.7 %reshape.201 = f32[3,512]{1,0:T(4,128)} reshape(f32[3,8,64]{2,1,0:T(8,128)S(1)} %get-tuple-element.29) | data formatting | bytes 12288 | tf_op jit(solution)/shard_map/reshape | solution.py:71
  46.6 14.8 %all-to-all-done.2 = f32[64,2,640]{2,1,0:T(2,128)S(1)} async-done(((f32[64,2,640]{2,1,0:T(2,128)}), f32[64,2,640]{2,1,0:T(2,128)S(1)}, u32[]{:S(2)}, u32[]{:S(2)}) %all-to-all-start.2) | async-done | bytes 327712 | tf_op jit(solution)/shard_map/all_to_all | solution.py:92
  61.4 0.1 reduce_sum.69
  61.5 0.1 fusion.14
  61.6 0.7 %slice_divide_fusion = f32[2,512]{1,0:T(2,128)} fusion(f32[2,640]{1,0:T(2,128)S(1)} %reduce_sum.69, f32[2]{0:T(128)S(1)} %fusion.14), kind=kLoop, calls=%fused_computation.16 | loop fusion | flops 1024 | bytes 8200 | tf_op jit(solution)/shard_map/div | solution.py:94
  (9 shorter events, 0.1 us)
Async XLA Ops:
  0.6 17.5 %copy-start = (f32[64,64]{1,0:T(8,128)S(1)}, f32[64,64]{1,0:T(8,128)}, u32[]{:S(2)}) copy-start(f32[64,64]{1,0:T(8,128)} %param.17) | copy-start | bytes 49156
  0.6 7.9 %copy-start.3 = (s32[100]{0:T(128)S(1)}, s32[100]{0:T(128)}, u32[]{:S(2)}) copy-start(s32[100]{0:T(128)} %param.21) | copy-start | bytes 1204
  0.7 8.1 %copy-start.2 = (s32[3]{0:T(128)S(1)}, s32[3]{0:T(128)}, u32[]{:S(2)}) copy-start(s32[3]{0:T(128)} %param.19) | copy-start | bytes 40
  0.7 8.3 %copy-start.1 = (f32[64,64]{1,0:T(8,128)S(1)}, f32[64,64]{1,0:T(8,128)}, u32[]{:S(2)}) copy-start(f32[64,64]{1,0:T(8,128)} %param.18) | copy-start | bytes 49156
  0.7 9.3 %copy-start.4 = (s32[3]{0:T(128)S(1)}, s32[3]{0:T(128)}, u32[]{:S(2)}) copy-start(s32[3]{0:T(128)} %param.20) | copy-start | bytes 40
  4.2 13.2 %all-to-all-start = ((f32[8,96,128]{2,1,0:T(8,128)}), f32[8,96,128]{2,1,0:T(8,128)S(1)}, u32[]{:S(2)}, u32[]{:S(2)}) async-start(f32[8,96,128]{2,1,0:T(8,128)} %bitcast.24), calls=%async_computation | async-start | bytes 786432 | tf_op jit(solution)/shard_map/all_to_all | solution.py:49
  18.9 9.1 %all-to-all-start.1 = ((f32[8,8,384]{2,1,0:T(8,128)}), f32[8,8,384]{2,1,0:T(8,128)S(1)}, u32[]{:S(2)}, u32[]{:S(2)}) async-start(f32[8,8,384]{2,1,0:T(8,128)} %fusion.1), calls=%async_computation.1 | async-start | bytes 196608 | tf_op jit(solution)/shard_map/all_to_all | solution.py:69
  29.3 32.0 %all-to-all-start.2 = ((f32[64,2,640]{2,1,0:T(2,128)}), f32[64,2,640]{2,1,0:T(2,128)S(1)}, u32[]{:S(2)}, u32[]{:S(2)}) async-start(f32[64,2,640]{2,1,0:T(2,128)} %copy.20), calls=%async_computation.2 | async-start | bytes 655360 | tf_op jit(solution)/shard_map/all_to_all | solution.py:92
